TPU v7x, 32 devices: a whole 2x2x4 slice. The times are simulated.
32 devices in a mesh: head: 2 (over x), seq: 16 (over z, y, core).
Axes of the slice: x: 2, y: 2, z: 4, core: 2. Of those that a mesh axis runs over, the one named last changes fastest.
Arguments:
- queries: bfloat16 [4096, 5120], P('seq', 'head'), may hold values from -6 to 6
- keys: bfloat16 [4096, 5120], P('seq', 'head'), may hold values from -6 to 6
- values: bfloat16 [4096, 5120], P('seq', 'head'), may hold values from -6 to 6
- out_weight: bfloat16 [5120, 5120], P('head', 'seq'), may hold values from -0.3125 to 0.3125
- tile_lists: int32 [32, 12], replicated, may hold values from 0 to 31, as said below
- tile_counts: int32 [32], replicated, may hold values from 1 to 12, as said below
Outputs:
- mixed: bfloat16 [4096, 5120], P('seq', 'head')
Inputs may be any that keep to these rules, and one draw needn't show every extreme that they name: `tile_lists`: each row q holds 12 distinct key tiles; its first entry is q itself; every entry k has |k div 2 - q div 2| <= 5. Entries after the first tile_counts[q] take no part. `tile_counts`: some query tile uses all 12 entries of its list.
All inputs are finite; a program needn't handle non-finite values.
Results may differ from a plain program's by a relative error of at most 0.008.
Values may be sent and summed in bfloat16 or wider, within the bound.
No kernel may reach another device: no remote copies, remote signals or barrier semaphores. Data moves between devices by JAX's collectives and lax.ppermute only.
A program may use at most 192 MiB of HBM per device.

v0:
```python
import functools
import math

import jax
import jax.numpy as jnp
from jax import lax
from jax.experimental import pallas as pl
from jax.experimental.pallas import tpu as pltpu
from jax.sharding import Mesh
from jax.sharding import PartitionSpec as P

HD = 128
TILE = 128
REACH = 5

SEQ = ("chip", "core")

masked_floor = -1e30


def shifted(x, axis, by):
    peers = lax.axis_size(axis)
    pairs = [(i, i + by) for i in range(peers) if 0 <= i + by < peers]
    return lax.ppermute(x, axis, pairs)


def swapped(x, axis):
    return lax.ppermute(x, axis, [(0, 1), (1, 0)])


def fifth_neighbour(x, chips):
    peers = chips * 2
    pairs = []
    for s in range(peers):
        t = s + REACH if s % 2 == 1 else s - REACH
        if 0 <= t < peers:
            pairs.append((s, t))
    return lax.ppermute(x, SEQ, pairs)


def attention_kernel(n_blocks, tiles, mask_ref, q_ref, *refs):
    kv_refs = refs[:n_blocks]
    out_ref = refs[n_blocks]
    score_ref = refs[n_blocks + 1]
    rows = q_ref.shape[0]
    query = q_ref[...]
    for b in range(n_blocks):
        keys = kv_refs[b][0]
        scores = lax.dot_general(
            query, keys, (((1,), (1,)), ((), ())), preferred_element_type=jnp.float32
        ) / math.sqrt(HD)
        score_ref[:, b * rows:(b + 1) * rows] = scores
        for qi in range(tiles):
            for kt in range(tiles):
                flag = mask_ref[(b * tiles + qi) * tiles + kt]

                @pl.when(flag == 0)
                def _(b=b, qi=qi, kt=kt):
                    score_ref[qi * TILE:(qi + 1) * TILE, b * rows + kt * TILE:b * rows + (kt + 1) * TILE] = (
                        jnp.full((TILE, TILE), masked_floor, jnp.float32)
                    )

    scores = score_ref[...]
    peak = jnp.max(scores, axis=1, keepdims=True)
    weights = jnp.exp(scores - peak)
    totals = jnp.sum(weights, axis=1, keepdims=True)
    rounded = weights.astype(jnp.bfloat16)
    summed = jnp.zeros((rows, HD), jnp.float32)
    for b in range(n_blocks):
        summed = summed + jnp.dot(
            rounded[:, b * rows:(b + 1) * rows], kv_refs[b][1], preferred_element_type=jnp.float32
        )
    out_ref[...] = (summed / totals).astype(out_ref.dtype)


def block_attention(queries, kv_list, flat_masks):
    rows, width = queries.shape
    heads = width // HD
    n_blocks = len(kv_list)
    tiles = rows // TILE
    kv_spec = pl.BlockSpec((2, rows, HD), lambda h, m: (0, 0, h))
    grid_spec = pltpu.PrefetchScalarGridSpec(
        num_scalar_prefetch=1,
        grid=(heads,),
        in_specs=[pl.BlockSpec((rows, HD), lambda h, m: (0, h))] + [kv_spec] * n_blocks,
        out_specs=pl.BlockSpec((rows, HD), lambda h, m: (0, h)),
        scratch_shapes=[pltpu.VMEM((rows, n_blocks * rows), jnp.float32)],
    )
    flops = 4 * rows * n_blocks * rows * HD * heads
    bytes_moved = 2 * (rows * width * 2 + n_blocks * 2 * rows * width)
    return pl.pallas_call(
        functools.partial(attention_kernel, n_blocks, tiles),
        grid_spec=grid_spec,
        out_shape=jax.ShapeDtypeStruct((rows, width), jnp.bfloat16),
        cost_estimate=pl.CostEstimate(
            flops=flops, transcendentals=rows * n_blocks * rows * heads, bytes_accessed=bytes_moved
        ),
    )(flat_masks, queries, *kv_list)


def local(queries, keys, values, out_weight, tile_lists, tile_counts):
    tok_rows, feat_width = queries.shape
    tiles_here = tok_rows // TILE
    heads_here = feat_width // HD
    chips = lax.axis_size("chip")
    core = lax.axis_index("core")
    device_index = lax.axis_index("chip") * 2 + core
    query_heads = queries.reshape(tok_rows, heads_here, HD)
    stacked = jnp.stack([keys, values])
    own_lists = lax.dynamic_slice_in_dim(tile_lists, device_index * tiles_here, tiles_here, 0)
    own_counts = lax.dynamic_slice_in_dim(tile_counts, device_index * tiles_here, tiles_here, 0)
    live_slots = jnp.arange(own_lists.shape[1], dtype=jnp.int32)[None, :] < own_counts[:, None]

    def tile_need(offset):
        key_tiles = (device_index + offset) * tiles_here + jnp.arange(tiles_here, dtype=jnp.int32)
        matches = (own_lists[:, :, None] == key_tiles[None, None, :]) & live_slots[:, :, None]
        return jnp.any(matches, axis=1)

    kv_blocks = [(0, stacked)]
    sibling = swapped(stacked, "core")
    kv_blocks.append((1 - 2 * core, sibling))
    kv_blocks.append((-REACH + 2 * REACH * core, fifth_neighbour(stacked, chips)))
    fetched = []
    for chip_step in (1, 2):
        for sign in (1, -1):
            block = shifted(stacked, "chip", sign * chip_step)
            fetched.append((-sign * 2 * chip_step, block))
            kv_blocks.append((-sign * 2 * chip_step, block))
    for offset, block in fetched:
        passed = swapped(block, "core")
        kv_blocks.append((offset + 1 - 2 * core, passed))

    tile_masks = jnp.stack([tile_need(offset) for offset, _ in kv_blocks]).astype(jnp.int32)
    attended = block_attention(queries, [b for _, b in kv_blocks], tile_masks.reshape(-1))
    weight_rows = lax.all_gather(out_weight, SEQ, axis=1, tiled=True)
    heads = lax.axis_size("head")
    if heads == 2:
        half = weight_rows.shape[1] // 2
        me = lax.axis_index("head")
        mine = lax.dynamic_slice_in_dim(weight_rows, me * half, half, 1)
        theirs = lax.dynamic_slice_in_dim(weight_rows, (1 - me) * half, half, 1)
        sent = jnp.dot(attended, theirs, preferred_element_type=jnp.float32).astype(jnp.bfloat16)
        got = swapped(sent, "head")
        kept_part = jnp.dot(attended, mine, preferred_element_type=jnp.float32).astype(jnp.bfloat16)
        kept_part = lax.optimization_barrier(kept_part)
        return (kept_part.astype(jnp.float32) + got.astype(jnp.float32)).astype(jnp.bfloat16)
    projected = jnp.dot(attended, weight_rows, preferred_element_type=jnp.float32)
    return lax.psum_scatter(projected.astype(jnp.bfloat16), "head", scatter_dimension=1, tiled=True)


def solution(mesh):
    heads = mesh.shape["head"]
    seq = mesh.shape["seq"]
    view = Mesh(mesh.devices.reshape(heads, seq // 2, 2), ("head", "chip", "core"))
    return jax.shard_map(
        local,
        mesh=view,
        in_specs=(P(SEQ, "head"), P(SEQ, "head"), P(SEQ, "head"), P("head", SEQ), P(), P()),
        out_specs=P(SEQ, "head"),
        check_vma=False,
    )
```

profile of v0, /device:TPU:5, one launch (start us, length us, event | category | flops | bytes accessed | tf_op | source)
XLA Modules:
  0.0 421.3 jit_solution(531916429400990907)
XLA Ops:
  6.5 0.7 all-gather.2.cloned.1.call-update
  7.3 2.0 pad_maximum_fusion.refs_0_
  9.2 3.1 collective-permute-start.2
  12.4 3.6 collective-permute-start.3
  16.0 3.2 collective-permute-start.4
  19.2 1.3 collective-permute-start.5
  20.5 1.6 collective-permute-start
  22.1 154.0 %collective-permute-done.2.refs_3_ = bf16[2,256,2560]{2,1,0:T(8,128)(2,1)} collective-permute-done((bf16[2,256,2560]{2,1,0:T(8,128)(2,1)S(1)}, bf16[2,256,2560]{2,1,0:T(8,128)(2,1)}, u32[]{:S(2)}, u32[]{:S(2)}) %collective-permute-start.2) | collective-permute-done | bytes 2621472 | tf_op jit(solution)/shard_map/ppermute | solution.py:24
  176.0 1.9 collective-permute-start.1
  178.0 0.0 collective-permute-done.3.refs_4_
  178.0 4.0 collective-permute-start.6
  182.0 17.5 %collective-permute-done.4.refs_5_ = bf16[2,256,2560]{2,1,0:T(8,128)(2,1)} collective-permute-done((bf16[2,256,2560]{2,1,0:T(8,128)(2,1)S(1)}, bf16[2,256,2560]{2,1,0:T(8,128)(2,1)}, u32[]{:S(2)}, u32[]{:S(2)}) %collective-permute-start.4) | collective-permute-done | bytes 2621472 | tf_op jit(solution)/shard_map/ppermute | solution.py:24
  199.5 5.0 %collective-permute-start.7 = (bf16[2,256,2560]{2,1,0:T(8,128)(2,1)}, bf16[2,256,2560]{2,1,0:T(8,128)(2,1)}, u32[]{:S(2)}, u32[]{:S(2)}) collective-permute-start(bf16[2,256,2560]{2,1,0:T(8,128)(2,1)} %collective-permute-done.3.refs_4_), channel_id=1, source_target_pairs={{0,1},{1,0},{2,3},{3,2},{4,5},{5,4},{6,7},{7,6},{8,9},{9,8},{10,11... | collective-permute-start | bytes 7864328 | tf_op jit(solution)/shard_map/ppermute | solution.py:28
  204.5 0.0 collective-permute-done.5.refs_6_
  204.5 0.0 collective-permute-start.8
  204.5 0.0 collective-permute-done.refs_1_
  204.5 1.5 copy-done.3
  206.1 0.5 collective-permute-start.9
  206.6 0.1 constant_dynamic-slice_fusion
  206.6 0.1 copy.22
  206.7 0.1 dynamic_slice.13
  206.9 0.1 iota_compare_fusion
  206.9 0.5 and_reduce_fusion
  207.5 0.1 copy.23
  207.6 0.1 copy.24
  207.7 0.1 copy.25
  207.8 0.1 copy.26
  207.9 0.1 copy.27
  208.0 0.1 copy.28
  208.2 0.1 copy.29
  208.3 0.1 copy.30
  208.4 0.1 copy.31
  208.5 0.1 copy.32
  208.6 0.1 copy.33
  208.7 0.1 stack.56
  208.9 0.1 copy.34
  209.0 0.6 reshape.70.mask_ref
  209.6 100.6 %collective-permute-done.1.refs_2_ = bf16[2,256,2560]{2,1,0:T(8,128)(2,1)} collective-permute-done((bf16[2,256,2560]{2,1,0:T(8,128)(2,1)S(1)}, bf16[2,256,2560]{2,1,0:T(8,128)(2,1)}, u32[]{:S(2)}, u32[]{:S(2)}) %collective-permute-start.1) | collective-permute-done | bytes 2621472 | tf_op jit(solution)/shard_map/ppermute | solution.py:38
  310.2 0.0 collective-permute-done.6.refs_7_
  310.2 0.0 collective-permute-done.7.refs_8_
  310.2 0.0 collective-permute-done.8.refs_9_
  310.2 76.3 %shard_map.64 = bf16[256,2560]{1,0:T(8,128)(2,1)} custom-call(s32[44]{0:T(128)} %reshape.70.mask_ref, bf16[256,2560]{1,0:T(8,128)(2,1)} %q_ref.1, bf16[2,256,2560]{2,1,0:T(8,128)(2,1)} %copy-done.2, bf16[2,256,2560]{2,1,0:T(8,128)(2,1)} %copy-done.3, bf16[2,256,2560]{2,1,0:T(8,128)(2,1)} %collective-permute-done.1.refs_2_, ...), custom_call_target="tpu_custom_call" | custom-call | flops 7381975040 | bytes 31457280 | tf_op jit(solution)/shard_map/pallas_call | solution.py:91
  386.5 0.0 all-gather.2.cloned.1.call-done
  386.5 9.8 %fusion.7 = bf16[256,2560]{1,0:T(8,128)(2,1)} fusion(bf16[256,2560]{1,0:T(8,128)(2,1)} %shard_map.64, bf16[2560,5120]{0,1:T(8,128)(2,1)} %all-gather.2.cloned.1.call-done, s32[]{:T(128)S(6)} %select_n.12), kind=kOutput, calls=%fused_computation.5 | convolution fusion | flops 3356098560 | bytes 15728644 | tf_op jit(solution)/shard_map/dot_general | solution.py:142
  396.4 1.2 collective-permute-start.10
  397.6 8.3 %fusion.4 = bf16[256,2560]{1,0:T(8,128)(2,1)S(1)} fusion(bf16[256,2560]{1,0:T(8,128)(2,1)S(1)} %copy-done.4, bf16[2560,5120]{0,1:T(8,128)(2,1)} %all-gather.2.cloned.1.call-done, s32[]{:T(128)S(6)} %select_n.11), kind=kOutput, calls=%fused_computation.4 | convolution fusion | flops 3356098560 | bytes 15728644 | tf_op jit(solution)/shard_map/dot_general | solution.py:144
  405.9 7.1 %collective-permute-done.10 = bf16[256,2560]{1,0:T(8,128)(2,1)S(1)} collective-permute-done((bf16[256,2560]{1,0:T(8,128)(2,1)}, bf16[256,2560]{1,0:T(8,128)(2,1)S(1)}, u32[]{:S(2)}, u32[]{:S(2)}) %collective-permute-start.10) | collective-permute-done | bytes 1310752 | tf_op jit(solution)/shard_map/ppermute | solution.py:28
  413.0 1.4 add_convert_fusion
  (20 shorter events, 0.1 us)
Async XLA Ops:
  6.5 200.0 %copy-start = (s32[32,12]{0,1:T(8,128)S(1)}, s32[32,12]{0,1:T(8,128)}, u32[]{:S(2)}) copy-start(s32[32,12]{0,1:T(8,128)} %param.10) | copy-start | bytes 4612
  6.5 380.0 %all-gather.2.cloned.1.call-start = ((), (), s32[]{:S(2)}) async-start(), calls=%async_computation | async-start | bytes 27852800 | tf_op jit(solution)/shard_map/all_gather | solution.py:135
  7.3 199.5 %copy-start.5 = (s32[32]{0:T(128)S(1)}, s32[32]{0:T(128)}, u32[]{:S(2)}) copy-start(s32[32]{0:T(128)} %param.11) | copy-start | bytes 388
  9.2 301.0 %copy-start.2 = (bf16[2,256,2560]{2,1,0:T(8,128)(2,1)}, bf16[2,256,2560]{2,1,0:T(8,128)(2,1)S(1)}, u32[]{:S(2)}) copy-start(bf16[2,256,2560]{2,1,0:T(8,128)(2,1)S(1)} %pad_maximum_fusion.refs_0_) | copy-start | bytes 7864324
  9.2 166.8 %collective-permute-start.2 = (bf16[2,256,2560]{2,1,0:T(8,128)(2,1)S(1)}, bf16[2,256,2560]{2,1,0:T(8,128)(2,1)}, u32[]{:S(2)}, u32[]{:S(2)}) collective-permute-start(bf16[2,256,2560]{2,1,0:T(8,128)(2,1)S(1)} %pad_maximum_fusion.refs_0_), channel_id=1, source_target_pairs={{0,2},{2,4},{4,6},{6,8},{8,10},{10,12},{12,14},{1,3},{3,5},{5,7},{... | collective-permute-start | bytes 7864328 | tf_op jit(solution)/shard_map/ppermute | solution.py:24
  12.4 165.6 %collective-permute-start.3 = (bf16[2,256,2560]{2,1,0:T(8,128)(2,1)S(1)}, bf16[2,256,2560]{2,1,0:T(8,128)(2,1)}, u32[]{:S(2)}, u32[]{:S(2)}) collective-permute-start(bf16[2,256,2560]{2,1,0:T(8,128)(2,1)S(1)} %pad_maximum_fusion.refs_0_), channel_id=1, source_target_pairs={{2,0},{4,2},{6,4},{8,6},{10,8},{12,10},{14,12},{3,1},{5,3},{7,5},{... | collective-permute-start | bytes 7864328 | tf_op jit(solution)/shard_map/ppermute | solution.py:24
  16.0 183.5 %collective-permute-start.4 = (bf16[2,256,2560]{2,1,0:T(8,128)(2,1)S(1)}, bf16[2,256,2560]{2,1,0:T(8,128)(2,1)}, u32[]{:S(2)}, u32[]{:S(2)}) collective-permute-start(bf16[2,256,2560]{2,1,0:T(8,128)(2,1)S(1)} %pad_maximum_fusion.refs_0_), channel_id=1, source_target_pairs={{0,4},{2,6},{4,8},{6,10},{8,12},{10,14},{1,5},{3,7},{5,9},{7,11},{... | collective-permute-start | bytes 7864328 | tf_op jit(solution)/shard_map/ppermute | solution.py:24
  19.2 185.3 %collective-permute-start.5 = (bf16[2,256,2560]{2,1,0:T(8,128)(2,1)S(1)}, bf16[2,256,2560]{2,1,0:T(8,128)(2,1)}, u32[]{:S(2)}, u32[]{:S(2)}) collective-permute-start(bf16[2,256,2560]{2,1,0:T(8,128)(2,1)S(1)} %pad_maximum_fusion.refs_0_), channel_id=1, source_target_pairs={{4,0},{6,2},{8,4},{10,6},{12,8},{14,10},{5,1},{7,3},{9,5},{11,7},{... | collective-permute-start | bytes 7864328 | tf_op jit(solution)/shard_map/ppermute | solution.py:24
  20.5 184.0 %collective-permute-start = (bf16[2,256,2560]{2,1,0:T(8,128)(2,1)S(1)}, bf16[2,256,2560]{2,1,0:T(8,128)(2,1)S(1)}, u32[]{:S(2)}, u32[]{:S(2)}) collective-permute-start(bf16[2,256,2560]{2,1,0:T(8,128)(2,1)S(1)} %pad_maximum_fusion.refs_0_), channel_id=1, source_target_pairs={{0,1},{1,0},{2,3},{3,2},{4,5},{5,4},{6,7},{7,6},{8,9},{9,8},{10,11... | collective-permute-start | bytes 7864328 | tf_op jit(solution)/shard_map/ppermute | solution.py:28
  176.0 134.1 %collective-permute-start.1 = (bf16[2,256,2560]{2,1,0:T(8,128)(2,1)S(1)}, bf16[2,256,2560]{2,1,0:T(8,128)(2,1)}, u32[]{:S(2)}, u32[]{:S(2)}) collective-permute-start(bf16[2,256,2560]{2,1,0:T(8,128)(2,1)S(1)} %pad_maximum_fusion.refs_0_), channel_id=1, source_target_pairs={{1,6},{3,8},{5,10},{6,1},{7,12},{8,3},{9,14},{10,5},{12,7},{14,9},... | collective-permute-start | bytes 7864328 | tf_op jit(solution)/shard_map/ppermute | solution.py:38
  178.0 132.2 %collective-permute-start.6 = (bf16[2,256,2560]{2,1,0:T(8,128)(2,1)}, bf16[2,256,2560]{2,1,0:T(8,128)(2,1)}, u32[]{:S(2)}, u32[]{:S(2)}) collective-permute-start(bf16[2,256,2560]{2,1,0:T(8,128)(2,1)} %collective-permute-done.2.refs_3_), channel_id=1, source_target_pairs={{0,1},{1,0},{2,3},{3,2},{4,5},{5,4},{6,7},{7,6},{8,9},{9,8},{10,11... | collective-permute-start | bytes 7864328 | tf_op jit(solution)/shard_map/ppermute | solution.py:28
  199.5 110.7 %collective-permute-start.7 = (bf16[2,256,2560]{2,1,0:T(8,128)(2,1)}, bf16[2,256,2560]{2,1,0:T(8,128)(2,1)}, u32[]{:S(2)}, u32[]{:S(2)}) collective-permute-start(bf16[2,256,2560]{2,1,0:T(8,128)(2,1)} %collective-permute-done.3.refs_4_), channel_id=1, source_target_pairs={{0,1},{1,0},{2,3},{3,2},{4,5},{5,4},{6,7},{7,6},{8,9},{9,8},{10,11... | collective-permute-start | bytes 7864328 | tf_op jit(solution)/shard_map/ppermute | solution.py:28
  204.5 105.7 %collective-permute-start.8 = (bf16[2,256,2560]{2,1,0:T(8,128)(2,1)}, bf16[2,256,2560]{2,1,0:T(8,128)(2,1)}, u32[]{:S(2)}, u32[]{:S(2)}) collective-permute-start(bf16[2,256,2560]{2,1,0:T(8,128)(2,1)} %collective-permute-done.4.refs_5_), channel_id=1, source_target_pairs={{0,1},{1,0},{2,3},{3,2},{4,5},{5,4},{6,7},{7,6},{8,9},{9,8},{10,11... | collective-permute-start | bytes 7864328 | tf_op jit(solution)/shard_map/ppermute | solution.py:28
  204.5 1.6 copy-start.3
  206.1 104.1 %collective-permute-start.9 = (bf16[2,256,2560]{2,1,0:T(8,128)(2,1)}, bf16[2,256,2560]{2,1,0:T(8,128)(2,1)}, u32[]{:S(2)}, u32[]{:S(2)}) collective-permute-start(bf16[2,256,2560]{2,1,0:T(8,128)(2,1)} %collective-permute-done.5.refs_6_), channel_id=1, source_target_pairs={{0,1},{1,0},{2,3},{3,2},{4,5},{5,4},{6,7},{7,6},{8,9},{9,8},{10,11... | collective-permute-start | bytes 7864328 | tf_op jit(solution)/shard_map/ppermute | solution.py:28
  386.5 11.1 %copy-start.4 = (bf16[256,2560]{1,0:T(8,128)(2,1)S(1)}, bf16[256,2560]{1,0:T(8,128)(2,1)}, u32[]{:S(2)}) copy-start(bf16[256,2560]{1,0:T(8,128)(2,1)} %shard_map.64) | copy-start | bytes 3932164
  396.4 16.7 %collective-permute-start.10 = (bf16[256,2560]{1,0:T(8,128)(2,1)}, bf16[256,2560]{1,0:T(8,128)(2,1)S(1)}, u32[]{:S(2)}, u32[]{:S(2)}) collective-permute-start(bf16[256,2560]{1,0:T(8,128)(2,1)} %fusion.7), channel_id=1, source_target_pairs={{0,16},{16,0},{1,17},{17,1},{2,18},{18,2},{3,19},{19,3},{4,20},{20... | collective-permute-start | bytes 3932168 | tf_op jit(solution)/shard_map/ppermute | solution.py:28
  397.6 16.8 %copy-start.1 = (s32[32,12]{0,1:T(8,128)S(1)}, s32[32,12]{0,1:T(8,128)}, u32[]{:S(2)}) copy-start(s32[32,12]{0,1:T(8,128)} %param.10) | copy-start | bytes 4612
Sparse Core Ops, SparseCore 0:
  9.0 263.0 all-gather.1
where the time goes:
time: 422 us; the launch traced here: 421 us
  waiting for transfers between devices  280 us (66%)
  Pallas kernels  76.3 us (18%)
  starting transfers between devices  25.5 us (6%)
  matrix products  18.2 us (4%)
  between operations  13.6 us (3%)
    ppermute x4, waiting for transfers between devices, shifted(): return lax.ppermute(x, axis, pairs)  171 us
    ppermute x1, waiting for transfers between devices, fifth_neighbour(): return lax.ppermute(x, SEQ, pairs)  101 us
    pallas_call x1, Pallas kernels, block_attention(): pl.pallas_call(functools.partial(attention_kernel, n_blocks, tiles), grid...  76.3 us
    ppermute x6, starting transfers between devices, swapped(): return lax.ppermute(x, axis, [(0, 1), (1, 0)])  12.3 us
    ppermute x4, starting transfers between devices, shifted(): return lax.ppermute(x, axis, pairs)  11.2 us
    dot_general x1, matrix products, local(): jnp.dot(attended, theirs, preferred_element_type=jnp.float32)  9.85 us
  transfers between devices with their start and end apart: 12, of which 4 were waited for; matrix products, arithmetic and copies ran while one was open for 3% of the time, Pallas kernels for 18%

commit v1 on v0

--- a/solution.py
+++ b/solution.py
@@ -38,58 +38,62 @@
     return lax.ppermute(x, SEQ, pairs)
 
 
-def attention_kernel(n_blocks, tiles, mask_ref, q_ref, *refs):
+def attention_kernel(n_blocks, tiles, group, mask_ref, q_ref, *refs):
     kv_refs = refs[:n_blocks]
     out_ref = refs[n_blocks]
     score_ref = refs[n_blocks + 1]
     rows = q_ref.shape[0]
-    query = q_ref[...]
-    for b in range(n_blocks):
-        keys = kv_refs[b][0]
-        scores = lax.dot_general(
-            query, keys, (((1,), (1,)), ((), ())), preferred_element_type=jnp.float32
-        ) / math.sqrt(HD)
-        score_ref[:, b * rows:(b + 1) * rows] = scores
-        for qi in range(tiles):
-            for kt in range(tiles):
-                flag = mask_ref[(b * tiles + qi) * tiles + kt]
+    for g in range(group):
+        cols = slice(g * HD, (g + 1) * HD)
+        query = q_ref[:, cols]
+        for b in range(n_blocks):
+            keys = kv_refs[b][0, :, cols]
+            scores = lax.dot_general(
+                query, keys, (((1,), (1,)), ((), ())), preferred_element_type=jnp.float32
+            ) / math.sqrt(HD)
+            score_ref[:, b * rows:(b + 1) * rows] = scores
+            for qi in range(tiles):
+                for kt in range(tiles):
+                    flag = mask_ref[(b * tiles + qi) * tiles + kt]
 
-                @pl.when(flag == 0)
-                def _(b=b, qi=qi, kt=kt):
-                    score_ref[qi * TILE:(qi + 1) * TILE, b * rows + kt * TILE:b * rows + (kt + 1) * TILE] = (
-                        jnp.full((TILE, TILE), masked_floor, jnp.float32)
-                    )
+                    @pl.when(flag == 0)
+                    def _(b=b, qi=qi, kt=kt):
+                        score_ref[qi * TILE:(qi + 1) * TILE, b * rows + kt * TILE:b * rows + (kt + 1) * TILE] = (
+                            jnp.full((TILE, TILE), masked_floor, jnp.float32)
+                        )
 
-    scores = score_ref[...]
-    peak = jnp.max(scores, axis=1, keepdims=True)
-    weights = jnp.exp(scores - peak)
-    totals = jnp.sum(weights, axis=1, keepdims=True)
-    rounded = weights.astype(jnp.bfloat16)
-    summed = jnp.zeros((rows, HD), jnp.float32)
-    for b in range(n_blocks):
-        summed = summed + jnp.dot(
-            rounded[:, b * rows:(b + 1) * rows], kv_refs[b][1], preferred_element_type=jnp.float32
-        )
-    out_ref[...] = (summed / totals).astype(out_ref.dtype)
+        scores = score_ref[...]
+        peak = jnp.max(scores, axis=1, keepdims=True)
+        weights = jnp.exp(scores - peak)
+        totals = jnp.sum(weights, axis=1, keepdims=True)
+        rounded = weights.astype(jnp.bfloat16)
+        summed = jnp.zeros((rows, HD), jnp.float32)
+        for b in range(n_blocks):
+            summed = summed + jnp.dot(
+                rounded[:, b * rows:(b + 1) * rows], kv_refs[b][1, :, cols], preferred_element_type=jnp.float32
+            )
+        out_ref[:, cols] = (summed / totals).astype(out_ref.dtype)
 
 
 def block_attention(queries, kv_list, flat_masks):
     rows, width = queries.shape
     heads = width // HD
+    group = 5 if heads % 5 == 0 else 1
     n_blocks = len(kv_list)
     tiles = rows // TILE
-    kv_spec = pl.BlockSpec((2, rows, HD), lambda h, m: (0, 0, h))
+    span = group * HD
+    kv_spec = pl.BlockSpec((2, rows, span), lambda h, m: (0, 0, h))
     grid_spec = pltpu.PrefetchScalarGridSpec(
         num_scalar_prefetch=1,
-        grid=(heads,),
-        in_specs=[pl.BlockSpec((rows, HD), lambda h, m: (0, h))] + [kv_spec] * n_blocks,
-        out_specs=pl.BlockSpec((rows, HD), lambda h, m: (0, h)),
+        grid=(heads // group,),
+        in_specs=[pl.BlockSpec((rows, span), lambda h, m: (0, h))] + [kv_spec] * n_blocks,
+        out_specs=pl.BlockSpec((rows, span), lambda h, m: (0, h)),
         scratch_shapes=[pltpu.VMEM((rows, n_blocks * rows), jnp.float32)],
     )
     flops = 4 * rows * n_blocks * rows * HD * heads
     bytes_moved = 2 * (rows * width * 2 + n_blocks * 2 * rows * width)
     return pl.pallas_call(
-        functools.partial(attention_kernel, n_blocks, tiles),
+        functools.partial(attention_kernel, n_blocks, tiles, group),
         grid_spec=grid_spec,
         out_shape=jax.ShapeDtypeStruct((rows, width), jnp.bfloat16),
         cost_estimate=pl.CostEstimate(

time: 422 us -> 419 us (level)
  no operation moved by 1% of the time
where the time goes in v1:
time: 419 us
  waiting for transfers between devices  280 us (67%)
  Pallas kernels  73.7 us (18%)
  starting transfers between devices  25.5 us (6%)
  matrix products  18.2 us (4%)
  between operations  13.6 us (3%)
    ppermute x4, waiting for transfers between devices, shifted(): return lax.ppermute(x, axis, pairs)  171 us
    ppermute x1, waiting for transfers between devices, fifth_neighbour(): return lax.ppermute(x, SEQ, pairs)  101 us
    pallas_call x1, Pallas kernels, block_attention(): pl.pallas_call(functools.partial(attention_kernel, n_blocks, tiles, group...  73.7 us
    ppermute x6, starting transfers between devices, swapped(): return lax.ppermute(x, axis, [(0, 1), (1, 0)])  12.3 us
    ppermute x4, starting transfers between devices, shifted(): return lax.ppermute(x, axis, pairs)  11.2 us
    dot_general x1, matrix products, local(): jnp.dot(attended, theirs, preferred_element_type=jnp.float32)  9.85 us
  transfers between devices with their start and end apart: 12, of which 4 were waited for; matrix products, arithmetic and copies ran while one was open for 3% of the time, Pallas kernels for 18%

profile of v1, /device:TPU:5, one launch (start us, length us, event | category | flops | bytes accessed | tf_op | source)
XLA Modules:
  0.0 418.7 jit_solution(14461389480680177565)
XLA Ops:
  6.5 0.7 all-gather.2.cloned.1.call-update
  7.3 2.0 pad_maximum_fusion.refs_0_
  9.2 3.1 collective-permute-start.2
  12.4 3.6 collective-permute-start.3
  16.0 3.2 collective-permute-start.4
  19.2 1.3 collective-permute-start.5
  20.5 1.6 collective-permute-start
  22.1 154.0 %collective-permute-done.2.refs_3_ = bf16[2,256,2560]{2,1,0:T(8,128)(2,1)} collective-permute-done((bf16[2,256,2560]{2,1,0:T(8,128)(2,1)S(1)}, bf16[2,256,2560]{2,1,0:T(8,128)(2,1)}, u32[]{:S(2)}, u32[]{:S(2)}) %collective-permute-start.2) | collective-permute-done | bytes 2621472 | tf_op jit(solution)/shard_map/ppermute | solution.py:24
  176.0 1.9 collective-permute-start.1
  178.0 0.0 collective-permute-done.3.refs_4_
  178.0 4.0 collective-permute-start.6
  182.0 17.5 %collective-permute-done.4.refs_5_ = bf16[2,256,2560]{2,1,0:T(8,128)(2,1)} collective-permute-done((bf16[2,256,2560]{2,1,0:T(8,128)(2,1)S(1)}, bf16[2,256,2560]{2,1,0:T(8,128)(2,1)}, u32[]{:S(2)}, u32[]{:S(2)}) %collective-permute-start.4) | collective-permute-done | bytes 2621472 | tf_op jit(solution)/shard_map/ppermute | solution.py:24
  199.5 5.0 %collective-permute-start.7 = (bf16[2,256,2560]{2,1,0:T(8,128)(2,1)}, bf16[2,256,2560]{2,1,0:T(8,128)(2,1)}, u32[]{:S(2)}, u32[]{:S(2)}) collective-permute-start(bf16[2,256,2560]{2,1,0:T(8,128)(2,1)} %collective-permute-done.3.refs_4_), channel_id=1, source_target_pairs={{0,1},{1,0},{2,3},{3,2},{4,5},{5,4},{6,7},{7,6},{8,9},{9,8},{10,11... | collective-permute-start | bytes 7864328 | tf_op jit(solution)/shard_map/ppermute | solution.py:28
  204.5 0.0 collective-permute-done.5.refs_6_
  204.5 0.0 collective-permute-start.8
  204.5 0.0 collective-permute-done.refs_1_
  204.5 1.5 copy-done.3
  206.1 0.5 collective-permute-start.9
  206.6 0.1 constant_dynamic-slice_fusion
  206.6 0.1 copy.22
  206.7 0.1 dynamic_slice.13
  206.9 0.1 iota_compare_fusion
  206.9 0.5 and_reduce_fusion
  207.5 0.1 copy.23
  207.6 0.1 copy.24
  207.7 0.1 copy.25
  207.8 0.1 copy.26
  207.9 0.1 copy.27
  208.0 0.1 copy.28
  208.2 0.1 copy.29
  208.3 0.1 copy.30
  208.4 0.1 copy.31
  208.5 0.1 copy.32
  208.6 0.1 copy.33
  208.7 0.1 stack.56
  208.9 0.1 copy.34
  209.0 0.6 reshape.70.mask_ref
  209.6 100.6 %collective-permute-done.1.refs_2_ = bf16[2,256,2560]{2,1,0:T(8,128)(2,1)} collective-permute-done((bf16[2,256,2560]{2,1,0:T(8,128)(2,1)S(1)}, bf16[2,256,2560]{2,1,0:T(8,128)(2,1)}, u32[]{:S(2)}, u32[]{:S(2)}) %collective-permute-start.1) | collective-permute-done | bytes 2621472 | tf_op jit(solution)/shard_map/ppermute | solution.py:38
  310.2 0.0 collective-permute-done.6.refs_7_
  310.2 0.0 collective-permute-done.9.refs_10_
  310.2 73.7 %shard_map.64 = bf16[256,2560]{1,0:T(8,128)(2,1)} custom-call(s32[44]{0:T(128)} %reshape.70.mask_ref, bf16[256,2560]{1,0:T(8,128)(2,1)} %q_ref.1, bf16[2,256,2560]{2,1,0:T(8,128)(2,1)} %copy-done.2, bf16[2,256,2560]{2,1,0:T(8,128)(2,1)} %copy-done.3, bf16[2,256,2560]{2,1,0:T(8,128)(2,1)} %collective-permute-done.1.refs_2_, ...), custom_call_target="tpu_custom_call" | custom-call | flops 7381975040 | bytes 31457280 | tf_op jit(solution)/shard_map/pallas_call | solution.py:95
  384.0 0.0 copy-start.4
  384.0 0.0 all-gather.2.cloned.1.call-done
  384.0 9.8 %fusion.7 = bf16[256,2560]{1,0:T(8,128)(2,1)} fusion(bf16[256,2560]{1,0:T(8,128)(2,1)} %shard_map.64, bf16[2560,5120]{0,1:T(8,128)(2,1)} %all-gather.2.cloned.1.call-done, s32[]{:T(128)S(6)} %select_n.12), kind=kOutput, calls=%fused_computation.5 | convolution fusion | flops 3356098560 | bytes 15728644 | tf_op jit(solution)/shard_map/dot_general | solution.py:146
  393.8 1.2 collective-permute-start.10
  395.1 8.3 %fusion.4 = bf16[256,2560]{1,0:T(8,128)(2,1)S(1)} fusion(bf16[256,2560]{1,0:T(8,128)(2,1)S(1)} %copy-done.4, bf16[2560,5120]{0,1:T(8,128)(2,1)} %all-gather.2.cloned.1.call-done, s32[]{:T(128)S(6)} %select_n.11), kind=kOutput, calls=%fused_computation.4 | convolution fusion | flops 3356098560 | bytes 15728644 | tf_op jit(solution)/shard_map/dot_general | solution.py:148
  403.4 7.1 %collective-permute-done.10 = bf16[256,2560]{1,0:T(8,128)(2,1)S(1)} collective-permute-done((bf16[256,2560]{1,0:T(8,128)(2,1)}, bf16[256,2560]{1,0:T(8,128)(2,1)S(1)}, u32[]{:S(2)}, u32[]{:S(2)}) %collective-permute-start.10) | collective-permute-done | bytes 1310752 | tf_op jit(solution)/shard_map/ppermute | solution.py:28
  410.5 1.4 add_convert_fusion
  (20 shorter events, 0.1 us)
Async XLA Ops:
  6.5 200.0 %copy-start = (s32[32,12]{0,1:T(8,128)S(1)}, s32[32,12]{0,1:T(8,128)}, u32[]{:S(2)}) copy-start(s32[32,12]{0,1:T(8,128)} %param.10) | copy-start | bytes 4612
  6.5 377.5 %all-gather.2.cloned.1.call-start = ((), (), s32[]{:S(2)}) async-start(), calls=%async_computation | async-start | bytes 27852800 | tf_op jit(solution)/shard_map/all_gather | solution.py:139
  7.3 199.5 %copy-start.5 = (s32[32]{0:T(128)S(1)}, s32[32]{0:T(128)}, u32[]{:S(2)}) copy-start(s32[32]{0:T(128)} %param.11) | copy-start | bytes 388
  9.2 301.0 %copy-start.2 = (bf16[2,256,2560]{2,1,0:T(8,128)(2,1)}, bf16[2,256,2560]{2,1,0:T(8,128)(2,1)S(1)}, u32[]{:S(2)}) copy-start(bf16[2,256,2560]{2,1,0:T(8,128)(2,1)S(1)} %pad_maximum_fusion.refs_0_) | copy-start | bytes 7864324
  9.2 166.8 %collective-permute-start.2 = (bf16[2,256,2560]{2,1,0:T(8,128)(2,1)S(1)}, bf16[2,256,2560]{2,1,0:T(8,128)(2,1)}, u32[]{:S(2)}, u32[]{:S(2)}) collective-permute-start(bf16[2,256,2560]{2,1,0:T(8,128)(2,1)S(1)} %pad_maximum_fusion.refs_0_), channel_id=1, source_target_pairs={{0,2},{2,4},{4,6},{6,8},{8,10},{10,12},{12,14},{1,3},{3,5},{5,7},{... | collective-permute-start | bytes 7864328 | tf_op jit(solution)/shard_map/ppermute | solution.py:24
  12.4 165.6 %collective-permute-start.3 = (bf16[2,256,2560]{2,1,0:T(8,128)(2,1)S(1)}, bf16[2,256,2560]{2,1,0:T(8,128)(2,1)}, u32[]{:S(2)}, u32[]{:S(2)}) collective-permute-start(bf16[2,256,2560]{2,1,0:T(8,128)(2,1)S(1)} %pad_maximum_fusion.refs_0_), channel_id=1, source_target_pairs={{2,0},{4,2},{6,4},{8,6},{10,8},{12,10},{14,12},{3,1},{5,3},{7,5},{... | collective-permute-start | bytes 7864328 | tf_op jit(solution)/shard_map/ppermute | solution.py:24
  16.0 183.5 %collective-permute-start.4 = (bf16[2,256,2560]{2,1,0:T(8,128)(2,1)S(1)}, bf16[2,256,2560]{2,1,0:T(8,128)(2,1)}, u32[]{:S(2)}, u32[]{:S(2)}) collective-permute-start(bf16[2,256,2560]{2,1,0:T(8,128)(2,1)S(1)} %pad_maximum_fusion.refs_0_), channel_id=1, source_target_pairs={{0,4},{2,6},{4,8},{6,10},{8,12},{10,14},{1,5},{3,7},{5,9},{7,11},{... | collective-permute-start | bytes 7864328 | tf_op jit(solution)/shard_map/ppermute | solution.py:24
  19.2 185.3 %collective-permute-start.5 = (bf16[2,256,2560]{2,1,0:T(8,128)(2,1)S(1)}, bf16[2,256,2560]{2,1,0:T(8,128)(2,1)}, u32[]{:S(2)}, u32[]{:S(2)}) collective-permute-start(bf16[2,256,2560]{2,1,0:T(8,128)(2,1)S(1)} %pad_maximum_fusion.refs_0_), channel_id=1, source_target_pairs={{4,0},{6,2},{8,4},{10,6},{12,8},{14,10},{5,1},{7,3},{9,5},{11,7},{... | collective-permute-start | bytes 7864328 | tf_op jit(solution)/shard_map/ppermute | solution.py:24
  20.5 184.0 %collective-permute-start = (bf16[2,256,2560]{2,1,0:T(8,128)(2,1)S(1)}, bf16[2,256,2560]{2,1,0:T(8,128)(2,1)S(1)}, u32[]{:S(2)}, u32[]{:S(2)}) collective-permute-start(bf16[2,256,2560]{2,1,0:T(8,128)(2,1)S(1)} %pad_maximum_fusion.refs_0_), channel_id=1, source_target_pairs={{0,1},{1,0},{2,3},{3,2},{4,5},{5,4},{6,7},{7,6},{8,9},{9,8},{10,11... | collective-permute-start | bytes 7864328 | tf_op jit(solution)/shard_map/ppermute | solution.py:28
  176.0 134.1 %collective-permute-start.1 = (bf16[2,256,2560]{2,1,0:T(8,128)(2,1)S(1)}, bf16[2,256,2560]{2,1,0:T(8,128)(2,1)}, u32[]{:S(2)}, u32[]{:S(2)}) collective-permute-start(bf16[2,256,2560]{2,1,0:T(8,128)(2,1)S(1)} %pad_maximum_fusion.refs_0_), channel_id=1, source_target_pairs={{1,6},{3,8},{5,10},{6,1},{7,12},{8,3},{9,14},{10,5},{12,7},{14,9},... | collective-permute-start | bytes 7864328 | tf_op jit(solution)/shard_map/ppermute | solution.py:38
  178.0 132.2 %collective-permute-start.6 = (bf16[2,256,2560]{2,1,0:T(8,128)(2,1)}, bf16[2,256,2560]{2,1,0:T(8,128)(2,1)}, u32[]{:S(2)}, u32[]{:S(2)}) collective-permute-start(bf16[2,256,2560]{2,1,0:T(8,128)(2,1)} %collective-permute-done.2.refs_3_), channel_id=1, source_target_pairs={{0,1},{1,0},{2,3},{3,2},{4,5},{5,4},{6,7},{7,6},{8,9},{9,8},{10,11... | collective-permute-start | bytes 7864328 | tf_op jit(solution)/shard_map/ppermute | solution.py:28
  199.5 110.7 %collective-permute-start.7 = (bf16[2,256,2560]{2,1,0:T(8,128)(2,1)}, bf16[2,256,2560]{2,1,0:T(8,128)(2,1)}, u32[]{:S(2)}, u32[]{:S(2)}) collective-permute-start(bf16[2,256,2560]{2,1,0:T(8,128)(2,1)} %collective-permute-done.3.refs_4_), channel_id=1, source_target_pairs={{0,1},{1,0},{2,3},{3,2},{4,5},{5,4},{6,7},{7,6},{8,9},{9,8},{10,11... | collective-permute-start | bytes 7864328 | tf_op jit(solution)/shard_map/ppermute | solution.py:28
  204.5 105.7 %collective-permute-start.8 = (bf16[2,256,2560]{2,1,0:T(8,128)(2,1)}, bf16[2,256,2560]{2,1,0:T(8,128)(2,1)}, u32[]{:S(2)}, u32[]{:S(2)}) collective-permute-start(bf16[2,256,2560]{2,1,0:T(8,128)(2,1)} %collective-permute-done.4.refs_5_), channel_id=1, source_target_pairs={{0,1},{1,0},{2,3},{3,2},{4,5},{5,4},{6,7},{7,6},{8,9},{9,8},{10,11... | collective-permute-start | bytes 7864328 | tf_op jit(solution)/shard_map/ppermute | solution.py:28
  204.5 1.6 copy-start.3
  206.1 104.1 %collective-permute-start.9 = (bf16[2,256,2560]{2,1,0:T(8,128)(2,1)}, bf16[2,256,2560]{2,1,0:T(8,128)(2,1)}, u32[]{:S(2)}, u32[]{:S(2)}) collective-permute-start(bf16[2,256,2560]{2,1,0:T(8,128)(2,1)} %collective-permute-done.5.refs_6_), channel_id=1, source_target_pairs={{0,1},{1,0},{2,3},{3,2},{4,5},{5,4},{6,7},{7,6},{8,9},{9,8},{10,11... | collective-permute-start | bytes 7864328 | tf_op jit(solution)/shard_map/ppermute | solution.py:28
  384.0 11.1 %copy-start.4 = (bf16[256,2560]{1,0:T(8,128)(2,1)S(1)}, bf16[256,2560]{1,0:T(8,128)(2,1)}, u32[]{:S(2)}) copy-start(bf16[256,2560]{1,0:T(8,128)(2,1)} %shard_map.64) | copy-start | bytes 3932164
  393.8 16.7 %collective-permute-start.10 = (bf16[256,2560]{1,0:T(8,128)(2,1)}, bf16[256,2560]{1,0:T(8,128)(2,1)S(1)}, u32[]{:S(2)}, u32[]{:S(2)}) collective-permute-start(bf16[256,2560]{1,0:T(8,128)(2,1)} %fusion.7), channel_id=1, source_target_pairs={{0,16},{16,0},{1,17},{17,1},{2,18},{18,2},{3,19},{19,3},{4,20},{20... | collective-permute-start | bytes 3932168 | tf_op jit(solution)/shard_map/ppermute | solution.py:28
  395.0 16.8 %copy-start.1 = (s32[32,12]{0,1:T(8,128)S(1)}, s32[32,12]{0,1:T(8,128)}, u32[]{:S(2)}) copy-start(s32[32,12]{0,1:T(8,128)} %param.10) | copy-start | bytes 4612
Sparse Core Ops, SparseCore 0:
  9.0 263.0 all-gather.1

commit v2 on v1

--- a/solution.py
+++ b/solution.py
@@ -50,17 +50,14 @@
             keys = kv_refs[b][0, :, cols]
             scores = lax.dot_general(
                 query, keys, (((1,), (1,)), ((), ())), preferred_element_type=jnp.float32
-            ) / math.sqrt(HD)
-            score_ref[:, b * rows:(b + 1) * rows] = scores
+            ) * (1.0 / math.sqrt(HD))
             for qi in range(tiles):
                 for kt in range(tiles):
                     flag = mask_ref[(b * tiles + qi) * tiles + kt]
-
-                    @pl.when(flag == 0)
-                    def _(b=b, qi=qi, kt=kt):
-                        score_ref[qi * TILE:(qi + 1) * TILE, b * rows + kt * TILE:b * rows + (kt + 1) * TILE] = (
-                            jnp.full((TILE, TILE), masked_floor, jnp.float32)
-                        )
+                    tile = scores[qi * TILE:(qi + 1) * TILE, kt * TILE:(kt + 1) * TILE]
+                    score_ref[qi * TILE:(qi + 1) * TILE, b * rows + kt * TILE:b * rows + (kt + 1) * TILE] = (
+                        jnp.where(flag != 0, tile, masked_floor)
+                    )
 
         scores = score_ref[...]
         peak = jnp.max(scores, axis=1, keepdims=True)

time: 419 us -> 374 us (0.89)
  Pallas kernels: 73.7 us -> 28.3 us
    pallas_call x1, Pallas kernels: 73.7 us -> 28.3 us  [block_attention(): pl.pallas_call(functools.partial(attention_kernel, n_blocks, tiles, group...]
  transfers between devices with their start and end apart: 12 -> 12, of which waited for: 4 -> 4; matrix products, arithmetic and copies ran while one was open for 3% -> 4% of each run, Pallas kernels for 18% -> 8%
where the time goes in v2:
time: 374 us; the launch traced here: 373 us
  waiting for transfers between devices  280 us (75%)
  Pallas kernels  28.3 us (8%)
  starting transfers between devices  25.5 us (7%)
  matrix products  18.2 us (5%)
  between operations  13.6 us (4%)
  other arithmetic  3.97 us (1%)
  local copies, waits for them, and re-layouts  3.9 us (1%)
    ppermute x4, waiting for transfers between devices, shifted(): return lax.ppermute(x, axis, pairs)  171 us
    ppermute x1, waiting for transfers between devices, fifth_neighbour(): return lax.ppermute(x, SEQ, pairs)  101 us
    pallas_call x1, Pallas kernels, block_attention(): pl.pallas_call(functools.partial(attention_kernel, n_blocks, tiles, group...  28.3 us
    ppermute x6, starting transfers between devices, swapped(): return lax.ppermute(x, axis, [(0, 1), (1, 0)])  12.3 us
    ppermute x4, starting transfers between devices, shifted(): return lax.ppermute(x, axis, pairs)  11.2 us
    dot_general x1, matrix products, local(): jnp.dot(attended, theirs, preferred_element_type=jnp.float32)  9.85 us
    dot_general x1, matrix products, local(): jnp.dot(attended, mine, preferred_element_type=jnp.float32)  8.31 us
  transfers between devices with their start and end apart: 12, of which 4 were waited for; matrix products, arithmetic and copies ran while one was open for 4% of the time, Pallas kernels for 8%

profile of v2, /device:TPU:5, one launch (start us, length us, event | category | flops | bytes accessed | tf_op | source)
XLA Modules:
  0.0 373.3 jit_solution(841096051827936744)
XLA Ops:
  6.5 0.7 all-gather.2.cloned.1.call-update
  7.3 2.0 pad_maximum_fusion.refs_0_
  9.2 3.1 collective-permute-start.2
  12.4 3.6 collective-permute-start.3
  16.0 3.2 collective-permute-start.4
  19.2 1.3 collective-permute-start.5
  20.5 1.6 collective-permute-start
  22.1 154.0 %collective-permute-done.2.refs_3_ = bf16[2,256,2560]{2,1,0:T(8,128)(2,1)} collective-permute-done((bf16[2,256,2560]{2,1,0:T(8,128)(2,1)S(1)}, bf16[2,256,2560]{2,1,0:T(8,128)(2,1)}, u32[]{:S(2)}, u32[]{:S(2)}) %collective-permute-start.2) | collective-permute-done | bytes 2621472 | tf_op jit(solution)/shard_map/ppermute | solution.py:24
  176.0 1.9 collective-permute-start.1
  178.0 0.0 collective-permute-done.3.refs_4_
  178.0 4.0 %collective-permute-start.6 = (bf16[2,256,2560]{2,1,0:T(8,128)(2,1)}, bf16[2,256,2560]{2,1,0:T(8,128)(2,1)}, u32[]{:S(2)}, u32[]{:S(2)}) collective-permute-start(bf16[2,256,2560]{2,1,0:T(8,128)(2,1)} %collective-permute-done.2.refs_3_), channel_id=1, source_target_pairs={{0,1},{1,0},{2,3},{3,2},{4,5},{5,4},{6,7},{7,6},{8,9},{9,8},{10,11... | collective-permute-start | bytes 7864328 | tf_op jit(solution)/shard_map/ppermute | solution.py:28
  182.0 17.5 %collective-permute-done.4.refs_5_ = bf16[2,256,2560]{2,1,0:T(8,128)(2,1)} collective-permute-done((bf16[2,256,2560]{2,1,0:T(8,128)(2,1)S(1)}, bf16[2,256,2560]{2,1,0:T(8,128)(2,1)}, u32[]{:S(2)}, u32[]{:S(2)}) %collective-permute-start.4) | collective-permute-done | bytes 2621472 | tf_op jit(solution)/shard_map/ppermute | solution.py:24
  199.5 5.0 %collective-permute-start.7 = (bf16[2,256,2560]{2,1,0:T(8,128)(2,1)}, bf16[2,256,2560]{2,1,0:T(8,128)(2,1)}, u32[]{:S(2)}, u32[]{:S(2)}) collective-permute-start(bf16[2,256,2560]{2,1,0:T(8,128)(2,1)} %collective-permute-done.3.refs_4_), channel_id=1, source_target_pairs={{0,1},{1,0},{2,3},{3,2},{4,5},{5,4},{6,7},{7,6},{8,9},{9,8},{10,11... | collective-permute-start | bytes 7864328 | tf_op jit(solution)/shard_map/ppermute | solution.py:28
  204.5 0.0 collective-permute-done.5.refs_6_
  204.5 0.0 collective-permute-start.8
  204.5 0.0 collective-permute-done.refs_1_
  204.5 1.5 copy-done.3
  206.1 0.5 collective-permute-start.9
  206.6 0.1 constant_dynamic-slice_fusion
  206.6 0.1 copy.22
  206.7 0.1 dynamic_slice.13
  206.9 0.1 iota_compare_fusion
  206.9 0.5 and_reduce_fusion
  207.5 0.1 copy.23
  207.6 0.1 copy.24
  207.7 0.1 copy.25
  207.8 0.1 copy.26
  207.9 0.1 copy.27
  208.0 0.1 copy.28
  208.2 0.1 copy.29
  208.3 0.1 copy.30
  208.4 0.1 copy.31
  208.5 0.1 copy.32
  208.6 0.1 copy.33
  208.7 0.1 stack.56
  208.9 0.1 copy.34
  209.0 0.6 reshape.70.mask_ref
  209.6 100.6 %collective-permute-done.1.refs_2_ = bf16[2,256,2560]{2,1,0:T(8,128)(2,1)} collective-permute-done((bf16[2,256,2560]{2,1,0:T(8,128)(2,1)S(1)}, bf16[2,256,2560]{2,1,0:T(8,128)(2,1)}, u32[]{:S(2)}, u32[]{:S(2)}) %collective-permute-start.1) | collective-permute-done | bytes 2621472 | tf_op jit(solution)/shard_map/ppermute | solution.py:38
  310.2 0.0 collective-permute-done.6.refs_7_
  310.2 0.0 collective-permute-done.7.refs_8_
  310.2 0.0 collective-permute-done.9.refs_10_
  310.2 28.3 %shard_map.64 = bf16[256,2560]{1,0:T(8,128)(2,1)} custom-call(s32[44]{0:T(128)} %reshape.70.mask_ref, bf16[256,2560]{1,0:T(8,128)(2,1)} %q_ref.1, bf16[2,256,2560]{2,1,0:T(8,128)(2,1)} %copy-done.2, bf16[2,256,2560]{2,1,0:T(8,128)(2,1)} %copy-done.3, bf16[2,256,2560]{2,1,0:T(8,128)(2,1)} %collective-permute-done.1.refs_2_, ...), custom_call_target="tpu_custom_call" | custom-call | flops 7381975040 | bytes 31457280 | tf_op jit(solution)/shard_map/pallas_call | solution.py:92
  338.6 0.0 all-gather.2.cloned.1.call-done
  338.6 9.8 %fusion.7 = bf16[256,2560]{1,0:T(8,128)(2,1)} fusion(bf16[256,2560]{1,0:T(8,128)(2,1)} %shard_map.64, bf16[2560,5120]{0,1:T(8,128)(2,1)} %all-gather.2.cloned.1.call-done, s32[]{:T(128)S(6)} %select_n.12), kind=kOutput, calls=%fused_computation.5 | convolution fusion | flops 3356098560 | bytes 15728644 | tf_op jit(solution)/shard_map/dot_general | solution.py:143
  348.4 1.2 collective-permute-start.10
  349.7 8.3 %fusion.4 = bf16[256,2560]{1,0:T(8,128)(2,1)S(1)} fusion(bf16[256,2560]{1,0:T(8,128)(2,1)S(1)} %copy-done.4, bf16[2560,5120]{0,1:T(8,128)(2,1)} %all-gather.2.cloned.1.call-done, s32[]{:T(128)S(6)} %select_n.11), kind=kOutput, calls=%fused_computation.4 | convolution fusion | flops 3356098560 | bytes 15728644 | tf_op jit(solution)/shard_map/dot_general | solution.py:145
  358.0 7.1 %collective-permute-done.10 = bf16[256,2560]{1,0:T(8,128)(2,1)S(1)} collective-permute-done((bf16[256,2560]{1,0:T(8,128)(2,1)}, bf16[256,2560]{1,0:T(8,128)(2,1)S(1)}, u32[]{:S(2)}, u32[]{:S(2)}) %collective-permute-start.10) | collective-permute-done | bytes 1310752 | tf_op jit(solution)/shard_map/ppermute | solution.py:28
  365.1 1.4 add_convert_fusion
  (20 shorter events, 0.1 us)
Async XLA Ops:
  6.5 200.0 %copy-start = (s32[32,12]{0,1:T(8,128)S(1)}, s32[32,12]{0,1:T(8,128)}, u32[]{:S(2)}) copy-start(s32[32,12]{0,1:T(8,128)} %param.10) | copy-start | bytes 4612
  6.5 332.1 %all-gather.2.cloned.1.call-start = ((), (), s32[]{:S(2)}) async-start(), calls=%async_computation | async-start | bytes 27852800 | tf_op jit(solution)/shard_map/all_gather | solution.py:136
  7.3 199.5 %copy-start.5 = (s32[32]{0:T(128)S(1)}, s32[32]{0:T(128)}, u32[]{:S(2)}) copy-start(s32[32]{0:T(128)} %param.11) | copy-start | bytes 388
  9.2 301.0 %copy-start.2 = (bf16[2,256,2560]{2,1,0:T(8,128)(2,1)}, bf16[2,256,2560]{2,1,0:T(8,128)(2,1)S(1)}, u32[]{:S(2)}) copy-start(bf16[2,256,2560]{2,1,0:T(8,128)(2,1)S(1)} %pad_maximum_fusion.refs_0_) | copy-start | bytes 7864324
  9.2 166.8 %collective-permute-start.2 = (bf16[2,256,2560]{2,1,0:T(8,128)(2,1)S(1)}, bf16[2,256,2560]{2,1,0:T(8,128)(2,1)}, u32[]{:S(2)}, u32[]{:S(2)}) collective-permute-start(bf16[2,256,2560]{2,1,0:T(8,128)(2,1)S(1)} %pad_maximum_fusion.refs_0_), channel_id=1, source_target_pairs={{0,2},{2,4},{4,6},{6,8},{8,10},{10,12},{12,14},{1,3},{3,5},{5,7},{... | collective-permute-start | bytes 7864328 | tf_op jit(solution)/shard_map/ppermute | solution.py:24
  12.4 165.6 %collective-permute-start.3 = (bf16[2,256,2560]{2,1,0:T(8,128)(2,1)S(1)}, bf16[2,256,2560]{2,1,0:T(8,128)(2,1)}, u32[]{:S(2)}, u32[]{:S(2)}) collective-permute-start(bf16[2,256,2560]{2,1,0:T(8,128)(2,1)S(1)} %pad_maximum_fusion.refs_0_), channel_id=1, source_target_pairs={{2,0},{4,2},{6,4},{8,6},{10,8},{12,10},{14,12},{3,1},{5,3},{7,5},{... | collective-permute-start | bytes 7864328 | tf_op jit(solution)/shard_map/ppermute | solution.py:24
  16.0 183.5 %collective-permute-start.4 = (bf16[2,256,2560]{2,1,0:T(8,128)(2,1)S(1)}, bf16[2,256,2560]{2,1,0:T(8,128)(2,1)}, u32[]{:S(2)}, u32[]{:S(2)}) collective-permute-start(bf16[2,256,2560]{2,1,0:T(8,128)(2,1)S(1)} %pad_maximum_fusion.refs_0_), channel_id=1, source_target_pairs={{0,4},{2,6},{4,8},{6,10},{8,12},{10,14},{1,5},{3,7},{5,9},{7,11},{... | collective-permute-start | bytes 7864328 | tf_op jit(solution)/shard_map/ppermute | solution.py:24
  19.2 185.3 %collective-permute-start.5 = (bf16[2,256,2560]{2,1,0:T(8,128)(2,1)S(1)}, bf16[2,256,2560]{2,1,0:T(8,128)(2,1)}, u32[]{:S(2)}, u32[]{:S(2)}) collective-permute-start(bf16[2,256,2560]{2,1,0:T(8,128)(2,1)S(1)} %pad_maximum_fusion.refs_0_), channel_id=1, source_target_pairs={{4,0},{6,2},{8,4},{10,6},{12,8},{14,10},{5,1},{7,3},{9,5},{11,7},{... | collective-permute-start | bytes 7864328 | tf_op jit(solution)/shard_map/ppermute | solution.py:24
  20.5 184.0 %collective-permute-start = (bf16[2,256,2560]{2,1,0:T(8,128)(2,1)S(1)}, bf16[2,256,2560]{2,1,0:T(8,128)(2,1)S(1)}, u32[]{:S(2)}, u32[]{:S(2)}) collective-permute-start(bf16[2,256,2560]{2,1,0:T(8,128)(2,1)S(1)} %pad_maximum_fusion.refs_0_), channel_id=1, source_target_pairs={{0,1},{1,0},{2,3},{3,2},{4,5},{5,4},{6,7},{7,6},{8,9},{9,8},{10,11... | collective-permute-start | bytes 7864328 | tf_op jit(solution)/shard_map/ppermute | solution.py:28
  176.0 134.1 %collective-permute-start.1 = (bf16[2,256,2560]{2,1,0:T(8,128)(2,1)S(1)}, bf16[2,256,2560]{2,1,0:T(8,128)(2,1)}, u32[]{:S(2)}, u32[]{:S(2)}) collective-permute-start(bf16[2,256,2560]{2,1,0:T(8,128)(2,1)S(1)} %pad_maximum_fusion.refs_0_), channel_id=1, source_target_pairs={{1,6},{3,8},{5,10},{6,1},{7,12},{8,3},{9,14},{10,5},{12,7},{14,9},... | collective-permute-start | bytes 7864328 | tf_op jit(solution)/shard_map/ppermute | solution.py:38
  178.0 132.2 %collective-permute-start.6 = (bf16[2,256,2560]{2,1,0:T(8,128)(2,1)}, bf16[2,256,2560]{2,1,0:T(8,128)(2,1)}, u32[]{:S(2)}, u32[]{:S(2)}) collective-permute-start(bf16[2,256,2560]{2,1,0:T(8,128)(2,1)} %collective-permute-done.2.refs_3_), channel_id=1, source_target_pairs={{0,1},{1,0},{2,3},{3,2},{4,5},{5,4},{6,7},{7,6},{8,9},{9,8},{10,11... | collective-permute-start | bytes 7864328 | tf_op jit(solution)/shard_map/ppermute | solution.py:28
  199.5 110.7 %collective-permute-start.7 = (bf16[2,256,2560]{2,1,0:T(8,128)(2,1)}, bf16[2,256,2560]{2,1,0:T(8,128)(2,1)}, u32[]{:S(2)}, u32[]{:S(2)}) collective-permute-start(bf16[2,256,2560]{2,1,0:T(8,128)(2,1)} %collective-permute-done.3.refs_4_), channel_id=1, source_target_pairs={{0,1},{1,0},{2,3},{3,2},{4,5},{5,4},{6,7},{7,6},{8,9},{9,8},{10,11... | collective-permute-start | bytes 7864328 | tf_op jit(solution)/shard_map/ppermute | solution.py:28
  204.5 105.7 %collective-permute-start.8 = (bf16[2,256,2560]{2,1,0:T(8,128)(2,1)}, bf16[2,256,2560]{2,1,0:T(8,128)(2,1)}, u32[]{:S(2)}, u32[]{:S(2)}) collective-permute-start(bf16[2,256,2560]{2,1,0:T(8,128)(2,1)} %collective-permute-done.4.refs_5_), channel_id=1, source_target_pairs={{0,1},{1,0},{2,3},{3,2},{4,5},{5,4},{6,7},{7,6},{8,9},{9,8},{10,11... | collective-permute-start | bytes 7864328 | tf_op jit(solution)/shard_map/ppermute | solution.py:28
  204.5 1.6 copy-start.3
  206.1 104.1 %collective-permute-start.9 = (bf16[2,256,2560]{2,1,0:T(8,128)(2,1)}, bf16[2,256,2560]{2,1,0:T(8,128)(2,1)}, u32[]{:S(2)}, u32[]{:S(2)}) collective-permute-start(bf16[2,256,2560]{2,1,0:T(8,128)(2,1)} %collective-permute-done.5.refs_6_), channel_id=1, source_target_pairs={{0,1},{1,0},{2,3},{3,2},{4,5},{5,4},{6,7},{7,6},{8,9},{9,8},{10,11... | collective-permute-start | bytes 7864328 | tf_op jit(solution)/shard_map/ppermute | solution.py:28
  338.6 11.1 %copy-start.4 = (bf16[256,2560]{1,0:T(8,128)(2,1)S(1)}, bf16[256,2560]{1,0:T(8,128)(2,1)}, u32[]{:S(2)}) copy-start(bf16[256,2560]{1,0:T(8,128)(2,1)} %shard_map.64) | copy-start | bytes 3932164
  348.4 16.7 %collective-permute-start.10 = (bf16[256,2560]{1,0:T(8,128)(2,1)}, bf16[256,2560]{1,0:T(8,128)(2,1)S(1)}, u32[]{:S(2)}, u32[]{:S(2)}) collective-permute-start(bf16[256,2560]{1,0:T(8,128)(2,1)} %fusion.7), channel_id=1, source_target_pairs={{0,16},{16,0},{1,17},{17,1},{2,18},{18,2},{3,19},{19,3},{4,20},{20... | collective-permute-start | bytes 3932168 | tf_op jit(solution)/shard_map/ppermute | solution.py:28
  349.7 16.8 %copy-start.1 = (s32[32,12]{0,1:T(8,128)S(1)}, s32[32,12]{0,1:T(8,128)}, u32[]{:S(2)}) copy-start(s32[32,12]{0,1:T(8,128)} %param.10) | copy-start | bytes 4612
Sparse Core Ops, SparseCore 0:
  9.0 263.0 all-gather.1

commit v3 on v2

--- a/solution.py
+++ b/solution.py
@@ -118,8 +118,6 @@
         return jnp.any(matches, axis=1)
 
     kv_blocks = [(0, stacked)]
-    sibling = swapped(stacked, "core")
-    kv_blocks.append((1 - 2 * core, sibling))
     kv_blocks.append((-REACH + 2 * REACH * core, fifth_neighbour(stacked, chips)))
     fetched = []
     for chip_step in (1, 2):
@@ -127,6 +125,8 @@
             block = shifted(stacked, "chip", sign * chip_step)
             fetched.append((-sign * 2 * chip_step, block))
             kv_blocks.append((-sign * 2 * chip_step, block))
+    own_late, _ = lax.optimization_barrier((stacked, fetched[0][1]))
+    kv_blocks.append((1 - 2 * core, swapped(own_late, "core")))
     for offset, block in fetched:
         passed = swapped(block, "core")
         kv_blocks.append((offset + 1 - 2 * core, passed))

time: 374 us -> 395 us (1.056)
  the two profiles are of different devices: /device:TPU:5 before, /device:TPU:4 now
where the time goes in v3:
time: 395 us; the launch traced here: 394 us
  waiting for transfers between devices  205 us (52%)
  starting transfers between devices  121 us (31%)
  Pallas kernels  28.5 us (7%)
  matrix products  18.2 us (5%)
  between operations  13.5 us (3%)
  other arithmetic  3.97 us (1%)
    ppermute x4, waiting for transfers between devices, shifted(): return lax.ppermute(x, axis, pairs)  181 us
    ppermute x6, starting transfers between devices, swapped(): return lax.ppermute(x, axis, [(0, 1), (1, 0)])  108 us
    pallas_call x1, Pallas kernels, block_attention(): pl.pallas_call(functools.partial(attention_kernel, n_blocks, tiles, group...  28.5 us
    ppermute x6, waiting for transfers between devices, swapped(): return lax.ppermute(x, axis, [(0, 1), (1, 0)])  23.3 us
    ppermute x4, starting transfers between devices, shifted(): return lax.ppermute(x, axis, pairs)  12.1 us
    dot_general x1, matrix products, local(): jnp.dot(attended, theirs, preferred_element_type=jnp.float32)  9.85 us
    dot_general x1, matrix products, local(): jnp.dot(attended, mine, preferred_element_type=jnp.float32)  8.31 us
  transfers between devices with their start and end apart: 12, of which 4 were waited for; matrix products, arithmetic and copies ran while one was open for 3% of the time, Pallas kernels for 7%

profile of v3, /device:TPU:4, one launch (start us, length us, event | category | flops | bytes accessed | tf_op | source)
XLA Modules:
  0.0 394.2 jit_solution(12796472552987482677)
XLA Ops:
  6.5 0.7 all-gather.2.cloned.1.call-update
  7.3 2.0 pad_maximum_fusion.refs_0_
  9.2 3.4 collective-permute-start.1
  12.7 3.9 collective-permute-start.2
  16.6 3.5 collective-permute-start.3
  20.1 1.3 collective-permute-start.4
  21.4 0.8 collective-permute-start
  22.2 157.0 %collective-permute-done.1.refs_2_ = bf16[2,256,2560]{2,1,0:T(8,128)(2,1)} collective-permute-done((bf16[2,256,2560]{2,1,0:T(8,128)(2,1)S(1)}, bf16[2,256,2560]{2,1,0:T(8,128)(2,1)}, u32[]{:S(2)}, u32[]{:S(2)}) %collective-permute-start.1) | collective-permute-done | bytes 2621472 | tf_op jit(solution)/shard_map/ppermute | solution.py:24
  179.2 0.0 collective-permute-start.5
  179.2 0.0 collective-permute-done.2.refs_3_
  179.2 0.5 collective-permute-start.6
  179.7 24.1 %collective-permute-done.3.refs_4_ = bf16[2,256,2560]{2,1,0:T(8,128)(2,1)} collective-permute-done((bf16[2,256,2560]{2,1,0:T(8,128)(2,1)S(1)}, bf16[2,256,2560]{2,1,0:T(8,128)(2,1)}, u32[]{:S(2)}, u32[]{:S(2)}) %collective-permute-start.3) | collective-permute-done | bytes 2621472 | tf_op jit(solution)/shard_map/ppermute | solution.py:24
  203.8 0.0 collective-permute-start.7
  203.8 0.0 collective-permute-done.4.refs_5_
  203.8 0.5 collective-permute-start.8
  204.3 0.0 collective-permute-done.refs_1_
  204.3 1.6 copy-done.3
  205.9 105.6 %collective-permute-start.9 = (bf16[2,256,2560]{2,1,0:T(8,128)(2,1)}, bf16[2,256,2560]{2,1,0:T(8,128)(2,1)}, u32[]{:S(2)}, u32[]{:S(2)}) collective-permute-start(bf16[2,256,2560]{2,1,0:T(8,128)(2,1)} %collective-permute-done.4.refs_5_), channel_id=1, source_target_pairs={{0,1},{1,0},{2,3},{3,2},{4,5},{5,4},{6,7},{7,6},{8,9},{9,8},{10,11... | collective-permute-start | bytes 7864328 | tf_op jit(solution)/shard_map/ppermute | solution.py:28
  311.5 0.1 constant_dynamic-slice_fusion
  311.5 0.1 copy.22
  311.6 0.1 dynamic_slice.13
  311.8 0.1 iota_compare_fusion
  311.8 0.5 and_reduce_fusion
  312.4 0.1 copy.23
  312.5 0.1 copy.24
  312.6 0.1 copy.25
  312.7 0.1 copy.26
  312.8 0.1 copy.27
  312.9 0.1 copy.28
  313.1 0.1 copy.29
  313.2 0.1 copy.30
  313.3 0.1 copy.31
  313.4 0.1 copy.32
  313.5 0.1 copy.33
  313.6 0.1 stack.56
  313.8 0.1 copy.34
  313.9 0.6 reshape.70.mask_ref
  314.5 0.0 collective-permute-done.5.refs_6_
  314.5 0.0 collective-permute-done.6.refs_7_
  314.5 0.0 collective-permute-done.8.refs_9_
  314.5 1.8 collective-permute-done.9.refs_10_
  316.4 28.5 %shard_map.64 = bf16[256,2560]{1,0:T(8,128)(2,1)} custom-call(s32[44]{0:T(128)} %reshape.70.mask_ref, bf16[256,2560]{1,0:T(8,128)(2,1)} %q_ref.1, bf16[2,256,2560]{2,1,0:T(8,128)(2,1)} %copy-done.2, bf16[2,256,2560]{2,1,0:T(8,128)(2,1)} %copy-done.3, bf16[2,256,2560]{2,1,0:T(8,128)(2,1)} %collective-permute-done.1.refs_2_, ...), custom_call_target="tpu_custom_call" | custom-call | flops 7381975040 | bytes 31457280 | tf_op jit(solution)/shard_map/pallas_call | solution.py:92
  344.9 0.0 all-gather.2.cloned.1.call-done
  344.9 9.8 %fusion.7 = bf16[256,2560]{1,0:T(8,128)(2,1)} fusion(bf16[256,2560]{1,0:T(8,128)(2,1)} %shard_map.64, bf16[2560,5120]{0,1:T(8,128)(2,1)} %all-gather.2.cloned.1.call-done, s32[]{:T(128)S(6)} %select_n.12), kind=kOutput, calls=%fused_computation.5 | convolution fusion | flops 3356098560 | bytes 15728644 | tf_op jit(solution)/shard_map/dot_general | solution.py:143
  354.7 1.5 collective-permute-start.10
  356.3 8.3 %fusion.4 = bf16[256,2560]{1,0:T(8,128)(2,1)S(1)} fusion(bf16[256,2560]{1,0:T(8,128)(2,1)S(1)} %copy-done.4, bf16[2560,5120]{0,1:T(8,128)(2,1)} %all-gather.2.cloned.1.call-done, s32[]{:T(128)S(6)} %select_n.11), kind=kOutput, calls=%fused_computation.4 | convolution fusion | flops 3356098560 | bytes 15728644 | tf_op jit(solution)/shard_map/dot_general | solution.py:145
  364.6 21.4 %collective-permute-done.10 = bf16[256,2560]{1,0:T(8,128)(2,1)S(1)} collective-permute-done((bf16[256,2560]{1,0:T(8,128)(2,1)}, bf16[256,2560]{1,0:T(8,128)(2,1)S(1)}, u32[]{:S(2)}, u32[]{:S(2)}) %collective-permute-start.10) | collective-permute-done | bytes 1310752 | tf_op jit(solution)/shard_map/ppermute | solution.py:28
  386.0 1.4 add_convert_fusion
  (20 shorter events, 0.1 us)
Async XLA Ops:
  6.5 304.9 %copy-start = (s32[32,12]{0,1:T(8,128)S(1)}, s32[32,12]{0,1:T(8,128)}, u32[]{:S(2)}) copy-start(s32[32,12]{0,1:T(8,128)} %param.10) | copy-start | bytes 4612
  6.5 338.4 %all-gather.2.cloned.1.call-start = ((), (), s32[]{:S(2)}) async-start(), calls=%async_computation | async-start | bytes 27852800 | tf_op jit(solution)/shard_map/all_gather | solution.py:136
  7.3 304.4 %copy-start.5 = (s32[32]{0:T(128)S(1)}, s32[32]{0:T(128)}, u32[]{:S(2)}) copy-start(s32[32]{0:T(128)} %param.11) | copy-start | bytes 388
  9.2 307.1 %copy-start.2 = (bf16[2,256,2560]{2,1,0:T(8,128)(2,1)}, bf16[2,256,2560]{2,1,0:T(8,128)(2,1)S(1)}, u32[]{:S(2)}) copy-start(bf16[2,256,2560]{2,1,0:T(8,128)(2,1)S(1)} %pad_maximum_fusion.refs_0_) | copy-start | bytes 7864324
  9.2 170.0 %collective-permute-start.1 = (bf16[2,256,2560]{2,1,0:T(8,128)(2,1)S(1)}, bf16[2,256,2560]{2,1,0:T(8,128)(2,1)}, u32[]{:S(2)}, u32[]{:S(2)}) collective-permute-start(bf16[2,256,2560]{2,1,0:T(8,128)(2,1)S(1)} %pad_maximum_fusion.refs_0_), channel_id=1, source_target_pairs={{0,2},{2,4},{4,6},{6,8},{8,10},{10,12},{12,14},{1,3},{3,5},{5,7},{... | collective-permute-start | bytes 7864328 | tf_op jit(solution)/shard_map/ppermute | solution.py:24
  12.7 166.5 %collective-permute-start.2 = (bf16[2,256,2560]{2,1,0:T(8,128)(2,1)S(1)}, bf16[2,256,2560]{2,1,0:T(8,128)(2,1)}, u32[]{:S(2)}, u32[]{:S(2)}) collective-permute-start(bf16[2,256,2560]{2,1,0:T(8,128)(2,1)S(1)} %pad_maximum_fusion.refs_0_), channel_id=1, source_target_pairs={{2,0},{4,2},{6,4},{8,6},{10,8},{12,10},{14,12},{3,1},{5,3},{7,5},{... | collective-permute-start | bytes 7864328 | tf_op jit(solution)/shard_map/ppermute | solution.py:24
  16.6 187.3 %collective-permute-start.3 = (bf16[2,256,2560]{2,1,0:T(8,128)(2,1)S(1)}, bf16[2,256,2560]{2,1,0:T(8,128)(2,1)}, u32[]{:S(2)}, u32[]{:S(2)}) collective-permute-start(bf16[2,256,2560]{2,1,0:T(8,128)(2,1)S(1)} %pad_maximum_fusion.refs_0_), channel_id=1, source_target_pairs={{0,4},{2,6},{4,8},{6,10},{8,12},{10,14},{1,5},{3,7},{5,9},{7,11},{... | collective-permute-start | bytes 7864328 | tf_op jit(solution)/shard_map/ppermute | solution.py:24
  20.1 183.8 %collective-permute-start.4 = (bf16[2,256,2560]{2,1,0:T(8,128)(2,1)S(1)}, bf16[2,256,2560]{2,1,0:T(8,128)(2,1)}, u32[]{:S(2)}, u32[]{:S(2)}) collective-permute-start(bf16[2,256,2560]{2,1,0:T(8,128)(2,1)S(1)} %pad_maximum_fusion.refs_0_), channel_id=1, source_target_pairs={{4,0},{6,2},{8,4},{10,6},{12,8},{14,10},{5,1},{7,3},{9,5},{11,7},{... | collective-permute-start | bytes 7864328 | tf_op jit(solution)/shard_map/ppermute | solution.py:24
  21.4 183.0 %collective-permute-start = (bf16[2,256,2560]{2,1,0:T(8,128)(2,1)S(1)}, bf16[2,256,2560]{2,1,0:T(8,128)(2,1)S(1)}, u32[]{:S(2)}, u32[]{:S(2)}) collective-permute-start(bf16[2,256,2560]{2,1,0:T(8,128)(2,1)S(1)} %pad_maximum_fusion.refs_0_), channel_id=1, source_target_pairs={{1,6},{3,8},{5,10},{6,1},{7,12},{8,3},{9,14},{10,5},{12,7},{14,9},... | collective-permute-start | bytes 7864328 | tf_op jit(solution)/shard_map/ppermute | solution.py:38
  179.2 135.3 %collective-permute-start.5 = (bf16[2,256,2560]{2,1,0:T(8,128)(2,1)S(1)}, bf16[2,256,2560]{2,1,0:T(8,128)(2,1)}, u32[]{:S(2)}, u32[]{:S(2)}) collective-permute-start(bf16[2,256,2560]{2,1,0:T(8,128)(2,1)S(1)} %pad_maximum_fusion.refs_0_), channel_id=1, source_target_pairs={{0,1},{1,0},{2,3},{3,2},{4,5},{5,4},{6,7},{7,6},{8,9},{9,8},{10,11... | collective-permute-start | bytes 7864328 | tf_op jit(solution)/shard_map/ppermute | solution.py:28
  179.2 135.3 %collective-permute-start.6 = (bf16[2,256,2560]{2,1,0:T(8,128)(2,1)}, bf16[2,256,2560]{2,1,0:T(8,128)(2,1)}, u32[]{:S(2)}, u32[]{:S(2)}) collective-permute-start(bf16[2,256,2560]{2,1,0:T(8,128)(2,1)} %collective-permute-done.1.refs_2_), channel_id=1, source_target_pairs={{0,1},{1,0},{2,3},{3,2},{4,5},{5,4},{6,7},{7,6},{8,9},{9,8},{10,11... | collective-permute-start | bytes 7864328 | tf_op jit(solution)/shard_map/ppermute | solution.py:28
  203.8 110.7 %collective-permute-start.7 = (bf16[2,256,2560]{2,1,0:T(8,128)(2,1)}, bf16[2,256,2560]{2,1,0:T(8,128)(2,1)}, u32[]{:S(2)}, u32[]{:S(2)}) collective-permute-start(bf16[2,256,2560]{2,1,0:T(8,128)(2,1)} %collective-permute-done.2.refs_3_), channel_id=1, source_target_pairs={{0,1},{1,0},{2,3},{3,2},{4,5},{5,4},{6,7},{7,6},{8,9},{9,8},{10,11... | collective-permute-start | bytes 7864328 | tf_op jit(solution)/shard_map/ppermute | solution.py:28
  203.8 110.7 %collective-permute-start.8 = (bf16[2,256,2560]{2,1,0:T(8,128)(2,1)}, bf16[2,256,2560]{2,1,0:T(8,128)(2,1)}, u32[]{:S(2)}, u32[]{:S(2)}) collective-permute-start(bf16[2,256,2560]{2,1,0:T(8,128)(2,1)} %collective-permute-done.3.refs_4_), channel_id=1, source_target_pairs={{0,1},{1,0},{2,3},{3,2},{4,5},{5,4},{6,7},{7,6},{8,9},{9,8},{10,11... | collective-permute-start | bytes 7864328 | tf_op jit(solution)/shard_map/ppermute | solution.py:28
  204.3 1.6 copy-start.3
  205.9 110.5 %collective-permute-start.9 = (bf16[2,256,2560]{2,1,0:T(8,128)(2,1)}, bf16[2,256,2560]{2,1,0:T(8,128)(2,1)}, u32[]{:S(2)}, u32[]{:S(2)}) collective-permute-start(bf16[2,256,2560]{2,1,0:T(8,128)(2,1)} %collective-permute-done.4.refs_5_), channel_id=1, source_target_pairs={{0,1},{1,0},{2,3},{3,2},{4,5},{5,4},{6,7},{7,6},{8,9},{9,8},{10,11... | collective-permute-start | bytes 7864328 | tf_op jit(solution)/shard_map/ppermute | solution.py:28
  344.9 11.4 %copy-start.4 = (bf16[256,2560]{1,0:T(8,128)(2,1)S(1)}, bf16[256,2560]{1,0:T(8,128)(2,1)}, u32[]{:S(2)}) copy-start(bf16[256,2560]{1,0:T(8,128)(2,1)} %shard_map.64) | copy-start | bytes 3932164
  354.7 31.3 %collective-permute-start.10 = (bf16[256,2560]{1,0:T(8,128)(2,1)}, bf16[256,2560]{1,0:T(8,128)(2,1)S(1)}, u32[]{:S(2)}, u32[]{:S(2)}) collective-permute-start(bf16[256,2560]{1,0:T(8,128)(2,1)} %fusion.7), channel_id=1, source_target_pairs={{0,16},{16,0},{1,17},{17,1},{2,18},{18,2},{3,19},{19,3},{4,20},{20... | collective-permute-start | bytes 3932168 | tf_op jit(solution)/shard_map/ppermute | solution.py:28
  356.2 31.1 %copy-start.1 = (s32[32,12]{0,1:T(8,128)S(1)}, s32[32,12]{0,1:T(8,128)}, u32[]{:S(2)}) copy-start(s32[32,12]{0,1:T(8,128)} %param.10) | copy-start | bytes 4612
Sparse Core Ops, SparseCore 0:
  9.0 262.7 all-gather.1

commit v4 on v2

--- a/solution.py
+++ b/solution.py
@@ -28,11 +28,11 @@
     return lax.ppermute(x, axis, [(0, 1), (1, 0)])
 
 
-def fifth_neighbour(x, chips):
+def third_neighbour(x, chips):
     peers = chips * 2
     pairs = []
     for s in range(peers):
-        t = s + REACH if s % 2 == 1 else s - REACH
+        t = s + 3 if s % 2 == 1 else s - 3
         if 0 <= t < peers:
             pairs.append((s, t))
     return lax.ppermute(x, SEQ, pairs)
@@ -120,13 +120,15 @@
     kv_blocks = [(0, stacked)]
     sibling = swapped(stacked, "core")
     kv_blocks.append((1 - 2 * core, sibling))
-    kv_blocks.append((-REACH + 2 * REACH * core, fifth_neighbour(stacked, chips)))
     fetched = []
     for chip_step in (1, 2):
         for sign in (1, -1):
             block = shifted(stacked, "chip", sign * chip_step)
             fetched.append((-sign * 2 * chip_step, block))
             kv_blocks.append((-sign * 2 * chip_step, block))
+    from_below, from_above = fetched[0][1], fetched[1][1]
+    onward = jnp.where(core == 1, from_below, from_above)
+    kv_blocks.append((-REACH + 2 * REACH * core, third_neighbour(onward, chips)))
     for offset, block in fetched:
         passed = swapped(block, "core")
         kv_blocks.append((offset + 1 - 2 * core, passed))

time: 374 us -> 359 us (0.960)
  the two profiles are of different devices: /device:TPU:5 before, /device:TPU:9 now
where the time goes in v4:
time: 359 us
  waiting for transfers between devices  217 us (60%)
  starting transfers between devices  70.1 us (20%)
  Pallas kernels  28.5 us (8%)
  matrix products  18.2 us (5%)
  between operations  13.5 us (4%)
  other arithmetic  7.53 us (2%)
  local copies, waits for them, and re-layouts  3.9 us (1%)
    ppermute x4, waiting for transfers between devices, shifted(): return lax.ppermute(x, axis, pairs)  159 us
    ppermute x6, starting transfers between devices, swapped(): return lax.ppermute(x, axis, [(0, 1), (1, 0)])  51.5 us
    ppermute x1, waiting for transfers between devices, third_neighbour(): return lax.ppermute(x, SEQ, pairs)  37 us
    pallas_call x1, Pallas kernels, block_attention(): pl.pallas_call(functools.partial(attention_kernel, n_blocks, tiles, group...  28.5 us
    ppermute x6, waiting for transfers between devices, swapped(): return lax.ppermute(x, axis, [(0, 1), (1, 0)])  20.3 us
    ppermute x4, starting transfers between devices, shifted(): return lax.ppermute(x, axis, pairs)  12.9 us
    dot_general x1, matrix products, local(): jnp.dot(attended, theirs, preferred_element_type=jnp.float32)  9.85 us
    dot_general x1, matrix products, local(): jnp.dot(attended, mine, preferred_element_type=jnp.float32)  8.31 us
  transfers between devices with their start and end apart: 12, of which 5 were waited for; matrix products, arithmetic and copies ran while one was open for 5% of the time, Pallas kernels for 8%

profile of v4, /device:TPU:9, one launch (start us, length us, event | category | flops | bytes accessed | tf_op | source)
XLA Modules:
  0.0 359.2 jit_solution(11843268008781450893)
XLA Ops:
  6.5 0.7 all-gather.2.cloned.1.call-update
  7.3 2.0 pad_maximum_fusion.refs_0_
  9.2 3.1 collective-permute-start.1
  12.4 3.0 collective-permute-start.2
  15.4 3.2 collective-permute-start.3
  18.6 3.5 collective-permute-start.4
  22.2 1.9 collective-permute-start
  24.0 95.3 %collective-permute-done.1.refs_2_ = bf16[2,256,2560]{2,1,0:T(8,128)(2,1)} collective-permute-done((bf16[2,256,2560]{2,1,0:T(8,128)(2,1)S(1)}, bf16[2,256,2560]{2,1,0:T(8,128)(2,1)}, u32[]{:S(2)}, u32[]{:S(2)}) %collective-permute-start.1) | collective-permute-done | bytes 2621472 | tf_op jit(solution)/shard_map/ppermute | solution.py:24
  119.3 7.8 %collective-permute-done.2.refs_3_ = bf16[2,256,2560]{2,1,0:T(8,128)(2,1)} collective-permute-done((bf16[2,256,2560]{2,1,0:T(8,128)(2,1)S(1)}, bf16[2,256,2560]{2,1,0:T(8,128)(2,1)}, u32[]{:S(2)}, u32[]{:S(2)}) %collective-permute-start.2) | collective-permute-done | bytes 2621472 | tf_op jit(solution)/shard_map/ppermute | solution.py:24
  127.1 3.6 broadcast_select_fusion
  130.7 5.7 %collective-permute-start.5 = (bf16[2,256,2560]{2,1,0:T(8,128)(2,1)}, bf16[2,256,2560]{2,1,0:T(8,128)(2,1)}, u32[]{:S(2)}, u32[]{:S(2)}) collective-permute-start(bf16[2,256,2560]{2,1,0:T(8,128)(2,1)} %broadcast_select_fusion), channel_id=1, source_target_pairs={{1,4},{3,6},{4,1},{5,8},{6,3},{7,10},{8,5},{9,12},{10,7},{11,14},{... | collective-permute-start | bytes 7864328 | tf_op jit(solution)/shard_map/ppermute | solution.py:38
  136.3 44.7 %collective-permute-start.6 = (bf16[2,256,2560]{2,1,0:T(8,128)(2,1)}, bf16[2,256,2560]{2,1,0:T(8,128)(2,1)}, u32[]{:S(2)}, u32[]{:S(2)}) collective-permute-start(bf16[2,256,2560]{2,1,0:T(8,128)(2,1)} %collective-permute-done.1.refs_2_), channel_id=1, source_target_pairs={{0,1},{1,0},{2,3},{3,2},{4,5},{5,4},{6,7},{7,6},{8,9},{9,8},{10,11... | collective-permute-start | bytes 7864328 | tf_op jit(solution)/shard_map/ppermute | solution.py:28
  181.1 0.0 collective-permute-done.3.refs_4_
  181.1 0.1 collective-permute-start.7
  181.1 56.2 %collective-permute-done.4.refs_5_ = bf16[2,256,2560]{2,1,0:T(8,128)(2,1)} collective-permute-done((bf16[2,256,2560]{2,1,0:T(8,128)(2,1)S(1)}, bf16[2,256,2560]{2,1,0:T(8,128)(2,1)}, u32[]{:S(2)}, u32[]{:S(2)}) %collective-permute-start.4) | collective-permute-done | bytes 2621472 | tf_op jit(solution)/shard_map/ppermute | solution.py:24
  237.4 3.7 %collective-permute-start.8 = (bf16[2,256,2560]{2,1,0:T(8,128)(2,1)}, bf16[2,256,2560]{2,1,0:T(8,128)(2,1)}, u32[]{:S(2)}, u32[]{:S(2)}) collective-permute-start(bf16[2,256,2560]{2,1,0:T(8,128)(2,1)} %collective-permute-done.3.refs_4_), channel_id=1, source_target_pairs={{0,1},{1,0},{2,3},{3,2},{4,5},{5,4},{6,7},{7,6},{8,9},{9,8},{10,11... | collective-permute-start | bytes 7864328 | tf_op jit(solution)/shard_map/ppermute | solution.py:28
  241.1 0.0 collective-permute-done.refs_1_
  241.1 0.1 constant_dynamic-slice_fusion
  241.1 0.1 copy.22
  241.2 0.1 dynamic_slice.13
  241.4 0.1 iota_compare_fusion
  241.4 0.5 and_reduce_fusion
  242.0 0.1 copy.23
  242.1 0.1 copy.24
  242.2 0.1 copy.25
  242.3 0.1 copy.26
  242.4 0.1 copy.27
  242.5 0.1 copy.28
  242.7 0.1 copy.29
  242.8 0.1 copy.30
  242.9 0.1 copy.31
  243.0 0.1 copy.32
  243.1 0.1 copy.33
  243.2 0.1 stack.56
  243.4 0.1 copy.34
  243.5 0.6 reshape.70.mask_ref
  244.1 37.0 %collective-permute-done.5.refs_6_ = bf16[2,256,2560]{2,1,0:T(8,128)(2,1)} collective-permute-done((bf16[2,256,2560]{2,1,0:T(8,128)(2,1)}, bf16[2,256,2560]{2,1,0:T(8,128)(2,1)}, u32[]{:S(2)}, u32[]{:S(2)}) %collective-permute-start.5) | collective-permute-done | bytes 2621472 | tf_op jit(solution)/shard_map/ppermute | solution.py:38
  281.1 0.0 collective-permute-done.6.refs_7_
  281.1 0.0 collective-permute-done.7.refs_8_
  281.1 0.0 collective-permute-done.8.refs_9_
  281.2 1.5 copy-done.3
  282.7 28.5 %shard_map.64 = bf16[256,2560]{1,0:T(8,128)(2,1)} custom-call(s32[44]{0:T(128)} %reshape.70.mask_ref, bf16[256,2560]{1,0:T(8,128)(2,1)} %q_ref.1, bf16[2,256,2560]{2,1,0:T(8,128)(2,1)} %copy-done.2, bf16[2,256,2560]{2,1,0:T(8,128)(2,1)} %collective-permute-done.refs_1_, bf16[2,256,2560]{2,1,0:T(8,128)(2,1)} %collective-permute-done.1.refs_2_, ...), custom_call_target="tpu_custom_call" | custom-call | flops 7381975040 | bytes 31457280 | tf_op jit(solution)/shard_map/pallas_call | solution.py:92
  311.2 0.0 all-gather.2.cloned.1.call-done
  311.3 9.8 %fusion.7 = bf16[256,2560]{1,0:T(8,128)(2,1)} fusion(bf16[256,2560]{1,0:T(8,128)(2,1)} %shard_map.64, bf16[2560,5120]{0,1:T(8,128)(2,1)} %all-gather.2.cloned.1.call-done, s32[]{:T(128)S(6)} %select_n.22), kind=kOutput, calls=%fused_computation.5 | convolution fusion | flops 3356098560 | bytes 15728644 | tf_op jit(solution)/shard_map/dot_general | solution.py:145
  321.1 1.2 collective-permute-start.10
  322.3 8.3 %fusion.4 = bf16[256,2560]{1,0:T(8,128)(2,1)S(1)} fusion(bf16[256,2560]{1,0:T(8,128)(2,1)S(1)} %copy-done.4, bf16[2560,5120]{0,1:T(8,128)(2,1)} %all-gather.2.cloned.1.call-done, s32[]{:T(128)S(6)} %select_n.21), kind=kOutput, calls=%fused_computation.4 | convolution fusion | flops 3356098560 | bytes 15728644 | tf_op jit(solution)/shard_map/dot_general | solution.py:147
  330.6 20.3 %collective-permute-done.10 = bf16[256,2560]{1,0:T(8,128)(2,1)S(1)} collective-permute-done((bf16[256,2560]{1,0:T(8,128)(2,1)}, bf16[256,2560]{1,0:T(8,128)(2,1)S(1)}, u32[]{:S(2)}, u32[]{:S(2)}) %collective-permute-start.10) | collective-permute-done | bytes 1310752 | tf_op jit(solution)/shard_map/ppermute | solution.py:28
  350.9 1.4 add_convert_fusion
  (21 shorter events, 0.1 us)
Async XLA Ops:
  6.5 234.5 %copy-start = (s32[32,12]{0,1:T(8,128)S(1)}, s32[32,12]{0,1:T(8,128)}, u32[]{:S(2)}) copy-start(s32[32,12]{0,1:T(8,128)} %param.10) | copy-start | bytes 4612
  6.5 304.7 %all-gather.2.cloned.1.call-start = ((), (), s32[]{:S(2)}) async-start(), calls=%async_computation | async-start | bytes 27852800 | tf_op jit(solution)/shard_map/all_gather | solution.py:138
  9.2 121.4 %copy-start.2 = (bf16[2,256,2560]{2,1,0:T(8,128)(2,1)}, bf16[2,256,2560]{2,1,0:T(8,128)(2,1)S(1)}, u32[]{:S(2)}) copy-start(bf16[2,256,2560]{2,1,0:T(8,128)(2,1)S(1)} %pad_maximum_fusion.refs_0_) | copy-start | bytes 7864324
  9.2 110.1 %collective-permute-start.1 = (bf16[2,256,2560]{2,1,0:T(8,128)(2,1)S(1)}, bf16[2,256,2560]{2,1,0:T(8,128)(2,1)}, u32[]{:S(2)}, u32[]{:S(2)}) collective-permute-start(bf16[2,256,2560]{2,1,0:T(8,128)(2,1)S(1)} %pad_maximum_fusion.refs_0_), channel_id=1, source_target_pairs={{0,2},{2,4},{4,6},{6,8},{8,10},{10,12},{12,14},{1,3},{3,5},{5,7},{... | collective-permute-start | bytes 7864328 | tf_op jit(solution)/shard_map/ppermute | solution.py:24
  12.4 114.7 %collective-permute-start.2 = (bf16[2,256,2560]{2,1,0:T(8,128)(2,1)S(1)}, bf16[2,256,2560]{2,1,0:T(8,128)(2,1)}, u32[]{:S(2)}, u32[]{:S(2)}) collective-permute-start(bf16[2,256,2560]{2,1,0:T(8,128)(2,1)S(1)} %pad_maximum_fusion.refs_0_), channel_id=1, source_target_pairs={{2,0},{4,2},{6,4},{8,6},{10,8},{12,10},{14,12},{3,1},{5,3},{7,5},{... | collective-permute-start | bytes 7864328 | tf_op jit(solution)/shard_map/ppermute | solution.py:24
  15.4 165.6 %collective-permute-start.3 = (bf16[2,256,2560]{2,1,0:T(8,128)(2,1)S(1)}, bf16[2,256,2560]{2,1,0:T(8,128)(2,1)}, u32[]{:S(2)}, u32[]{:S(2)}) collective-permute-start(bf16[2,256,2560]{2,1,0:T(8,128)(2,1)S(1)} %pad_maximum_fusion.refs_0_), channel_id=1, source_target_pairs={{0,4},{2,6},{4,8},{6,10},{8,12},{10,14},{1,5},{3,7},{5,9},{7,11},{... | collective-permute-start | bytes 7864328 | tf_op jit(solution)/shard_map/ppermute | solution.py:24
  18.6 218.8 %collective-permute-start.4 = (bf16[2,256,2560]{2,1,0:T(8,128)(2,1)S(1)}, bf16[2,256,2560]{2,1,0:T(8,128)(2,1)}, u32[]{:S(2)}, u32[]{:S(2)}) collective-permute-start(bf16[2,256,2560]{2,1,0:T(8,128)(2,1)S(1)} %pad_maximum_fusion.refs_0_), channel_id=1, source_target_pairs={{4,0},{6,2},{8,4},{10,6},{12,8},{14,10},{5,1},{7,3},{9,5},{11,7},{... | collective-permute-start | bytes 7864328 | tf_op jit(solution)/shard_map/ppermute | solution.py:24
  22.2 218.9 %collective-permute-start = (bf16[2,256,2560]{2,1,0:T(8,128)(2,1)S(1)}, bf16[2,256,2560]{2,1,0:T(8,128)(2,1)}, u32[]{:S(2)}, u32[]{:S(2)}) collective-permute-start(bf16[2,256,2560]{2,1,0:T(8,128)(2,1)S(1)} %pad_maximum_fusion.refs_0_), channel_id=1, source_target_pairs={{0,1},{1,0},{2,3},{3,2},{4,5},{5,4},{6,7},{7,6},{8,9},{9,8},{10,11... | collective-permute-start | bytes 7864328 | tf_op jit(solution)/shard_map/ppermute | solution.py:28
  24.0 217.2 %copy-start.5 = (s32[32]{0:T(128)S(1)}, s32[32]{0:T(128)}, u32[]{:S(2)}) copy-start(s32[32]{0:T(128)} %param.11) | copy-start | bytes 388
  130.7 150.5 %collective-permute-start.5 = (bf16[2,256,2560]{2,1,0:T(8,128)(2,1)}, bf16[2,256,2560]{2,1,0:T(8,128)(2,1)}, u32[]{:S(2)}, u32[]{:S(2)}) collective-permute-start(bf16[2,256,2560]{2,1,0:T(8,128)(2,1)} %broadcast_select_fusion), channel_id=1, source_target_pairs={{1,4},{3,6},{4,1},{5,8},{6,3},{7,10},{8,5},{9,12},{10,7},{11,14},{... | collective-permute-start | bytes 7864328 | tf_op jit(solution)/shard_map/ppermute | solution.py:38
  136.3 144.8 %collective-permute-start.6 = (bf16[2,256,2560]{2,1,0:T(8,128)(2,1)}, bf16[2,256,2560]{2,1,0:T(8,128)(2,1)}, u32[]{:S(2)}, u32[]{:S(2)}) collective-permute-start(bf16[2,256,2560]{2,1,0:T(8,128)(2,1)} %collective-permute-done.1.refs_2_), channel_id=1, source_target_pairs={{0,1},{1,0},{2,3},{3,2},{4,5},{5,4},{6,7},{7,6},{8,9},{9,8},{10,11... | collective-permute-start | bytes 7864328 | tf_op jit(solution)/shard_map/ppermute | solution.py:28
  181.1 100.1 %collective-permute-start.7 = (bf16[2,256,2560]{2,1,0:T(8,128)(2,1)}, bf16[2,256,2560]{2,1,0:T(8,128)(2,1)}, u32[]{:S(2)}, u32[]{:S(2)}) collective-permute-start(bf16[2,256,2560]{2,1,0:T(8,128)(2,1)} %collective-permute-done.2.refs_3_), channel_id=1, source_target_pairs={{0,1},{1,0},{2,3},{3,2},{4,5},{5,4},{6,7},{7,6},{8,9},{9,8},{10,11... | collective-permute-start | bytes 7864328 | tf_op jit(solution)/shard_map/ppermute | solution.py:28
  237.4 43.7 %collective-permute-start.8 = (bf16[2,256,2560]{2,1,0:T(8,128)(2,1)}, bf16[2,256,2560]{2,1,0:T(8,128)(2,1)}, u32[]{:S(2)}, u32[]{:S(2)}) collective-permute-start(bf16[2,256,2560]{2,1,0:T(8,128)(2,1)} %collective-permute-done.3.refs_4_), channel_id=1, source_target_pairs={{0,1},{1,0},{2,3},{3,2},{4,5},{5,4},{6,7},{7,6},{8,9},{9,8},{10,11... | collective-permute-start | bytes 7864328 | tf_op jit(solution)/shard_map/ppermute | solution.py:28
  241.1 40.1 %collective-permute-start.9 = (bf16[2,256,2560]{2,1,0:T(8,128)(2,1)}, bf16[2,256,2560]{2,1,0:T(8,128)(2,1)S(1)}, u32[]{:S(2)}, u32[]{:S(2)}) collective-permute-start(bf16[2,256,2560]{2,1,0:T(8,128)(2,1)} %collective-permute-done.4.refs_5_), channel_id=1, source_target_pairs={{0,1},{1,0},{2,3},{3,2},{4,5},{5,4},{6,7},{7,6},{8,9},{9,8},{10,11... | collective-permute-start | bytes 7864328 | tf_op jit(solution)/shard_map/ppermute | solution.py:28
  281.2 1.6 copy-start.3
  311.2 11.1 %copy-start.4 = (bf16[256,2560]{1,0:T(8,128)(2,1)S(1)}, bf16[256,2560]{1,0:T(8,128)(2,1)}, u32[]{:S(2)}) copy-start(bf16[256,2560]{1,0:T(8,128)(2,1)} %shard_map.64) | copy-start | bytes 3932164
  321.1 29.8 %collective-permute-start.10 = (bf16[256,2560]{1,0:T(8,128)(2,1)}, bf16[256,2560]{1,0:T(8,128)(2,1)S(1)}, u32[]{:S(2)}, u32[]{:S(2)}) collective-permute-start(bf16[256,2560]{1,0:T(8,128)(2,1)} %fusion.7), channel_id=1, source_target_pairs={{0,16},{16,0},{1,17},{17,1},{2,18},{18,2},{3,19},{19,3},{4,20},{20... | collective-permute-start | bytes 3932168 | tf_op jit(solution)/shard_map/ppermute | solution.py:28
  322.3 30.0 %copy-start.1 = (s32[32,12]{0,1:T(8,128)S(1)}, s32[32,12]{0,1:T(8,128)}, u32[]{:S(2)}) copy-start(s32[32,12]{0,1:T(8,128)} %param.10) | copy-start | bytes 4612
Sparse Core Ops, SparseCore 0:
  9.0 254.6 all-gather.1

commit v5 on v4

--- a/solution.py
+++ b/solution.py
@@ -38,10 +38,19 @@
     return lax.ppermute(x, SEQ, pairs)
 
 
-def attention_kernel(n_blocks, tiles, group, mask_ref, q_ref, *refs):
+def attention_kernel(n_blocks, tiles, group, carry_in, finish, mask_ref, q_ref, *refs):
     kv_refs = refs[:n_blocks]
-    out_ref = refs[n_blocks]
-    score_ref = refs[n_blocks + 1]
+    at = n_blocks
+    if carry_in:
+        acc_in, peak_in, total_in = refs[at:at + 3]
+        at += 3
+    if finish:
+        out_ref = refs[at]
+        at += 1
+    else:
+        acc_out, peak_out, total_out = refs[at:at + 3]
+        at += 3
+    score_ref = refs[at]
     rows = q_ref.shape[0]
     for g in range(group):
         cols = slice(g * HD, (g + 1) * HD)
@@ -61,6 +70,10 @@
 
         scores = score_ref[...]
         peak = jnp.max(scores, axis=1, keepdims=True)
+        if carry_in:
+            old_peak = peak_in[:, g * HD:g * HD + 1]
+            peak = jnp.maximum(peak, old_peak)
+            carried = jnp.exp(old_peak - peak)
         weights = jnp.exp(scores - peak)
         totals = jnp.sum(weights, axis=1, keepdims=True)
         rounded = weights.astype(jnp.bfloat16)
@@ -69,10 +82,18 @@
             summed = summed + jnp.dot(
                 rounded[:, b * rows:(b + 1) * rows], kv_refs[b][1, :, cols], preferred_element_type=jnp.float32
             )
-        out_ref[:, cols] = (summed / totals).astype(out_ref.dtype)
-
-
-def block_attention(queries, kv_list, flat_masks):
+        if carry_in:
+            totals = carried * total_in[:, g * HD:g * HD + 1] + totals
+            summed = carried * acc_in[:, cols] + summed
+        if finish:
+            out_ref[:, cols] = (summed / totals).astype(out_ref.dtype)
+        else:
+            acc_out[:, cols] = summed
+            peak_out[:, cols] = jnp.broadcast_to(peak, (rows, HD))
+            total_out[:, cols] = jnp.broadcast_to(totals, (rows, HD))
+
+
+def block_attention(queries, kv_list, flat_masks, carry=None, finish=True):
     rows, width = queries.shape
     heads = width // HD
     group = 5 if heads % 5 == 0 else 1
@@ -80,23 +101,36 @@
     tiles = rows // TILE
     span = group * HD
     kv_spec = pl.BlockSpec((2, rows, span), lambda h, m: (0, 0, h))
+    row_spec = pl.BlockSpec((rows, span), lambda h, m: (0, h))
+    state_shape = jax.ShapeDtypeStruct((rows, width), jnp.float32)
+    in_specs = [row_spec] + [kv_spec] * n_blocks
+    operands = [flat_masks, queries, *kv_list]
+    if carry is not None:
+        in_specs += [row_spec] * 3
+        operands += list(carry)
+    if finish:
+        out_shape = jax.ShapeDtypeStruct((rows, width), jnp.bfloat16)
+        out_specs = row_spec
+    else:
+        out_shape = (state_shape,) * 3
+        out_specs = (row_spec,) * 3
     grid_spec = pltpu.PrefetchScalarGridSpec(
         num_scalar_prefetch=1,
         grid=(heads // group,),
-        in_specs=[pl.BlockSpec((rows, span), lambda h, m: (0, h))] + [kv_spec] * n_blocks,
-        out_specs=pl.BlockSpec((rows, span), lambda h, m: (0, h)),
+        in_specs=in_specs,
+        out_specs=out_specs,
         scratch_shapes=[pltpu.VMEM((rows, n_blocks * rows), jnp.float32)],
     )
     flops = 4 * rows * n_blocks * rows * HD * heads
-    bytes_moved = 2 * (rows * width * 2 + n_blocks * 2 * rows * width)
+    bytes_moved = 2 * (rows * width * 2 + n_blocks * 2 * rows * width) + 24 * rows * width
     return pl.pallas_call(
-        functools.partial(attention_kernel, n_blocks, tiles, group),
+        functools.partial(attention_kernel, n_blocks, tiles, group, carry is not None, finish),
         grid_spec=grid_spec,
-        out_shape=jax.ShapeDtypeStruct((rows, width), jnp.bfloat16),
+        out_shape=out_shape,
         cost_estimate=pl.CostEstimate(
             flops=flops, transcendentals=rows * n_blocks * rows * heads, bytes_accessed=bytes_moved
         ),
-    )(flat_masks, queries, *kv_list)
+    )(*operands)
 
 
 def local(queries, keys, values, out_weight, tile_lists, tile_counts):
@@ -117,24 +151,27 @@
         matches = (own_lists[:, :, None] == key_tiles[None, None, :]) & live_slots[:, :, None]
         return jnp.any(matches, axis=1)
 
-    kv_blocks = [(0, stacked)]
+    early = [(0, stacked)]
     sibling = swapped(stacked, "core")
-    kv_blocks.append((1 - 2 * core, sibling))
+    early.append((1 - 2 * core, sibling))
     fetched = []
     for chip_step in (1, 2):
         for sign in (1, -1):
             block = shifted(stacked, "chip", sign * chip_step)
             fetched.append((-sign * 2 * chip_step, block))
-            kv_blocks.append((-sign * 2 * chip_step, block))
+            early.append((-sign * 2 * chip_step, block))
     from_below, from_above = fetched[0][1], fetched[1][1]
     onward = jnp.where(core == 1, from_below, from_above)
-    kv_blocks.append((-REACH + 2 * REACH * core, third_neighbour(onward, chips)))
+    late = [(-REACH + 2 * REACH * core, third_neighbour(onward, chips))]
     for offset, block in fetched:
         passed = swapped(block, "core")
-        kv_blocks.append((offset + 1 - 2 * core, passed))
-
-    tile_masks = jnp.stack([tile_need(offset) for offset, _ in kv_blocks]).astype(jnp.int32)
-    attended = block_attention(queries, [b for _, b in kv_blocks], tile_masks.reshape(-1))
+        late.append((offset + 1 - 2 * core, passed))
+
+    def masks_of(blocks):
+        return jnp.stack([tile_need(offset) for offset, _ in blocks]).astype(jnp.int32).reshape(-1)
+
+    carry = block_attention(queries, [b for _, b in early], masks_of(early), finish=False)
+    attended = block_attention(queries, [b for _, b in late], masks_of(late), carry=carry)
     weight_rows = lax.all_gather(out_weight, SEQ, axis=1, tiled=True)
     heads = lax.axis_size("head")
     if heads == 2:

time: 359 us -> 350 us (0.975)
  waiting for transfers between devices: 217 us -> 200 us
  Pallas kernels: 28.5 us -> 37 us
    ppermute x1, waiting for transfers between devices: 37 us -> 17 us  [third_neighbour(): return lax.ppermute(x, SEQ, pairs)]
    pallas_call x1 -> x2, Pallas kernels: 28.5 us -> 37 us  [block_attention(): pl.pallas_call(functools.partial(attention_kernel, n_blocks, tiles, group...]
  transfers between devices with their start and end apart: 12 -> 12, of which waited for: 5 -> 5; matrix products, arithmetic and copies ran while one was open for 5% -> 5% of each run, Pallas kernels for 8% -> 11%
where the time goes in v5:
time: 350 us; the launch traced here: 349 us
  waiting for transfers between devices  200 us (57%)
  starting transfers between devices  70.2 us (20%)
  Pallas kernels  37 us (11%)
  matrix products  18.2 us (5%)
  between operations  13.5 us (4%)
  other arithmetic  7.37 us (2%)
    ppermute x4, waiting for transfers between devices, shifted(): return lax.ppermute(x, axis, pairs)  162 us
    ppermute x6, starting transfers between devices, swapped(): return lax.ppermute(x, axis, [(0, 1), (1, 0)])  50.3 us
    pallas_call x2, Pallas kernels, block_attention(): pl.pallas_call(functools.partial(attention_kernel, n_blocks, tiles, group...  37 us
    ppermute x6, waiting for transfers between devices, swapped(): return lax.ppermute(x, axis, [(0, 1), (1, 0)])  20.4 us
    ppermute x1, waiting for transfers between devices, third_neighbour(): return lax.ppermute(x, SEQ, pairs)  17 us
    ppermute x4, starting transfers between devices, shifted(): return lax.ppermute(x, axis, pairs)  13 us
    dot_general x1, matrix products, local(): jnp.dot(attended, theirs, preferred_element_type=jnp.float32)  9.85 us
    dot_general x1, matrix products, local(): jnp.dot(attended, mine, preferred_element_type=jnp.float32)  8.31 us
  transfers between devices with their start and end apart: 12, of which 5 were waited for; matrix products, arithmetic and copies ran while one was open for 5% of the time, Pallas kernels for 11%

profile of v5, /device:TPU:9, one launch (start us, length us, event | category | flops | bytes accessed | tf_op | source)
XLA Modules:
  0.0 349.5 jit_solution(9829791114055053804)
XLA Ops:
  6.5 0.7 all-gather.2.cloned.1.call-update
  7.3 3.4 pad_maximum_fusion.refs_0_
  10.7 3.1 collective-permute-start
  13.8 3.0 collective-permute-start.1
  16.9 3.2 collective-permute-start.5
  20.1 3.6 %collective-permute-start.7 = (bf16[2,256,2560]{2,1,0:T(8,128)(2,1)}, bf16[2,256,2560]{2,1,0:T(8,128)(2,1)}, u32[]{:S(2)}, u32[]{:S(2)}) collective-permute-start(bf16[2,256,2560]{2,1,0:T(8,128)(2,1)} %pad_maximum_fusion.refs_0_), channel_id=1, source_target_pairs={{4,0},{6,2},{8,4},{10,6},{12,8},{14,10},{5,1},{7,3},{9,5},{11,7},{... | collective-permute-start | bytes 7864328 | tf_op jit(solution)/shard_map/ppermute | solution.py:24
  23.7 1.9 collective-permute-start.9
  25.6 94.4 %collective-permute-done.refs_2_ = bf16[2,256,2560]{2,1,0:T(8,128)(2,1)S(1)} collective-permute-done((bf16[2,256,2560]{2,1,0:T(8,128)(2,1)}, bf16[2,256,2560]{2,1,0:T(8,128)(2,1)S(1)}, u32[]{:S(2)}, u32[]{:S(2)}) %collective-permute-start) | collective-permute-done | bytes 2621472 | tf_op jit(solution)/shard_map/ppermute | solution.py:24
  119.9 9.2 %collective-permute-done.1.refs_3_ = bf16[2,256,2560]{2,1,0:T(8,128)(2,1)} collective-permute-done((bf16[2,256,2560]{2,1,0:T(8,128)(2,1)}, bf16[2,256,2560]{2,1,0:T(8,128)(2,1)}, u32[]{:S(2)}, u32[]{:S(2)}) %collective-permute-start.1) | collective-permute-done | bytes 2621472 | tf_op jit(solution)/shard_map/ppermute | solution.py:24
  129.2 1.9 broadcast_select_fusion
  131.1 6.9 %collective-permute-start.2 = (bf16[2,256,2560]{2,1,0:T(8,128)(2,1)}, bf16[2,256,2560]{2,1,0:T(8,128)(2,1)}, u32[]{:S(2)}, u32[]{:S(2)}) collective-permute-start(bf16[2,256,2560]{2,1,0:T(8,128)(2,1)} %broadcast_select_fusion), channel_id=1, source_target_pairs={{1,4},{3,6},{4,1},{5,8},{6,3},{7,10},{8,5},{9,12},{10,7},{11,14},{... | collective-permute-start | bytes 7864328 | tf_op jit(solution)/shard_map/ppermute | solution.py:38
  138.0 45.1 %collective-permute-start.3 = (bf16[2,256,2560]{2,1,0:T(8,128)(2,1)S(1)}, bf16[2,256,2560]{2,1,0:T(8,128)(2,1)}, u32[]{:S(2)}, u32[]{:S(2)}) collective-permute-start(bf16[2,256,2560]{2,1,0:T(8,128)(2,1)S(1)} %collective-permute-done.refs_2_), channel_id=1, source_target_pairs={{0,1},{1,0},{2,3},{3,2},{4,5},{5,4},{6,7},{7,6},{8,9},{9,8},{10,11... | collective-permute-start | bytes 7864328 | tf_op jit(solution)/shard_map/ppermute | solution.py:28
  183.2 0.1 collective-permute-start.4
  183.3 58.3 %collective-permute-done.7.refs_5_ = bf16[2,256,2560]{2,1,0:T(8,128)(2,1)} collective-permute-done((bf16[2,256,2560]{2,1,0:T(8,128)(2,1)}, bf16[2,256,2560]{2,1,0:T(8,128)(2,1)}, u32[]{:S(2)}, u32[]{:S(2)}) %collective-permute-start.7) | collective-permute-done | bytes 2621472 | tf_op jit(solution)/shard_map/ppermute | solution.py:24
  241.5 2.0 collective-permute-start.6
  243.6 0.0 collective-permute-done.9.refs_1_
  243.6 0.0 collective-permute-start.8
  243.6 0.1 constant_dynamic-slice_fusion
  243.6 0.1 copy.23
  243.7 0.1 dynamic_slice.13
  243.9 0.1 iota_compare_fusion
  243.9 0.5 and_reduce_fusion
  244.5 0.1 copy.30
  244.6 0.1 copy.31
  244.7 0.1 copy.32
  244.8 0.1 copy.33
  244.9 0.1 copy.34
  245.0 0.1 copy.35
  245.2 0.1 stack.63
  245.3 0.1 copy.36
  245.4 0.6 reshape.75.mask_ref
  246.0 0.1 copy.24
  246.1 0.1 copy.25
  246.2 0.1 copy.26
  246.3 0.1 copy.27
  246.4 0.1 copy.28
  246.6 0.1 stack.53
  246.7 0.1 copy.29
  246.8 0.7 reshape.74.mask_ref
  247.4 17.7 %shard_map.64 = (f32[256,2560]{1,0:T(8,128)}, f32[256,2560]{1,0:T(8,128)}, f32[256,2560]{1,0:T(8,128)}) custom-call(s32[24]{0:T(128)} %reshape.75.mask_ref, bf16[256,2560]{1,0:T(8,128)(2,1)} %q_ref.3, bf16[2,256,2560]{2,1,0:T(8,128)(2,1)} %pad_maximum_fusion.refs_0_, bf16[2,256,2560]{2,1,0:T(8,128)(2,1)} %collective-permute-done.9.refs_1_, ...), custom_call_target="tpu_custom_call" | custom-call | flops 4026531840 | bytes 34078720 | tf_op jit(solution)/shard_map/pallas_call | solution.py:126
  265.1 17.0 %collective-permute-done.2.refs_0_ = bf16[2,256,2560]{2,1,0:T(8,128)(2,1)} collective-permute-done((bf16[2,256,2560]{2,1,0:T(8,128)(2,1)}, bf16[2,256,2560]{2,1,0:T(8,128)(2,1)}, u32[]{:S(2)}, u32[]{:S(2)}) %collective-permute-start.2) | collective-permute-done | bytes 2621472 | tf_op jit(solution)/shard_map/ppermute | solution.py:38
  282.1 19.3 %shard_map.65 = bf16[256,2560]{1,0:T(8,128)(2,1)} custom-call(s32[20]{0:T(128)} %reshape.74.mask_ref, bf16[256,2560]{1,0:T(8,128)(2,1)} %q_ref.3, bf16[2,256,2560]{2,1,0:T(8,128)(2,1)} %collective-permute-done.2.refs_0_, bf16[2,256,2560]{2,1,0:T(8,128)(2,1)} %collective-permute-done.3.refs_1_, bf16[2,256,2560]{2,1,0:T(8,128)(2,1)} %collective-permute-done.4.refs_2_, ...), custom_call_target="tpu_custom_call" | custom-call | flops 3355443200 | bytes 31457280 | tf_op jit(solution)/shard_map/pallas_call | solution.py:126
  301.5 0.0 all-gather.2.cloned.1.call-done
  301.5 9.8 %fusion.7 = bf16[256,2560]{1,0:T(8,128)(2,1)} fusion(bf16[256,2560]{1,0:T(8,128)(2,1)} %shard_map.65, bf16[2560,5120]{0,1:T(8,128)(2,1)} %all-gather.2.cloned.1.call-done, s32[]{:T(128)S(6)} %select_n.22), kind=kOutput, calls=%fused_computation.5 | convolution fusion | flops 3356098560 | bytes 15728644 | tf_op jit(solution)/shard_map/dot_general | solution.py:182
  311.3 1.2 collective-permute-start.10
  312.5 8.3 %fusion.4 = bf16[256,2560]{1,0:T(8,128)(2,1)S(1)} fusion(bf16[256,2560]{1,0:T(8,128)(2,1)S(1)} %copy-done.3, bf16[2560,5120]{0,1:T(8,128)(2,1)} %all-gather.2.cloned.1.call-done, s32[]{:T(128)S(6)} %select_n.21), kind=kOutput, calls=%fused_computation.4 | convolution fusion | flops 3356098560 | bytes 15728644 | tf_op jit(solution)/shard_map/dot_general | solution.py:184
  320.9 20.4 %collective-permute-done.10 = bf16[256,2560]{1,0:T(8,128)(2,1)S(1)} collective-permute-done((bf16[256,2560]{1,0:T(8,128)(2,1)}, bf16[256,2560]{1,0:T(8,128)(2,1)S(1)}, u32[]{:S(2)}, u32[]{:S(2)}) %collective-permute-start.10) | collective-permute-done | bytes 1310752 | tf_op jit(solution)/shard_map/ppermute | solution.py:28
  341.3 1.4 add_convert_fusion
  (24 shorter events, 0.1 us)
Async XLA Ops:
  6.5 237.0 %copy-start = (s32[32,12]{0,1:T(8,128)S(1)}, s32[32,12]{0,1:T(8,128)}, u32[]{:S(2)}) copy-start(s32[32,12]{0,1:T(8,128)} %param.10) | copy-start | bytes 4612
  6.5 294.9 %all-gather.2.cloned.1.call-start = ((), (), s32[]{:S(2)}) async-start(), calls=%async_computation | async-start | bytes 27852800 | tf_op jit(solution)/shard_map/all_gather | solution.py:175
  10.7 109.2 %collective-permute-start = (bf16[2,256,2560]{2,1,0:T(8,128)(2,1)}, bf16[2,256,2560]{2,1,0:T(8,128)(2,1)S(1)}, u32[]{:S(2)}, u32[]{:S(2)}) collective-permute-start(bf16[2,256,2560]{2,1,0:T(8,128)(2,1)} %pad_maximum_fusion.refs_0_), channel_id=1, source_target_pairs={{0,2},{2,4},{4,6},{6,8},{8,10},{10,12},{12,14},{1,3},{3,5},{5,7},{... | collective-permute-start | bytes 7864328 | tf_op jit(solution)/shard_map/ppermute | solution.py:24
  13.8 115.3 %collective-permute-start.1 = (bf16[2,256,2560]{2,1,0:T(8,128)(2,1)}, bf16[2,256,2560]{2,1,0:T(8,128)(2,1)}, u32[]{:S(2)}, u32[]{:S(2)}) collective-permute-start(bf16[2,256,2560]{2,1,0:T(8,128)(2,1)} %pad_maximum_fusion.refs_0_), channel_id=1, source_target_pairs={{2,0},{4,2},{6,4},{8,6},{10,8},{12,10},{14,12},{3,1},{5,3},{7,5},{... | collective-permute-start | bytes 7864328 | tf_op jit(solution)/shard_map/ppermute | solution.py:24
  16.9 166.3 %collective-permute-start.5 = (bf16[2,256,2560]{2,1,0:T(8,128)(2,1)}, bf16[2,256,2560]{2,1,0:T(8,128)(2,1)}, u32[]{:S(2)}, u32[]{:S(2)}) collective-permute-start(bf16[2,256,2560]{2,1,0:T(8,128)(2,1)} %pad_maximum_fusion.refs_0_), channel_id=1, source_target_pairs={{0,4},{2,6},{4,8},{6,10},{8,12},{10,14},{1,5},{3,7},{5,9},{7,11},{... | collective-permute-start | bytes 7864328 | tf_op jit(solution)/shard_map/ppermute | solution.py:24
  20.1 221.4 %collective-permute-start.7 = (bf16[2,256,2560]{2,1,0:T(8,128)(2,1)}, bf16[2,256,2560]{2,1,0:T(8,128)(2,1)}, u32[]{:S(2)}, u32[]{:S(2)}) collective-permute-start(bf16[2,256,2560]{2,1,0:T(8,128)(2,1)} %pad_maximum_fusion.refs_0_), channel_id=1, source_target_pairs={{4,0},{6,2},{8,4},{10,6},{12,8},{14,10},{5,1},{7,3},{9,5},{11,7},{... | collective-permute-start | bytes 7864328 | tf_op jit(solution)/shard_map/ppermute | solution.py:24
  23.7 219.9 %collective-permute-start.9 = (bf16[2,256,2560]{2,1,0:T(8,128)(2,1)}, bf16[2,256,2560]{2,1,0:T(8,128)(2,1)}, u32[]{:S(2)}, u32[]{:S(2)}) collective-permute-start(bf16[2,256,2560]{2,1,0:T(8,128)(2,1)} %pad_maximum_fusion.refs_0_), channel_id=1, source_target_pairs={{0,1},{1,0},{2,3},{3,2},{4,5},{5,4},{6,7},{7,6},{8,9},{9,8},{10,11... | collective-permute-start | bytes 7864328 | tf_op jit(solution)/shard_map/ppermute | solution.py:28
  25.6 218.2 %copy-start.4 = (s32[32]{0:T(128)S(1)}, s32[32]{0:T(128)}, u32[]{:S(2)}) copy-start(s32[32]{0:T(128)} %param.11) | copy-start | bytes 388
  119.9 18.1 %copy-start.2 = (bf16[2,256,2560]{2,1,0:T(8,128)(2,1)}, bf16[2,256,2560]{2,1,0:T(8,128)(2,1)S(1)}, u32[]{:S(2)}) copy-start(bf16[2,256,2560]{2,1,0:T(8,128)(2,1)S(1)} %collective-permute-done.refs_2_) | copy-start | bytes 7864324
  131.1 151.0 %collective-permute-start.2 = (bf16[2,256,2560]{2,1,0:T(8,128)(2,1)}, bf16[2,256,2560]{2,1,0:T(8,128)(2,1)}, u32[]{:S(2)}, u32[]{:S(2)}) collective-permute-start(bf16[2,256,2560]{2,1,0:T(8,128)(2,1)} %broadcast_select_fusion), channel_id=1, source_target_pairs={{1,4},{3,6},{4,1},{5,8},{6,3},{7,10},{8,5},{9,12},{10,7},{11,14},{... | collective-permute-start | bytes 7864328 | tf_op jit(solution)/shard_map/ppermute | solution.py:38
  138.0 144.1 %collective-permute-start.3 = (bf16[2,256,2560]{2,1,0:T(8,128)(2,1)S(1)}, bf16[2,256,2560]{2,1,0:T(8,128)(2,1)}, u32[]{:S(2)}, u32[]{:S(2)}) collective-permute-start(bf16[2,256,2560]{2,1,0:T(8,128)(2,1)S(1)} %collective-permute-done.refs_2_), channel_id=1, source_target_pairs={{0,1},{1,0},{2,3},{3,2},{4,5},{5,4},{6,7},{7,6},{8,9},{9,8},{10,11... | collective-permute-start | bytes 7864328 | tf_op jit(solution)/shard_map/ppermute | solution.py:28
  183.2 98.9 %collective-permute-start.4 = (bf16[2,256,2560]{2,1,0:T(8,128)(2,1)}, bf16[2,256,2560]{2,1,0:T(8,128)(2,1)}, u32[]{:S(2)}, u32[]{:S(2)}) collective-permute-start(bf16[2,256,2560]{2,1,0:T(8,128)(2,1)} %collective-permute-done.1.refs_3_), channel_id=1, source_target_pairs={{0,1},{1,0},{2,3},{3,2},{4,5},{5,4},{6,7},{7,6},{8,9},{9,8},{10,11... | collective-permute-start | bytes 7864328 | tf_op jit(solution)/shard_map/ppermute | solution.py:28
  241.5 40.6 %collective-permute-start.6 = (bf16[2,256,2560]{2,1,0:T(8,128)(2,1)}, bf16[2,256,2560]{2,1,0:T(8,128)(2,1)}, u32[]{:S(2)}, u32[]{:S(2)}) collective-permute-start(bf16[2,256,2560]{2,1,0:T(8,128)(2,1)} %collective-permute-done.5.refs_4_), channel_id=1, source_target_pairs={{0,1},{1,0},{2,3},{3,2},{4,5},{5,4},{6,7},{7,6},{8,9},{9,8},{10,11... | collective-permute-start | bytes 7864328 | tf_op jit(solution)/shard_map/ppermute | solution.py:28
  243.6 38.6 %collective-permute-start.8 = (bf16[2,256,2560]{2,1,0:T(8,128)(2,1)}, bf16[2,256,2560]{2,1,0:T(8,128)(2,1)}, u32[]{:S(2)}, u32[]{:S(2)}) collective-permute-start(bf16[2,256,2560]{2,1,0:T(8,128)(2,1)} %collective-permute-done.7.refs_5_), channel_id=1, source_target_pairs={{0,1},{1,0},{2,3},{3,2},{4,5},{5,4},{6,7},{7,6},{8,9},{9,8},{10,11... | collective-permute-start | bytes 7864328 | tf_op jit(solution)/shard_map/ppermute | solution.py:28
  301.5 11.1 %copy-start.3 = (bf16[256,2560]{1,0:T(8,128)(2,1)S(1)}, bf16[256,2560]{1,0:T(8,128)(2,1)}, u32[]{:S(2)}) copy-start(bf16[256,2560]{1,0:T(8,128)(2,1)} %shard_map.65) | copy-start | bytes 3932164
  311.3 29.9 %collective-permute-start.10 = (bf16[256,2560]{1,0:T(8,128)(2,1)}, bf16[256,2560]{1,0:T(8,128)(2,1)S(1)}, u32[]{:S(2)}, u32[]{:S(2)}) collective-permute-start(bf16[256,2560]{1,0:T(8,128)(2,1)} %fusion.7), channel_id=1, source_target_pairs={{0,16},{16,0},{1,17},{17,1},{2,18},{18,2},{3,19},{19,3},{4,20},{20... | collective-permute-start | bytes 3932168 | tf_op jit(solution)/shard_map/ppermute | solution.py:28
  312.5 30.1 %copy-start.1 = (s32[32,12]{0,1:T(8,128)S(1)}, s32[32,12]{0,1:T(8,128)}, u32[]{:S(2)}) copy-start(s32[32,12]{0,1:T(8,128)} %param.10) | copy-start | bytes 4612
Sparse Core Ops, SparseCore 0:
  9.0 256.0 all-gather.1

commit v6 on v5

--- a/solution.py
+++ b/solution.py
@@ -38,7 +38,7 @@
     return lax.ppermute(x, SEQ, pairs)
 
 
-def attention_kernel(n_blocks, tiles, group, carry_in, finish, mask_ref, q_ref, *refs):
+def attention_kernel(n_blocks, q_tiles, k_tiles, group, carry_in, finish, mask_ref, q_ref, *refs):
     kv_refs = refs[:n_blocks]
     at = n_blocks
     if carry_in:
@@ -52,6 +52,7 @@
         at += 3
     score_ref = refs[at]
     rows = q_ref.shape[0]
+    k_rows = k_tiles * TILE
     for g in range(group):
         cols = slice(g * HD, (g + 1) * HD)
         query = q_ref[:, cols]
@@ -60,11 +61,11 @@
             scores = lax.dot_general(
                 query, keys, (((1,), (1,)), ((), ())), preferred_element_type=jnp.float32
             ) * (1.0 / math.sqrt(HD))
-            for qi in range(tiles):
-                for kt in range(tiles):
-                    flag = mask_ref[(b * tiles + qi) * tiles + kt]
+            for qi in range(q_tiles):
+                for kt in range(k_tiles):
+                    flag = mask_ref[(b * q_tiles + qi) * k_tiles + kt]
                     tile = scores[qi * TILE:(qi + 1) * TILE, kt * TILE:(kt + 1) * TILE]
-                    score_ref[qi * TILE:(qi + 1) * TILE, b * rows + kt * TILE:b * rows + (kt + 1) * TILE] = (
+                    score_ref[qi * TILE:(qi + 1) * TILE, b * k_rows + kt * TILE:b * k_rows + (kt + 1) * TILE] = (
                         jnp.where(flag != 0, tile, masked_floor)
                     )
 
@@ -80,7 +81,7 @@
         summed = jnp.zeros((rows, HD), jnp.float32)
         for b in range(n_blocks):
             summed = summed + jnp.dot(
-                rounded[:, b * rows:(b + 1) * rows], kv_refs[b][1, :, cols], preferred_element_type=jnp.float32
+                rounded[:, b * k_rows:(b + 1) * k_rows], kv_refs[b][1, :, cols], preferred_element_type=jnp.float32
             )
         if carry_in:
             totals = carried * total_in[:, g * HD:g * HD + 1] + totals
@@ -95,12 +96,12 @@
 
 def block_attention(queries, kv_list, flat_masks, carry=None, finish=True):
     rows, width = queries.shape
+    k_rows = kv_list[0].shape[1]
     heads = width // HD
     group = 5 if heads % 5 == 0 else 1
     n_blocks = len(kv_list)
-    tiles = rows // TILE
     span = group * HD
-    kv_spec = pl.BlockSpec((2, rows, span), lambda h, m: (0, 0, h))
+    kv_spec = pl.BlockSpec((2, k_rows, span), lambda h, m: (0, 0, h))
     row_spec = pl.BlockSpec((rows, span), lambda h, m: (0, h))
     state_shape = jax.ShapeDtypeStruct((rows, width), jnp.float32)
     in_specs = [row_spec] + [kv_spec] * n_blocks
@@ -119,16 +120,16 @@
         grid=(heads // group,),
         in_specs=in_specs,
         out_specs=out_specs,
-        scratch_shapes=[pltpu.VMEM((rows, n_blocks * rows), jnp.float32)],
+        scratch_shapes=[pltpu.VMEM((rows, n_blocks * k_rows), jnp.float32)],
     )
-    flops = 4 * rows * n_blocks * rows * HD * heads
-    bytes_moved = 2 * (rows * width * 2 + n_blocks * 2 * rows * width) + 24 * rows * width
+    flops = 4 * rows * n_blocks * k_rows * HD * heads
+    bytes_moved = 2 * (rows * width + n_blocks * 2 * k_rows * width) + 24 * rows * width
     return pl.pallas_call(
-        functools.partial(attention_kernel, n_blocks, tiles, group, carry is not None, finish),
+        functools.partial(attention_kernel, n_blocks, rows // TILE, k_rows // TILE, group, carry is not None, finish),
         grid_spec=grid_spec,
         out_shape=out_shape,
         cost_estimate=pl.CostEstimate(
-            flops=flops, transcendentals=rows * n_blocks * rows * heads, bytes_accessed=bytes_moved
+            flops=flops, transcendentals=rows * n_blocks * k_rows * heads, bytes_accessed=bytes_moved
         ),
     )(*operands)
 
@@ -167,25 +168,35 @@
         passed = swapped(block, "core")
         late.append((offset + 1 - 2 * core, passed))
 
-    def masks_of(blocks):
-        return jnp.stack([tile_need(offset) for offset, _ in blocks]).astype(jnp.int32).reshape(-1)
+    def masks_of(blocks, q_tile=None):
+        need = jnp.stack([tile_need(offset) for offset, _ in blocks]).astype(jnp.int32)
+        if q_tile is not None:
+            need = need[:, q_tile:q_tile + 1, :]
+        return need.reshape(-1)
 
     carry = block_attention(queries, [b for _, b in early], masks_of(early), finish=False)
-    attended = block_attention(queries, [b for _, b in late], masks_of(late), carry=carry)
     weight_rows = lax.all_gather(out_weight, SEQ, axis=1, tiled=True)
     heads = lax.axis_size("head")
-    if heads == 2:
-        half = weight_rows.shape[1] // 2
-        me = lax.axis_index("head")
-        mine = lax.dynamic_slice_in_dim(weight_rows, me * half, half, 1)
-        theirs = lax.dynamic_slice_in_dim(weight_rows, (1 - me) * half, half, 1)
+    if heads != 2:
+        attended = block_attention(queries, [b for _, b in late], masks_of(late), carry=carry)
+        projected = jnp.dot(attended, weight_rows, preferred_element_type=jnp.float32)
+        return lax.psum_scatter(projected.astype(jnp.bfloat16), "head", scatter_dimension=1, tiled=True)
+    half = weight_rows.shape[1] // 2
+    me = lax.axis_index("head")
+    mine = lax.dynamic_slice_in_dim(weight_rows, me * half, half, 1)
+    theirs = lax.dynamic_slice_in_dim(weight_rows, (1 - me) * half, half, 1)
+    pieces = []
+    for q_tile in range(tiles_here):
+        rows = slice(q_tile * TILE, (q_tile + 1) * TILE)
+        attended = block_attention(
+            queries[rows], [b for _, b in late], masks_of(late, q_tile), carry=[c[rows] for c in carry]
+        )
         sent = jnp.dot(attended, theirs, preferred_element_type=jnp.float32).astype(jnp.bfloat16)
         got = swapped(sent, "head")
         kept_part = jnp.dot(attended, mine, preferred_element_type=jnp.float32).astype(jnp.bfloat16)
         kept_part = lax.optimization_barrier(kept_part)
-        return (kept_part.astype(jnp.float32) + got.astype(jnp.float32)).astype(jnp.bfloat16)
-    projected = jnp.dot(attended, weight_rows, preferred_element_type=jnp.float32)
-    return lax.psum_scatter(projected.astype(jnp.bfloat16), "head", scatter_dimension=1, tiled=True)
+        pieces.append((kept_part.astype(jnp.float32) + got.astype(jnp.float32)).astype(jnp.bfloat16))
+    return jnp.concatenate(pieces, axis=0)
 
 
 def solution(mesh):

time: 350 us -> 364 us (1.040)
  waiting for transfers between devices: 200 us -> 175 us
  matrix products: 18.2 us -> 35.9 us
  local copies, waits for them, and re-layouts: 3.19 us -> 14.2 us
  Pallas kernels: 37 us -> 46.1 us
    ppermute x6 -> x7, waiting for transfers between devices: 20.4 us -> 6.5 us  [swapped(): return lax.ppermute(x, axis, [(0, 1), (1, 0)])]
    dot_general x1 -> x2, matrix products: 8.31 us -> 18 us  [local(): jnp.dot(attended, mine, preferred_element_type=jnp.float32)]
    slice x0 -> x7, local copies, waits for them, and re-layouts: none -> 9.5 us  [the longest x3 6.83 us: local(): c[rows]]
    pallas_call x2 -> x3, Pallas kernels: 37 us -> 46.1 us  [block_attention(): pl.pallas_call(functools.partial(attention_kernel, n_blocks, rows // TILE...]
    dot_general x1 -> x2, matrix products: 9.85 us -> 18 us  [local(): jnp.dot(attended, theirs, preferred_element_type=jnp.float32)]
    ppermute x4, waiting for transfers between devices: 162 us -> 155 us  [shifted(): return lax.ppermute(x, axis, pairs)]
    ppermute x1, waiting for transfers between devices: 17 us -> 13 us  [third_neighbour(): return lax.ppermute(x, SEQ, pairs)]
    ppermute x6 -> x7, starting transfers between devices: 50.3 us -> 50.8 us  [swapped(): return lax.ppermute(x, axis, [(0, 1), (1, 0)])]
  transfers between devices with their start and end apart: 12 -> 13, of which waited for: 5 -> 5; matrix products, arithmetic and copies ran while one was open for 5% -> 13% of each run, Pallas kernels for 11% -> 13%
where the time goes in v6:
time: 364 us; the launch traced here: 363 us
  waiting for transfers between devices  175 us (48%)
  starting transfers between devices  70.7 us (19%)
  Pallas kernels  46.1 us (13%)
  matrix products  35.9 us (10%)
  local copies, waits for them, and re-layouts  14.2 us (4%)
  between operations  13.6 us (4%)
  other arithmetic  7.4 us (2%)
    ppermute x4, waiting for transfers between devices, shifted(): return lax.ppermute(x, axis, pairs)  155 us
    ppermute x7, starting transfers between devices, swapped(): return lax.ppermute(x, axis, [(0, 1), (1, 0)])  50.8 us
    pallas_call x3, Pallas kernels, block_attention(): pl.pallas_call(functools.partial(attention_kernel, n_blocks, rows // TILE...  46.1 us
    dot_general x2, matrix products, local(): jnp.dot(attended, theirs, preferred_element_type=jnp.float32)  18 us
    dot_general x2, matrix products, local(): jnp.dot(attended, mine, preferred_element_type=jnp.float32)  18 us
    ppermute x1, waiting for transfers between devices, third_neighbour(): return lax.ppermute(x, SEQ, pairs)  13 us
    ppermute x4, starting transfers between devices, shifted(): return lax.ppermute(x, axis, pairs)  12.9 us
  transfers between devices with their start and end apart: 13, of which 5 were waited for; matrix products, arithmetic and copies ran while one was open for 13% of the time, Pallas kernels for 13%

profile of v6, /device:TPU:9, one launch (start us, length us, event | category | flops | bytes accessed | tf_op | source)
XLA Modules:
  0.0 363.0 jit_solution(7483513497782229038)
XLA Ops:
  6.5 0.7 all-gather.2.cloned.1.call-update
  7.3 3.4 pad_maximum_fusion.refs_0_
  10.7 3.1 collective-permute-start
  13.8 3.0 collective-permute-start.1
  16.9 3.2 collective-permute-start.5
  20.1 3.5 collective-permute-start.7
  23.6 1.9 collective-permute-start.9
  25.9 0.5 and_reduce_fusion
  26.4 0.1 copy.31
  26.5 0.1 copy.32
  26.6 0.1 copy.33
  26.7 0.1 copy.34
  26.9 0.1 copy.35
  27.0 0.1 copy.36
  27.3 0.6 reshape.78.mask_ref
  27.9 0.1 copy.25
  28.0 0.1 copy.26
  28.1 0.1 copy.27
  28.3 0.1 copy.28
  28.4 0.1 copy.29
  28.7 0.7 reshape.76.mask_ref
  29.5 0.6 reshape.77.mask_ref
  30.0 2.5 fusion.27
  32.5 87.4 %collective-permute-done.refs_2_ = bf16[2,256,2560]{2,1,0:T(8,128)(2,1)S(1)} collective-permute-done((bf16[2,256,2560]{2,1,0:T(8,128)(2,1)}, bf16[2,256,2560]{2,1,0:T(8,128)(2,1)S(1)}, u32[]{:S(2)}, u32[]{:S(2)}) %collective-permute-start) | collective-permute-done | bytes 2621472 | tf_op jit(solution)/shard_map/ppermute | solution.py:24
  119.9 9.2 %collective-permute-done.1.refs_3_ = bf16[2,256,2560]{2,1,0:T(8,128)(2,1)} collective-permute-done((bf16[2,256,2560]{2,1,0:T(8,128)(2,1)}, bf16[2,256,2560]{2,1,0:T(8,128)(2,1)}, u32[]{:S(2)}, u32[]{:S(2)}) %collective-permute-start.1) | collective-permute-done | bytes 2621472 | tf_op jit(solution)/shard_map/ppermute | solution.py:24
  129.1 1.9 broadcast_select_fusion
  131.0 6.9 %collective-permute-start.2 = (bf16[2,256,2560]{2,1,0:T(8,128)(2,1)}, bf16[2,256,2560]{2,1,0:T(8,128)(2,1)}, u32[]{:S(2)}, u32[]{:S(2)}) collective-permute-start(bf16[2,256,2560]{2,1,0:T(8,128)(2,1)} %broadcast_select_fusion), channel_id=1, source_target_pairs={{1,4},{3,6},{4,1},{5,8},{6,3},{7,10},{8,5},{9,12},{10,7},{11,14},{... | collective-permute-start | bytes 7864328 | tf_op jit(solution)/shard_map/ppermute | solution.py:38
  138.0 45.2 %collective-permute-start.3 = (bf16[2,256,2560]{2,1,0:T(8,128)(2,1)S(1)}, bf16[2,256,2560]{2,1,0:T(8,128)(2,1)}, u32[]{:S(2)}, u32[]{:S(2)}) collective-permute-start(bf16[2,256,2560]{2,1,0:T(8,128)(2,1)S(1)} %collective-permute-done.refs_2_), channel_id=1, source_target_pairs={{0,1},{1,0},{2,3},{3,2},{4,5},{5,4},{6,7},{7,6},{8,9},{9,8},{10,11... | collective-permute-start | bytes 7864328 | tf_op jit(solution)/shard_map/ppermute | solution.py:28
  183.3 58.2 %collective-permute-done.7.refs_5_ = bf16[2,256,2560]{2,1,0:T(8,128)(2,1)} collective-permute-done((bf16[2,256,2560]{2,1,0:T(8,128)(2,1)}, bf16[2,256,2560]{2,1,0:T(8,128)(2,1)}, u32[]{:S(2)}, u32[]{:S(2)}) %collective-permute-start.7) | collective-permute-done | bytes 2621472 | tf_op jit(solution)/shard_map/ppermute | solution.py:24
  241.5 2.1 collective-permute-start.6
  243.6 17.7 %shard_map.64 = (f32[256,2560]{1,0:T(8,128)}, f32[256,2560]{1,0:T(8,128)}, f32[256,2560]{1,0:T(8,128)}) custom-call(s32[24]{0:T(128)} %reshape.78.mask_ref, bf16[256,2560]{1,0:T(8,128)(2,1)} %q_ref.1, bf16[2,256,2560]{2,1,0:T(8,128)(2,1)} %pad_maximum_fusion.refs_0_, bf16[2,256,2560]{2,1,0:T(8,128)(2,1)} %collective-permute-done.9.refs_1_, ...), custom_call_target="tpu_custom_call" | custom-call | flops 4026531840 | bytes 32768000 | tf_op jit(solution)/shard_map/pallas_call | solution.py:127
  261.3 3.5 fusion.24
  264.8 1.6 fusion.25
  266.4 1.0 copy-done.5
  267.5 1.7 fusion.26
  269.1 13.0 %collective-permute-done.2.refs_0_ = bf16[2,256,2560]{2,1,0:T(8,128)(2,1)} collective-permute-done((bf16[2,256,2560]{2,1,0:T(8,128)(2,1)}, bf16[2,256,2560]{2,1,0:T(8,128)(2,1)}, u32[]{:S(2)}, u32[]{:S(2)}) %collective-permute-start.2) | collective-permute-done | bytes 2621472 | tf_op jit(solution)/shard_map/ppermute | solution.py:38
  282.1 14.1 %shard_map.65 = bf16[128,2560]{1,0:T(8,128)(2,1)} custom-call(s32[10]{0:T(128)} %reshape.76.mask_ref, bf16[128,2560]{1,0:T(8,128)(2,1)} %get-tuple-element.28.q_ref, bf16[2,256,2560]{2,1,0:T(8,128)(2,1)} %collective-permute-done.2.refs_0_, bf16[2,256,2560]{2,1,0:T(8,128)(2,1)} %collective-permute-done.3.refs_1_, ...), custom_call_target="tpu_custom_call" | custom-call | flops 1677721600 | bytes 21626880 | tf_op jit(solution)/shard_map/pallas_call | solution.py:127
  296.3 14.3 %shard_map.66 = bf16[128,2560]{1,0:T(8,128)(2,1)} custom-call(s32[10]{0:T(128)} %reshape.77.mask_ref, bf16[128,2560]{1,0:T(8,128)(2,1)} %get-tuple-element.29.q_ref, bf16[2,256,2560]{2,1,0:T(8,128)(2,1)} %collective-permute-done.2.refs_0_, bf16[2,256,2560]{2,1,0:T(8,128)(2,1)} %collective-permute-done.3.refs_1_, ...), custom_call_target="tpu_custom_call" | custom-call | flops 1677721600 | bytes 21626880 | tf_op jit(solution)/shard_map/pallas_call | solution.py:127
  310.6 9.0 %fusion.14 = bf16[128,2560]{1,0:T(8,128)(2,1)S(1)} fusion(bf16[128,2560]{1,0:T(8,128)(2,1)S(1)} %copy-done.3, bf16[2560,5120]{0,1:T(8,128)(2,1)} %all-gather.2.cloned.1.call-done, s32[]{:T(128)S(6)} %select_n.22), kind=kOutput, calls=%fused_computation.10 | convolution fusion | flops 1678049280 | bytes 14417924 | tf_op jit(solution)/shard_map/dot_general | solution.py:194
  319.6 1.2 collective-permute-start.10
  320.8 9.0 %fusion.8 = bf16[128,2560]{1,0:T(8,128)(2,1)S(1)} fusion(bf16[128,2560]{1,0:T(8,128)(2,1)S(1)} %copy-done.3, bf16[2560,5120]{0,1:T(8,128)(2,1)} %all-gather.2.cloned.1.call-done, s32[]{:T(128)S(6)} %select_n.21), kind=kOutput, calls=%fused_computation.8 | convolution fusion | flops 1678049280 | bytes 14417924 | tf_op jit(solution)/shard_map/dot_general | solution.py:196
  329.8 9.0 %fusion.17 = bf16[128,2560]{1,0:T(8,128)(2,1)S(1)} fusion(bf16[128,2560]{1,0:T(8,128)(2,1)S(1)} %copy-done.4, bf16[2560,5120]{0,1:T(8,128)(2,1)} %all-gather.2.cloned.1.call-done, s32[]{:T(128)S(6)} %select_n.22), kind=kOutput, calls=%fused_computation.11 | convolution fusion | flops 1678049280 | bytes 14417924 | tf_op jit(solution)/shard_map/dot_general | solution.py:194
  338.8 0.3 collective-permute-start.11
  339.2 9.0 %fusion.11 = bf16[128,2560]{1,0:T(8,128)(2,1)S(1)} fusion(bf16[128,2560]{1,0:T(8,128)(2,1)S(1)} %copy-done.4, bf16[2560,5120]{0,1:T(8,128)(2,1)} %all-gather.2.cloned.1.call-done, s32[]{:T(128)S(6)} %select_n.21), kind=kOutput, calls=%fused_computation.9 | convolution fusion | flops 1678049280 | bytes 14417924 | tf_op jit(solution)/shard_map/dot_general | solution.py:196
  348.2 0.2 add_convert_fusion.1
  348.3 6.5 %collective-permute-done.11 = bf16[128,2560]{1,0:T(8,128)(2,1)S(1)} collective-permute-done((bf16[128,2560]{1,0:T(8,128)(2,1)S(1)}, bf16[128,2560]{1,0:T(8,128)(2,1)S(1)}, u32[]{:S(2)}, u32[]{:S(2)}) %collective-permute-start.11) | collective-permute-done | bytes 655392 | tf_op jit(solution)/shard_map/ppermute | solution.py:28
  354.8 0.2 add_convert_fusion
  355.0 1.1 pad_maximum_fusion.1
  (44 shorter events, 1.0 us)
Async XLA Ops:
  6.5 19.0 %copy-start = (s32[32,12]{0,1:T(8,128)S(1)}, s32[32,12]{0,1:T(8,128)}, u32[]{:S(2)}) copy-start(s32[32,12]{0,1:T(8,128)} %param.10) | copy-start | bytes 4612
  6.5 304.0 %all-gather.2.cloned.1.call-start = ((), (), s32[]{:S(2)}) async-start(), calls=%async_computation | async-start | bytes 27852800 | tf_op jit(solution)/shard_map/all_gather | solution.py:178
  7.3 18.4 %copy-start.7 = (s32[32]{0:T(128)S(1)}, s32[32]{0:T(128)}, u32[]{:S(2)}) copy-start(s32[32]{0:T(128)} %param.11) | copy-start | bytes 388
  10.7 109.3 %collective-permute-start = (bf16[2,256,2560]{2,1,0:T(8,128)(2,1)}, bf16[2,256,2560]{2,1,0:T(8,128)(2,1)S(1)}, u32[]{:S(2)}, u32[]{:S(2)}) collective-permute-start(bf16[2,256,2560]{2,1,0:T(8,128)(2,1)} %pad_maximum_fusion.refs_0_), channel_id=1, source_target_pairs={{0,2},{2,4},{4,6},{6,8},{8,10},{10,12},{12,14},{1,3},{3,5},{5,7},{... | collective-permute-start | bytes 7864328 | tf_op jit(solution)/shard_map/ppermute | solution.py:24
  13.8 115.3 %collective-permute-start.1 = (bf16[2,256,2560]{2,1,0:T(8,128)(2,1)}, bf16[2,256,2560]{2,1,0:T(8,128)(2,1)}, u32[]{:S(2)}, u32[]{:S(2)}) collective-permute-start(bf16[2,256,2560]{2,1,0:T(8,128)(2,1)} %pad_maximum_fusion.refs_0_), channel_id=1, source_target_pairs={{2,0},{4,2},{6,4},{8,6},{10,8},{12,10},{14,12},{3,1},{5,3},{7,5},{... | collective-permute-start | bytes 7864328 | tf_op jit(solution)/shard_map/ppermute | solution.py:24
  16.9 166.3 %collective-permute-start.5 = (bf16[2,256,2560]{2,1,0:T(8,128)(2,1)}, bf16[2,256,2560]{2,1,0:T(8,128)(2,1)}, u32[]{:S(2)}, u32[]{:S(2)}) collective-permute-start(bf16[2,256,2560]{2,1,0:T(8,128)(2,1)} %pad_maximum_fusion.refs_0_), channel_id=1, source_target_pairs={{0,4},{2,6},{4,8},{6,10},{8,12},{10,14},{1,5},{3,7},{5,9},{7,11},{... | collective-permute-start | bytes 7864328 | tf_op jit(solution)/shard_map/ppermute | solution.py:24
  20.1 221.4 %collective-permute-start.7 = (bf16[2,256,2560]{2,1,0:T(8,128)(2,1)}, bf16[2,256,2560]{2,1,0:T(8,128)(2,1)}, u32[]{:S(2)}, u32[]{:S(2)}) collective-permute-start(bf16[2,256,2560]{2,1,0:T(8,128)(2,1)} %pad_maximum_fusion.refs_0_), channel_id=1, source_target_pairs={{4,0},{6,2},{8,4},{10,6},{12,8},{14,10},{5,1},{7,3},{9,5},{11,7},{... | collective-permute-start | bytes 7864328 | tf_op jit(solution)/shard_map/ppermute | solution.py:24
  23.6 219.9 %collective-permute-start.9 = (bf16[2,256,2560]{2,1,0:T(8,128)(2,1)}, bf16[2,256,2560]{2,1,0:T(8,128)(2,1)}, u32[]{:S(2)}, u32[]{:S(2)}) collective-permute-start(bf16[2,256,2560]{2,1,0:T(8,128)(2,1)} %pad_maximum_fusion.refs_0_), channel_id=1, source_target_pairs={{0,1},{1,0},{2,3},{3,2},{4,5},{5,4},{6,7},{7,6},{8,9},{9,8},{10,11... | collective-permute-start | bytes 7864328 | tf_op jit(solution)/shard_map/ppermute | solution.py:28
  119.9 18.0 %copy-start.2 = (bf16[2,256,2560]{2,1,0:T(8,128)(2,1)}, bf16[2,256,2560]{2,1,0:T(8,128)(2,1)S(1)}, u32[]{:S(2)}) copy-start(bf16[2,256,2560]{2,1,0:T(8,128)(2,1)S(1)} %collective-permute-done.refs_2_) | copy-start | bytes 7864324
  131.0 151.1 %collective-permute-start.2 = (bf16[2,256,2560]{2,1,0:T(8,128)(2,1)}, bf16[2,256,2560]{2,1,0:T(8,128)(2,1)}, u32[]{:S(2)}, u32[]{:S(2)}) collective-permute-start(bf16[2,256,2560]{2,1,0:T(8,128)(2,1)} %broadcast_select_fusion), channel_id=1, source_target_pairs={{1,4},{3,6},{4,1},{5,8},{6,3},{7,10},{8,5},{9,12},{10,7},{11,14},{... | collective-permute-start | bytes 7864328 | tf_op jit(solution)/shard_map/ppermute | solution.py:38
  138.0 144.1 %collective-permute-start.3 = (bf16[2,256,2560]{2,1,0:T(8,128)(2,1)S(1)}, bf16[2,256,2560]{2,1,0:T(8,128)(2,1)}, u32[]{:S(2)}, u32[]{:S(2)}) collective-permute-start(bf16[2,256,2560]{2,1,0:T(8,128)(2,1)S(1)} %collective-permute-done.refs_2_), channel_id=1, source_target_pairs={{0,1},{1,0},{2,3},{3,2},{4,5},{5,4},{6,7},{7,6},{8,9},{9,8},{10,11... | collective-permute-start | bytes 7864328 | tf_op jit(solution)/shard_map/ppermute | solution.py:28
  183.2 98.9 %collective-permute-start.4 = (bf16[2,256,2560]{2,1,0:T(8,128)(2,1)}, bf16[2,256,2560]{2,1,0:T(8,128)(2,1)}, u32[]{:S(2)}, u32[]{:S(2)}) collective-permute-start(bf16[2,256,2560]{2,1,0:T(8,128)(2,1)} %collective-permute-done.1.refs_3_), channel_id=1, source_target_pairs={{0,1},{1,0},{2,3},{3,2},{4,5},{5,4},{6,7},{7,6},{8,9},{9,8},{10,11... | collective-permute-start | bytes 7864328 | tf_op jit(solution)/shard_map/ppermute | solution.py:28
  241.5 40.6 %collective-permute-start.6 = (bf16[2,256,2560]{2,1,0:T(8,128)(2,1)}, bf16[2,256,2560]{2,1,0:T(8,128)(2,1)}, u32[]{:S(2)}, u32[]{:S(2)}) collective-permute-start(bf16[2,256,2560]{2,1,0:T(8,128)(2,1)} %collective-permute-done.5.refs_4_), channel_id=1, source_target_pairs={{0,1},{1,0},{2,3},{3,2},{4,5},{5,4},{6,7},{7,6},{8,9},{9,8},{10,11... | collective-permute-start | bytes 7864328 | tf_op jit(solution)/shard_map/ppermute | solution.py:28
  243.6 38.6 %collective-permute-start.8 = (bf16[2,256,2560]{2,1,0:T(8,128)(2,1)}, bf16[2,256,2560]{2,1,0:T(8,128)(2,1)}, u32[]{:S(2)}, u32[]{:S(2)}) collective-permute-start(bf16[2,256,2560]{2,1,0:T(8,128)(2,1)} %collective-permute-done.7.refs_5_), channel_id=1, source_target_pairs={{0,1},{1,0},{2,3},{3,2},{4,5},{5,4},{6,7},{7,6},{8,9},{9,8},{10,11... | collective-permute-start | bytes 7864328 | tf_op jit(solution)/shard_map/ppermute | solution.py:28
  261.2 3.5 copy-start.6
  264.8 2.7 copy-start.5
  296.3 14.3 %copy-start.3 = (bf16[128,2560]{1,0:T(8,128)(2,1)S(1)}, bf16[128,2560]{1,0:T(8,128)(2,1)}, u32[]{:S(2)}) copy-start(bf16[128,2560]{1,0:T(8,128)(2,1)} %shard_map.65) | copy-start | bytes 1966084
  319.6 10.3 %copy-start.4 = (bf16[128,2560]{1,0:T(8,128)(2,1)S(1)}, bf16[128,2560]{1,0:T(8,128)(2,1)}, u32[]{:S(2)}) copy-start(bf16[128,2560]{1,0:T(8,128)(2,1)} %shard_map.66) | copy-start | bytes 1966084
  319.6 28.6 %collective-permute-start.10 = (bf16[128,2560]{1,0:T(8,128)(2,1)S(1)}, bf16[128,2560]{1,0:T(8,128)(2,1)S(1)}, u32[]{:S(2)}, u32[]{:S(2)}) collective-permute-start(bf16[128,2560]{1,0:T(8,128)(2,1)S(1)} %fusion.14), channel_id=1, source_target_pairs={{0,16},{16,0},{1,17},{17,1},{2,18},{18,2},{3,19},{19,3},{4,20},{20... | collective-permute-start | bytes 1966088 | tf_op jit(solution)/shard_map/ppermute | solution.py:28
  338.8 16.0 %collective-permute-start.11 = (bf16[128,2560]{1,0:T(8,128)(2,1)S(1)}, bf16[128,2560]{1,0:T(8,128)(2,1)S(1)}, u32[]{:S(2)}, u32[]{:S(2)}) collective-permute-start(bf16[128,2560]{1,0:T(8,128)(2,1)S(1)} %fusion.17), channel_id=1, source_target_pairs={{0,16},{16,0},{1,17},{17,1},{2,18},{18,2},{3,19},{19,3},{4,20},{20... | collective-permute-start | bytes 1966088 | tf_op jit(solution)/shard_map/ppermute | solution.py:28
  348.2 8.0 %copy-start.1 = (s32[32,12]{0,1:T(8,128)S(1)}, s32[32,12]{0,1:T(8,128)}, u32[]{:S(2)}) copy-start(s32[32,12]{0,1:T(8,128)} %param.10) | copy-start | bytes 4612
Sparse Core Ops, SparseCore 0:
  9.0 256.0 all-gather.1

commit v7 on v5

--- a/solution.py
+++ b/solution.py
@@ -179,10 +179,15 @@
         me = lax.axis_index("head")
         mine = lax.dynamic_slice_in_dim(weight_rows, me * half, half, 1)
         theirs = lax.dynamic_slice_in_dim(weight_rows, (1 - me) * half, half, 1)
-        sent = jnp.dot(attended, theirs, preferred_element_type=jnp.float32).astype(jnp.bfloat16)
-        got = swapped(sent, "head")
+        chunk = half // 2
+        got = []
+        for part in range(2):
+            cols = slice(part * chunk, (part + 1) * chunk)
+            sent = jnp.dot(attended, theirs[:, cols], preferred_element_type=jnp.float32).astype(jnp.bfloat16)
+            got.append(swapped(sent, "head"))
         kept_part = jnp.dot(attended, mine, preferred_element_type=jnp.float32).astype(jnp.bfloat16)
         kept_part = lax.optimization_barrier(kept_part)
+        got = jnp.concatenate(got, axis=1)
         return (kept_part.astype(jnp.float32) + got.astype(jnp.float32)).astype(jnp.bfloat16)
     projected = jnp.dot(attended, weight_rows, preferred_element_type=jnp.float32)
     return lax.psum_scatter(projected.astype(jnp.bfloat16), "head", scatter_dimension=1, tiled=True)

time: 350 us -> 345 us (0.986)
  waiting for transfers between devices: 200 us -> 195 us
    ppermute x6 -> x7, waiting for transfers between devices: 20.4 us -> 15.1 us  [swapped(): return lax.ppermute(x, axis, [(0, 1), (1, 0)])]
    ppermute x6 -> x7, starting transfers between devices: 50.3 us -> 50.7 us  [swapped(): return lax.ppermute(x, axis, [(0, 1), (1, 0)])]
    dot_general x1 -> x2, matrix products: 9.85 us -> 10 us  [local(): jnp.dot(attended, theirs[:, cols], preferred_element_type=jnp.float32)]
  transfers between devices with their start and end apart: 12 -> 13, of which waited for: 5 -> 6; matrix products, arithmetic and copies ran while one was open for 5% -> 6% of each run, Pallas kernels for 11% -> 11%
where the time goes in v7:
time: 345 us
  waiting for transfers between devices  195 us (57%)
  starting transfers between devices  70.6 us (20%)
  Pallas kernels  37 us (11%)
  matrix products  18.3 us (5%)
  between operations  13.6 us (4%)
  other arithmetic  7.4 us (2%)
    ppermute x4, waiting for transfers between devices, shifted(): return lax.ppermute(x, axis, pairs)  162 us
    ppermute x7, starting transfers between devices, swapped(): return lax.ppermute(x, axis, [(0, 1), (1, 0)])  50.7 us
    pallas_call x2, Pallas kernels, block_attention(): pl.pallas_call(functools.partial(attention_kernel, n_blocks, tiles, group...  37 us
    ppermute x1, waiting for transfers between devices, third_neighbour(): return lax.ppermute(x, SEQ, pairs)  17 us
    ppermute x7, waiting for transfers between devices, swapped(): return lax.ppermute(x, axis, [(0, 1), (1, 0)])  15.1 us
    ppermute x4, starting transfers between devices, shifted(): return lax.ppermute(x, axis, pairs)  13 us
    dot_general x2, matrix products, local(): jnp.dot(attended, theirs[:, cols], preferred_element_type=jnp.float32)  10 us
    dot_general x1, matrix products, local(): jnp.dot(attended, mine, preferred_element_type=jnp.float32)  8.31 us
  transfers between devices with their start and end apart: 13, of which 6 were waited for; matrix products, arithmetic and copies ran while one was open for 6% of the time, Pallas kernels for 11%

profile of v7, /device:TPU:9, one launch (start us, length us, event | category | flops | bytes accessed | tf_op | source)
XLA Modules:
  0.0 344.8 jit_solution(702537047026987059)
XLA Ops:
  6.5 0.7 all-gather.2.cloned.1.call-update
  7.3 3.4 pad_maximum_fusion.refs_0_
  10.7 3.1 collective-permute-start
  13.8 3.0 collective-permute-start.1
  16.9 3.2 collective-permute-start.5
  20.1 3.6 %collective-permute-start.7 = (bf16[2,256,2560]{2,1,0:T(8,128)(2,1)}, bf16[2,256,2560]{2,1,0:T(8,128)(2,1)}, u32[]{:S(2)}, u32[]{:S(2)}) collective-permute-start(bf16[2,256,2560]{2,1,0:T(8,128)(2,1)} %pad_maximum_fusion.refs_0_), channel_id=1, source_target_pairs={{4,0},{6,2},{8,4},{10,6},{12,8},{14,10},{5,1},{7,3},{9,5},{11,7},{... | collective-permute-start | bytes 7864328 | tf_op jit(solution)/shard_map/ppermute | solution.py:24
  23.7 1.9 collective-permute-start.9
  25.6 94.4 %collective-permute-done.refs_2_ = bf16[2,256,2560]{2,1,0:T(8,128)(2,1)S(1)} collective-permute-done((bf16[2,256,2560]{2,1,0:T(8,128)(2,1)}, bf16[2,256,2560]{2,1,0:T(8,128)(2,1)S(1)}, u32[]{:S(2)}, u32[]{:S(2)}) %collective-permute-start) | collective-permute-done | bytes 2621472 | tf_op jit(solution)/shard_map/ppermute | solution.py:24
  119.9 9.2 %collective-permute-done.1.refs_3_ = bf16[2,256,2560]{2,1,0:T(8,128)(2,1)} collective-permute-done((bf16[2,256,2560]{2,1,0:T(8,128)(2,1)}, bf16[2,256,2560]{2,1,0:T(8,128)(2,1)}, u32[]{:S(2)}, u32[]{:S(2)}) %collective-permute-start.1) | collective-permute-done | bytes 2621472 | tf_op jit(solution)/shard_map/ppermute | solution.py:24
  129.2 1.9 broadcast_select_fusion
  131.1 6.9 %collective-permute-start.2 = (bf16[2,256,2560]{2,1,0:T(8,128)(2,1)}, bf16[2,256,2560]{2,1,0:T(8,128)(2,1)}, u32[]{:S(2)}, u32[]{:S(2)}) collective-permute-start(bf16[2,256,2560]{2,1,0:T(8,128)(2,1)} %broadcast_select_fusion), channel_id=1, source_target_pairs={{1,4},{3,6},{4,1},{5,8},{6,3},{7,10},{8,5},{9,12},{10,7},{11,14},{... | collective-permute-start | bytes 7864328 | tf_op jit(solution)/shard_map/ppermute | solution.py:38
  138.0 45.1 %collective-permute-start.3 = (bf16[2,256,2560]{2,1,0:T(8,128)(2,1)S(1)}, bf16[2,256,2560]{2,1,0:T(8,128)(2,1)}, u32[]{:S(2)}, u32[]{:S(2)}) collective-permute-start(bf16[2,256,2560]{2,1,0:T(8,128)(2,1)S(1)} %collective-permute-done.refs_2_), channel_id=1, source_target_pairs={{0,1},{1,0},{2,3},{3,2},{4,5},{5,4},{6,7},{7,6},{8,9},{9,8},{10,11... | collective-permute-start | bytes 7864328 | tf_op jit(solution)/shard_map/ppermute | solution.py:28
  183.2 0.1 collective-permute-start.4
  183.3 58.3 %collective-permute-done.7.refs_5_ = bf16[2,256,2560]{2,1,0:T(8,128)(2,1)} collective-permute-done((bf16[2,256,2560]{2,1,0:T(8,128)(2,1)}, bf16[2,256,2560]{2,1,0:T(8,128)(2,1)}, u32[]{:S(2)}, u32[]{:S(2)}) %collective-permute-start.7) | collective-permute-done | bytes 2621472 | tf_op jit(solution)/shard_map/ppermute | solution.py:24
  241.5 2.0 collective-permute-start.6
  243.6 0.1 constant_dynamic-slice_fusion
  243.6 0.1 copy.23
  243.7 0.1 dynamic_slice.13
  243.9 0.1 iota_compare_fusion
  243.9 0.5 and_reduce_fusion
  244.5 0.1 copy.30
  244.6 0.1 copy.31
  244.7 0.1 copy.32
  244.8 0.1 copy.33
  244.9 0.1 copy.34
  245.0 0.1 copy.35
  245.2 0.1 stack.63
  245.3 0.1 copy.36
  245.4 0.6 reshape.75.mask_ref
  246.0 0.1 copy.24
  246.1 0.1 copy.25
  246.2 0.1 copy.26
  246.3 0.1 copy.27
  246.4 0.1 copy.28
  246.6 0.1 stack.53
  246.7 0.1 copy.29
  246.8 0.7 reshape.74.mask_ref
  247.4 17.7 %shard_map.64 = (f32[256,2560]{1,0:T(8,128)}, f32[256,2560]{1,0:T(8,128)}, f32[256,2560]{1,0:T(8,128)}) custom-call(s32[24]{0:T(128)} %reshape.75.mask_ref, bf16[256,2560]{1,0:T(8,128)(2,1)} %q_ref.3, bf16[2,256,2560]{2,1,0:T(8,128)(2,1)} %pad_maximum_fusion.refs_0_, bf16[2,256,2560]{2,1,0:T(8,128)(2,1)} %collective-permute-done.9.refs_1_, ...), custom_call_target="tpu_custom_call" | custom-call | flops 4026531840 | bytes 34078720 | tf_op jit(solution)/shard_map/pallas_call | solution.py:126
  265.1 17.0 %collective-permute-done.2.refs_0_ = bf16[2,256,2560]{2,1,0:T(8,128)(2,1)} collective-permute-done((bf16[2,256,2560]{2,1,0:T(8,128)(2,1)}, bf16[2,256,2560]{2,1,0:T(8,128)(2,1)}, u32[]{:S(2)}, u32[]{:S(2)}) %collective-permute-start.2) | collective-permute-done | bytes 2621472 | tf_op jit(solution)/shard_map/ppermute | solution.py:38
  282.1 19.3 %shard_map.65 = bf16[256,2560]{1,0:T(8,128)(2,1)} custom-call(s32[20]{0:T(128)} %reshape.74.mask_ref, bf16[256,2560]{1,0:T(8,128)(2,1)} %q_ref.3, bf16[2,256,2560]{2,1,0:T(8,128)(2,1)} %collective-permute-done.2.refs_0_, bf16[2,256,2560]{2,1,0:T(8,128)(2,1)} %collective-permute-done.3.refs_1_, bf16[2,256,2560]{2,1,0:T(8,128)(2,1)} %collective-permute-done.4.refs_2_, ...), custom_call_target="tpu_custom_call" | custom-call | flops 3355443200 | bytes 31457280 | tf_op jit(solution)/shard_map/pallas_call | solution.py:126
  301.5 5.3 %fusion.12 = bf16[256,1280]{1,0:T(8,128)(2,1)S(1)} fusion(bf16[256,2560]{1,0:T(8,128)(2,1)} %shard_map.65, bf16[2560,5120]{0,1:T(8,128)(2,1)} %all-gather.2.cloned.1.call-done, s32[]{:T(128)S(6)} %add.193), kind=kOutput, calls=%fused_computation.11 | convolution fusion | flops 1678049280 | bytes 8519684 | tf_op jit(solution)/shard_map/dot_general | solution.py:186
  306.8 1.2 collective-permute-start.11
  308.0 4.7 %fusion.9 = bf16[256,1280]{1,0:T(8,128)(2,1)S(1)} fusion(bf16[256,2560]{1,0:T(8,128)(2,1)S(1)} %copy-done.3, bf16[2560,5120]{0,1:T(8,128)(2,1)} %all-gather.2.cloned.1.call-done, s32[]{:T(128)S(6)} %select_n.22), kind=kOutput, calls=%fused_computation.10 | convolution fusion | flops 1678049280 | bytes 8519684 | tf_op jit(solution)/shard_map/dot_general | solution.py:186
  312.7 0.4 collective-permute-start.10
  313.1 8.3 %fusion.6 = bf16[256,2560]{1,0:T(8,128)(2,1)S(1)} fusion(bf16[256,2560]{1,0:T(8,128)(2,1)S(1)} %copy-done.3, bf16[2560,5120]{0,1:T(8,128)(2,1)} %all-gather.2.cloned.1.call-done, s32[]{:T(128)S(6)} %select_n.21), kind=kOutput, calls=%fused_computation.6 | convolution fusion | flops 3356098560 | bytes 15728644 | tf_op jit(solution)/shard_map/dot_general | solution.py:188
  321.4 2.1 collective-permute-done.11
  323.6 13.0 %collective-permute-done.10 = bf16[256,1280]{1,0:T(8,128)(2,1)S(1)} collective-permute-done((bf16[256,1280]{1,0:T(8,128)(2,1)S(1)}, bf16[256,1280]{1,0:T(8,128)(2,1)S(1)}, u32[]{:S(2)}, u32[]{:S(2)}) %collective-permute-start.10) | collective-permute-done | bytes 655392 | tf_op jit(solution)/shard_map/ppermute | solution.py:28
  336.6 1.4 add_convert_fusion
  (27 shorter events, 0.1 us)
Async XLA Ops:
  6.5 237.0 %copy-start = (s32[32,12]{0,1:T(8,128)S(1)}, s32[32,12]{0,1:T(8,128)}, u32[]{:S(2)}) copy-start(s32[32,12]{0,1:T(8,128)} %param.10) | copy-start | bytes 4612
  6.5 294.9 %all-gather.2.cloned.1.call-start = ((), (), s32[]{:S(2)}) async-start(), calls=%async_computation | async-start | bytes 27852800 | tf_op jit(solution)/shard_map/all_gather | solution.py:175
  10.7 109.2 %collective-permute-start = (bf16[2,256,2560]{2,1,0:T(8,128)(2,1)}, bf16[2,256,2560]{2,1,0:T(8,128)(2,1)S(1)}, u32[]{:S(2)}, u32[]{:S(2)}) collective-permute-start(bf16[2,256,2560]{2,1,0:T(8,128)(2,1)} %pad_maximum_fusion.refs_0_), channel_id=1, source_target_pairs={{0,2},{2,4},{4,6},{6,8},{8,10},{10,12},{12,14},{1,3},{3,5},{5,7},{... | collective-permute-start | bytes 7864328 | tf_op jit(solution)/shard_map/ppermute | solution.py:24
  13.8 115.3 %collective-permute-start.1 = (bf16[2,256,2560]{2,1,0:T(8,128)(2,1)}, bf16[2,256,2560]{2,1,0:T(8,128)(2,1)}, u32[]{:S(2)}, u32[]{:S(2)}) collective-permute-start(bf16[2,256,2560]{2,1,0:T(8,128)(2,1)} %pad_maximum_fusion.refs_0_), channel_id=1, source_target_pairs={{2,0},{4,2},{6,4},{8,6},{10,8},{12,10},{14,12},{3,1},{5,3},{7,5},{... | collective-permute-start | bytes 7864328 | tf_op jit(solution)/shard_map/ppermute | solution.py:24
  16.9 166.3 %collective-permute-start.5 = (bf16[2,256,2560]{2,1,0:T(8,128)(2,1)}, bf16[2,256,2560]{2,1,0:T(8,128)(2,1)}, u32[]{:S(2)}, u32[]{:S(2)}) collective-permute-start(bf16[2,256,2560]{2,1,0:T(8,128)(2,1)} %pad_maximum_fusion.refs_0_), channel_id=1, source_target_pairs={{0,4},{2,6},{4,8},{6,10},{8,12},{10,14},{1,5},{3,7},{5,9},{7,11},{... | collective-permute-start | bytes 7864328 | tf_op jit(solution)/shard_map/ppermute | solution.py:24
  20.1 221.4 %collective-permute-start.7 = (bf16[2,256,2560]{2,1,0:T(8,128)(2,1)}, bf16[2,256,2560]{2,1,0:T(8,128)(2,1)}, u32[]{:S(2)}, u32[]{:S(2)}) collective-permute-start(bf16[2,256,2560]{2,1,0:T(8,128)(2,1)} %pad_maximum_fusion.refs_0_), channel_id=1, source_target_pairs={{4,0},{6,2},{8,4},{10,6},{12,8},{14,10},{5,1},{7,3},{9,5},{11,7},{... | collective-permute-start | bytes 7864328 | tf_op jit(solution)/shard_map/ppermute | solution.py:24
  23.7 219.9 %collective-permute-start.9 = (bf16[2,256,2560]{2,1,0:T(8,128)(2,1)}, bf16[2,256,2560]{2,1,0:T(8,128)(2,1)}, u32[]{:S(2)}, u32[]{:S(2)}) collective-permute-start(bf16[2,256,2560]{2,1,0:T(8,128)(2,1)} %pad_maximum_fusion.refs_0_), channel_id=1, source_target_pairs={{0,1},{1,0},{2,3},{3,2},{4,5},{5,4},{6,7},{7,6},{8,9},{9,8},{10,11... | collective-permute-start | bytes 7864328 | tf_op jit(solution)/shard_map/ppermute | solution.py:28
  25.6 218.2 %copy-start.4 = (s32[32]{0:T(128)S(1)}, s32[32]{0:T(128)}, u32[]{:S(2)}) copy-start(s32[32]{0:T(128)} %param.11) | copy-start | bytes 388
  119.9 18.1 %copy-start.2 = (bf16[2,256,2560]{2,1,0:T(8,128)(2,1)}, bf16[2,256,2560]{2,1,0:T(8,128)(2,1)S(1)}, u32[]{:S(2)}) copy-start(bf16[2,256,2560]{2,1,0:T(8,128)(2,1)S(1)} %collective-permute-done.refs_2_) | copy-start | bytes 7864324
  131.1 151.0 %collective-permute-start.2 = (bf16[2,256,2560]{2,1,0:T(8,128)(2,1)}, bf16[2,256,2560]{2,1,0:T(8,128)(2,1)}, u32[]{:S(2)}, u32[]{:S(2)}) collective-permute-start(bf16[2,256,2560]{2,1,0:T(8,128)(2,1)} %broadcast_select_fusion), channel_id=1, source_target_pairs={{1,4},{3,6},{4,1},{5,8},{6,3},{7,10},{8,5},{9,12},{10,7},{11,14},{... | collective-permute-start | bytes 7864328 | tf_op jit(solution)/shard_map/ppermute | solution.py:38
  138.0 144.1 %collective-permute-start.3 = (bf16[2,256,2560]{2,1,0:T(8,128)(2,1)S(1)}, bf16[2,256,2560]{2,1,0:T(8,128)(2,1)}, u32[]{:S(2)}, u32[]{:S(2)}) collective-permute-start(bf16[2,256,2560]{2,1,0:T(8,128)(2,1)S(1)} %collective-permute-done.refs_2_), channel_id=1, source_target_pairs={{0,1},{1,0},{2,3},{3,2},{4,5},{5,4},{6,7},{7,6},{8,9},{9,8},{10,11... | collective-permute-start | bytes 7864328 | tf_op jit(solution)/shard_map/ppermute | solution.py:28
  183.2 98.9 %collective-permute-start.4 = (bf16[2,256,2560]{2,1,0:T(8,128)(2,1)}, bf16[2,256,2560]{2,1,0:T(8,128)(2,1)}, u32[]{:S(2)}, u32[]{:S(2)}) collective-permute-start(bf16[2,256,2560]{2,1,0:T(8,128)(2,1)} %collective-permute-done.1.refs_3_), channel_id=1, source_target_pairs={{0,1},{1,0},{2,3},{3,2},{4,5},{5,4},{6,7},{7,6},{8,9},{9,8},{10,11... | collective-permute-start | bytes 7864328 | tf_op jit(solution)/shard_map/ppermute | solution.py:28
  241.5 40.6 %collective-permute-start.6 = (bf16[2,256,2560]{2,1,0:T(8,128)(2,1)}, bf16[2,256,2560]{2,1,0:T(8,128)(2,1)}, u32[]{:S(2)}, u32[]{:S(2)}) collective-permute-start(bf16[2,256,2560]{2,1,0:T(8,128)(2,1)} %collective-permute-done.5.refs_4_), channel_id=1, source_target_pairs={{0,1},{1,0},{2,3},{3,2},{4,5},{5,4},{6,7},{7,6},{8,9},{9,8},{10,11... | collective-permute-start | bytes 7864328 | tf_op jit(solution)/shard_map/ppermute | solution.py:28
  243.6 38.6 %collective-permute-start.8 = (bf16[2,256,2560]{2,1,0:T(8,128)(2,1)}, bf16[2,256,2560]{2,1,0:T(8,128)(2,1)}, u32[]{:S(2)}, u32[]{:S(2)}) collective-permute-start(bf16[2,256,2560]{2,1,0:T(8,128)(2,1)} %collective-permute-done.7.refs_5_), channel_id=1, source_target_pairs={{0,1},{1,0},{2,3},{3,2},{4,5},{5,4},{6,7},{7,6},{8,9},{9,8},{10,11... | collective-permute-start | bytes 7864328 | tf_op jit(solution)/shard_map/ppermute | solution.py:28
  301.5 6.5 %copy-start.3 = (bf16[256,2560]{1,0:T(8,128)(2,1)S(1)}, bf16[256,2560]{1,0:T(8,128)(2,1)}, u32[]{:S(2)}) copy-start(bf16[256,2560]{1,0:T(8,128)(2,1)} %shard_map.65) | copy-start | bytes 3932164
  306.8 16.8 %collective-permute-start.11 = (bf16[256,1280]{1,0:T(8,128)(2,1)S(1)}, bf16[256,1280]{1,0:T(8,128)(2,1)S(1)}, u32[]{:S(2)}, u32[]{:S(2)}) collective-permute-start(bf16[256,1280]{1,0:T(8,128)(2,1)S(1)} %fusion.12), channel_id=1, source_target_pairs={{0,16},{16,0},{1,17},{17,1},{2,18},{18,2},{3,19},{19,3},{4,20},{20... | collective-permute-start | bytes 1966088 | tf_op jit(solution)/shard_map/ppermute | solution.py:28
  312.7 23.8 %collective-permute-start.10 = (bf16[256,1280]{1,0:T(8,128)(2,1)S(1)}, bf16[256,1280]{1,0:T(8,128)(2,1)S(1)}, u32[]{:S(2)}, u32[]{:S(2)}) collective-permute-start(bf16[256,1280]{1,0:T(8,128)(2,1)S(1)} %fusion.9), channel_id=1, source_target_pairs={{0,16},{16,0},{1,17},{17,1},{2,18},{18,2},{3,19},{19,3},{4,20},{20... | collective-permute-start | bytes 1966088 | tf_op jit(solution)/shard_map/ppermute | solution.py:28
  313.1 24.9 %copy-start.1 = (s32[32,12]{0,1:T(8,128)S(1)}, s32[32,12]{0,1:T(8,128)}, u32[]{:S(2)}) copy-start(s32[32,12]{0,1:T(8,128)} %param.10) | copy-start | bytes 4612
Sparse Core Ops, SparseCore 0:
  9.0 256.0 all-gather.1

commit v8 on v7

--- a/solution.py
+++ b/solution.py
@@ -179,9 +179,10 @@
         me = lax.axis_index("head")
         mine = lax.dynamic_slice_in_dim(weight_rows, me * half, half, 1)
         theirs = lax.dynamic_slice_in_dim(weight_rows, (1 - me) * half, half, 1)
-        chunk = half // 2
+        parts = 4
+        chunk = half // parts
         got = []
-        for part in range(2):
+        for part in range(parts):
             cols = slice(part * chunk, (part + 1) * chunk)
             sent = jnp.dot(attended, theirs[:, cols], preferred_element_type=jnp.float32).astype(jnp.bfloat16)
             got.append(swapped(sent, "head"))

time: 345 us -> 344 us (level)
  waiting for transfers between devices: 195 us -> 188 us
    ppermute x7 -> x9, waiting for transfers between devices: 15.1 us -> 8.86 us  [swapped(): return lax.ppermute(x, axis, [(0, 1), (1, 0)])]
    dot_general x2 -> x4, matrix products: 10 us -> 13 us  [local(): jnp.dot(attended, theirs[:, cols], preferred_element_type=jnp.float32)]
    ppermute x7 -> x9, starting transfers between devices: 50.7 us -> 52.3 us  [swapped(): return lax.ppermute(x, axis, [(0, 1), (1, 0)])]
  transfers between devices with their start and end apart: 13 -> 15, of which waited for: 6 -> 6; matrix products, arithmetic and copies ran while one was open for 6% -> 8% of each run, Pallas kernels for 11% -> 11%
where the time goes in v8:
time: 344 us; the launch traced here: 343 us
  waiting for transfers between devices  188 us (55%)
  starting transfers between devices  72.2 us (21%)
  Pallas kernels  37 us (11%)
  matrix products  21.3 us (6%)
  between operations  13.6 us (4%)
  other arithmetic  7.38 us (2%)
    ppermute x4, waiting for transfers between devices, shifted(): return lax.ppermute(x, axis, pairs)  162 us
    ppermute x9, starting transfers between devices, swapped(): return lax.ppermute(x, axis, [(0, 1), (1, 0)])  52.3 us
    pallas_call x2, Pallas kernels, block_attention(): pl.pallas_call(functools.partial(attention_kernel, n_blocks, tiles, group...  37 us
    ppermute x1, waiting for transfers between devices, third_neighbour(): return lax.ppermute(x, SEQ, pairs)  17 us
    dot_general x4, matrix products, local(): jnp.dot(attended, theirs[:, cols], preferred_element_type=jnp.float32)  13 us
    ppermute x4, starting transfers between devices, shifted(): return lax.ppermute(x, axis, pairs)  13 us
    ppermute x9, waiting for transfers between devices, swapped(): return lax.ppermute(x, axis, [(0, 1), (1, 0)])  8.86 us
    dot_general x1, matrix products, local(): jnp.dot(attended, mine, preferred_element_type=jnp.float32)  8.31 us
  transfers between devices with their start and end apart: 15, of which 6 were waited for; matrix products, arithmetic and copies ran while one was open for 8% of the time, Pallas kernels for 11%

profile of v8, /device:TPU:9, one launch (start us, length us, event | category | flops | bytes accessed | tf_op | source)
XLA Modules:
  0.0 343.2 jit_solution(4743832146868287153)
XLA Ops:
  6.5 0.7 all-gather.2.cloned.1.call-update
  7.3 3.4 pad_maximum_fusion.refs_0_
  10.7 3.1 collective-permute-start
  13.8 3.0 collective-permute-start.1
  16.9 3.2 collective-permute-start.5
  20.1 3.6 %collective-permute-start.7 = (bf16[2,256,2560]{2,1,0:T(8,128)(2,1)}, bf16[2,256,2560]{2,1,0:T(8,128)(2,1)}, u32[]{:S(2)}, u32[]{:S(2)}) collective-permute-start(bf16[2,256,2560]{2,1,0:T(8,128)(2,1)} %pad_maximum_fusion.refs_0_), channel_id=1, source_target_pairs={{4,0},{6,2},{8,4},{10,6},{12,8},{14,10},{5,1},{7,3},{9,5},{11,7},{... | collective-permute-start | bytes 7864328 | tf_op jit(solution)/shard_map/ppermute | solution.py:24
  23.7 1.9 collective-permute-start.9
  25.6 94.4 %collective-permute-done.refs_2_ = bf16[2,256,2560]{2,1,0:T(8,128)(2,1)S(1)} collective-permute-done((bf16[2,256,2560]{2,1,0:T(8,128)(2,1)}, bf16[2,256,2560]{2,1,0:T(8,128)(2,1)S(1)}, u32[]{:S(2)}, u32[]{:S(2)}) %collective-permute-start) | collective-permute-done | bytes 2621472 | tf_op jit(solution)/shard_map/ppermute | solution.py:24
  119.9 9.2 %collective-permute-done.1.refs_3_ = bf16[2,256,2560]{2,1,0:T(8,128)(2,1)} collective-permute-done((bf16[2,256,2560]{2,1,0:T(8,128)(2,1)}, bf16[2,256,2560]{2,1,0:T(8,128)(2,1)}, u32[]{:S(2)}, u32[]{:S(2)}) %collective-permute-start.1) | collective-permute-done | bytes 2621472 | tf_op jit(solution)/shard_map/ppermute | solution.py:24
  129.2 1.9 broadcast_select_fusion
  131.1 6.9 %collective-permute-start.2 = (bf16[2,256,2560]{2,1,0:T(8,128)(2,1)}, bf16[2,256,2560]{2,1,0:T(8,128)(2,1)}, u32[]{:S(2)}, u32[]{:S(2)}) collective-permute-start(bf16[2,256,2560]{2,1,0:T(8,128)(2,1)} %broadcast_select_fusion), channel_id=1, source_target_pairs={{1,4},{3,6},{4,1},{5,8},{6,3},{7,10},{8,5},{9,12},{10,7},{11,14},{... | collective-permute-start | bytes 7864328 | tf_op jit(solution)/shard_map/ppermute | solution.py:38
  138.0 45.1 %collective-permute-start.3 = (bf16[2,256,2560]{2,1,0:T(8,128)(2,1)S(1)}, bf16[2,256,2560]{2,1,0:T(8,128)(2,1)}, u32[]{:S(2)}, u32[]{:S(2)}) collective-permute-start(bf16[2,256,2560]{2,1,0:T(8,128)(2,1)S(1)} %collective-permute-done.refs_2_), channel_id=1, source_target_pairs={{0,1},{1,0},{2,3},{3,2},{4,5},{5,4},{6,7},{7,6},{8,9},{9,8},{10,11... | collective-permute-start | bytes 7864328 | tf_op jit(solution)/shard_map/ppermute | solution.py:28
  183.3 58.3 %collective-permute-done.7.refs_5_ = bf16[2,256,2560]{2,1,0:T(8,128)(2,1)} collective-permute-done((bf16[2,256,2560]{2,1,0:T(8,128)(2,1)}, bf16[2,256,2560]{2,1,0:T(8,128)(2,1)}, u32[]{:S(2)}, u32[]{:S(2)}) %collective-permute-start.7) | collective-permute-done | bytes 2621472 | tf_op jit(solution)/shard_map/ppermute | solution.py:24
  241.5 2.0 collective-permute-start.6
  243.6 0.1 copy.23
  243.9 0.5 and_reduce_fusion
  244.5 0.1 copy.30
  244.6 0.1 copy.31
  244.7 0.1 copy.32
  244.8 0.1 copy.33
  244.9 0.1 copy.34
  245.0 0.1 copy.35
  245.2 0.1 stack.63
  245.3 0.1 copy.36
  245.4 0.6 reshape.75.mask_ref
  246.0 0.1 copy.24
  246.1 0.1 copy.25
  246.2 0.1 copy.26
  246.3 0.1 copy.27
  246.4 0.1 copy.28
  246.6 0.1 stack.53
  246.7 0.1 copy.29
  246.8 0.7 reshape.74.mask_ref
  247.4 17.7 %shard_map.64 = (f32[256,2560]{1,0:T(8,128)}, f32[256,2560]{1,0:T(8,128)}, f32[256,2560]{1,0:T(8,128)}) custom-call(s32[24]{0:T(128)} %reshape.75.mask_ref, bf16[256,2560]{1,0:T(8,128)(2,1)} %q_ref.3, bf16[2,256,2560]{2,1,0:T(8,128)(2,1)} %pad_maximum_fusion.refs_0_, bf16[2,256,2560]{2,1,0:T(8,128)(2,1)} %collective-permute-done.9.refs_1_, ...), custom_call_target="tpu_custom_call" | custom-call | flops 4026531840 | bytes 34078720 | tf_op jit(solution)/shard_map/pallas_call | solution.py:126
  265.1 17.0 %collective-permute-done.2.refs_0_ = bf16[2,256,2560]{2,1,0:T(8,128)(2,1)} collective-permute-done((bf16[2,256,2560]{2,1,0:T(8,128)(2,1)}, bf16[2,256,2560]{2,1,0:T(8,128)(2,1)}, u32[]{:S(2)}, u32[]{:S(2)}) %collective-permute-start.2) | collective-permute-done | bytes 2621472 | tf_op jit(solution)/shard_map/ppermute | solution.py:38
  282.1 19.3 %shard_map.65 = bf16[256,2560]{1,0:T(8,128)(2,1)} custom-call(s32[20]{0:T(128)} %reshape.74.mask_ref, bf16[256,2560]{1,0:T(8,128)(2,1)} %q_ref.3, bf16[2,256,2560]{2,1,0:T(8,128)(2,1)} %collective-permute-done.2.refs_0_, bf16[2,256,2560]{2,1,0:T(8,128)(2,1)} %collective-permute-done.3.refs_1_, bf16[2,256,2560]{2,1,0:T(8,128)(2,1)} %collective-permute-done.4.refs_2_, ...), custom_call_target="tpu_custom_call" | custom-call | flops 3355443200 | bytes 31457280 | tf_op jit(solution)/shard_map/pallas_call | solution.py:126
  301.5 3.6 %fusion.16 = bf16[256,640]{1,0:T(8,128)(2,1)S(1)} fusion(bf16[256,2560]{1,0:T(8,128)(2,1)} %shard_map.65, bf16[2560,5120]{0,1:T(8,128)(2,1)} %all-gather.2.cloned.1.call-done, s32[]{:T(128)S(6)} %add.193), kind=kOutput, calls=%fused_computation.15 | convolution fusion | flops 839024640 | bytes 4915204 | tf_op jit(solution)/shard_map/dot_general | solution.py:187
  305.1 1.3 collective-permute-start.11
  306.4 3.1 fusion.19
  309.5 0.3 collective-permute-start.12
  309.9 3.1 fusion.22
  313.0 1.3 collective-permute-start.13
  314.3 3.1 fusion.13
  317.4 0.3 collective-permute-start.10
  317.8 8.3 %fusion.2 = bf16[256,2560]{1,0:T(8,128)(2,1)S(1)} fusion(bf16[256,2560]{1,0:T(8,128)(2,1)S(1)} %copy-done.3, bf16[2560,5120]{0,1:T(8,128)(2,1)} %all-gather.2.cloned.1.call-done, s32[]{:T(128)S(6)} %select_n.21), kind=kOutput, calls=%fused_computation.2 | convolution fusion | flops 3356098560 | bytes 15728644 | tf_op jit(solution)/shard_map/dot_general | solution.py:189
  326.1 2.9 collective-permute-done.13
  328.9 6.0 %collective-permute-done.10 = bf16[256,640]{1,0:T(8,128)(2,1)S(1)} collective-permute-done((bf16[256,640]{1,0:T(8,128)(2,1)S(1)}, bf16[256,640]{1,0:T(8,128)(2,1)S(1)}, u32[]{:S(2)}, u32[]{:S(2)}) %collective-permute-start.10) | collective-permute-done | bytes 327712 | tf_op jit(solution)/shard_map/ppermute | solution.py:28
  334.9 1.4 add_convert_fusion
  (33 shorter events, 0.4 us)
Async XLA Ops:
  6.5 237.0 %copy-start = (s32[32,12]{0,1:T(8,128)S(1)}, s32[32,12]{0,1:T(8,128)}, u32[]{:S(2)}) copy-start(s32[32,12]{0,1:T(8,128)} %param.10) | copy-start | bytes 4612
  6.5 294.9 %all-gather.2.cloned.1.call-start = ((), (), s32[]{:S(2)}) async-start(), calls=%async_computation | async-start | bytes 27852800 | tf_op jit(solution)/shard_map/all_gather | solution.py:175
  10.7 109.2 %collective-permute-start = (bf16[2,256,2560]{2,1,0:T(8,128)(2,1)}, bf16[2,256,2560]{2,1,0:T(8,128)(2,1)S(1)}, u32[]{:S(2)}, u32[]{:S(2)}) collective-permute-start(bf16[2,256,2560]{2,1,0:T(8,128)(2,1)} %pad_maximum_fusion.refs_0_), channel_id=1, source_target_pairs={{0,2},{2,4},{4,6},{6,8},{8,10},{10,12},{12,14},{1,3},{3,5},{5,7},{... | collective-permute-start | bytes 7864328 | tf_op jit(solution)/shard_map/ppermute | solution.py:24
  13.8 115.3 %collective-permute-start.1 = (bf16[2,256,2560]{2,1,0:T(8,128)(2,1)}, bf16[2,256,2560]{2,1,0:T(8,128)(2,1)}, u32[]{:S(2)}, u32[]{:S(2)}) collective-permute-start(bf16[2,256,2560]{2,1,0:T(8,128)(2,1)} %pad_maximum_fusion.refs_0_), channel_id=1, source_target_pairs={{2,0},{4,2},{6,4},{8,6},{10,8},{12,10},{14,12},{3,1},{5,3},{7,5},{... | collective-permute-start | bytes 7864328 | tf_op jit(solution)/shard_map/ppermute | solution.py:24
  16.9 166.3 %collective-permute-start.5 = (bf16[2,256,2560]{2,1,0:T(8,128)(2,1)}, bf16[2,256,2560]{2,1,0:T(8,128)(2,1)}, u32[]{:S(2)}, u32[]{:S(2)}) collective-permute-start(bf16[2,256,2560]{2,1,0:T(8,128)(2,1)} %pad_maximum_fusion.refs_0_), channel_id=1, source_target_pairs={{0,4},{2,6},{4,8},{6,10},{8,12},{10,14},{1,5},{3,7},{5,9},{7,11},{... | collective-permute-start | bytes 7864328 | tf_op jit(solution)/shard_map/ppermute | solution.py:24
  20.1 221.4 %collective-permute-start.7 = (bf16[2,256,2560]{2,1,0:T(8,128)(2,1)}, bf16[2,256,2560]{2,1,0:T(8,128)(2,1)}, u32[]{:S(2)}, u32[]{:S(2)}) collective-permute-start(bf16[2,256,2560]{2,1,0:T(8,128)(2,1)} %pad_maximum_fusion.refs_0_), channel_id=1, source_target_pairs={{4,0},{6,2},{8,4},{10,6},{12,8},{14,10},{5,1},{7,3},{9,5},{11,7},{... | collective-permute-start | bytes 7864328 | tf_op jit(solution)/shard_map/ppermute | solution.py:24
  23.7 219.9 %collective-permute-start.9 = (bf16[2,256,2560]{2,1,0:T(8,128)(2,1)}, bf16[2,256,2560]{2,1,0:T(8,128)(2,1)}, u32[]{:S(2)}, u32[]{:S(2)}) collective-permute-start(bf16[2,256,2560]{2,1,0:T(8,128)(2,1)} %pad_maximum_fusion.refs_0_), channel_id=1, source_target_pairs={{0,1},{1,0},{2,3},{3,2},{4,5},{5,4},{6,7},{7,6},{8,9},{9,8},{10,11... | collective-permute-start | bytes 7864328 | tf_op jit(solution)/shard_map/ppermute | solution.py:28
  25.6 218.2 %copy-start.4 = (s32[32]{0:T(128)S(1)}, s32[32]{0:T(128)}, u32[]{:S(2)}) copy-start(s32[32]{0:T(128)} %param.11) | copy-start | bytes 388
  119.9 18.1 %copy-start.2 = (bf16[2,256,2560]{2,1,0:T(8,128)(2,1)}, bf16[2,256,2560]{2,1,0:T(8,128)(2,1)S(1)}, u32[]{:S(2)}) copy-start(bf16[2,256,2560]{2,1,0:T(8,128)(2,1)S(1)} %collective-permute-done.refs_2_) | copy-start | bytes 7864324
  131.1 151.0 %collective-permute-start.2 = (bf16[2,256,2560]{2,1,0:T(8,128)(2,1)}, bf16[2,256,2560]{2,1,0:T(8,128)(2,1)}, u32[]{:S(2)}, u32[]{:S(2)}) collective-permute-start(bf16[2,256,2560]{2,1,0:T(8,128)(2,1)} %broadcast_select_fusion), channel_id=1, source_target_pairs={{1,4},{3,6},{4,1},{5,8},{6,3},{7,10},{8,5},{9,12},{10,7},{11,14},{... | collective-permute-start | bytes 7864328 | tf_op jit(solution)/shard_map/ppermute | solution.py:38
  138.0 144.1 %collective-permute-start.3 = (bf16[2,256,2560]{2,1,0:T(8,128)(2,1)S(1)}, bf16[2,256,2560]{2,1,0:T(8,128)(2,1)}, u32[]{:S(2)}, u32[]{:S(2)}) collective-permute-start(bf16[2,256,2560]{2,1,0:T(8,128)(2,1)S(1)} %collective-permute-done.refs_2_), channel_id=1, source_target_pairs={{0,1},{1,0},{2,3},{3,2},{4,5},{5,4},{6,7},{7,6},{8,9},{9,8},{10,11... | collective-permute-start | bytes 7864328 | tf_op jit(solution)/shard_map/ppermute | solution.py:28
  183.2 98.9 %collective-permute-start.4 = (bf16[2,256,2560]{2,1,0:T(8,128)(2,1)}, bf16[2,256,2560]{2,1,0:T(8,128)(2,1)}, u32[]{:S(2)}, u32[]{:S(2)}) collective-permute-start(bf16[2,256,2560]{2,1,0:T(8,128)(2,1)} %collective-permute-done.1.refs_3_), channel_id=1, source_target_pairs={{0,1},{1,0},{2,3},{3,2},{4,5},{5,4},{6,7},{7,6},{8,9},{9,8},{10,11... | collective-permute-start | bytes 7864328 | tf_op jit(solution)/shard_map/ppermute | solution.py:28
  241.5 40.6 %collective-permute-start.6 = (bf16[2,256,2560]{2,1,0:T(8,128)(2,1)}, bf16[2,256,2560]{2,1,0:T(8,128)(2,1)}, u32[]{:S(2)}, u32[]{:S(2)}) collective-permute-start(bf16[2,256,2560]{2,1,0:T(8,128)(2,1)} %collective-permute-done.5.refs_4_), channel_id=1, source_target_pairs={{0,1},{1,0},{2,3},{3,2},{4,5},{5,4},{6,7},{7,6},{8,9},{9,8},{10,11... | collective-permute-start | bytes 7864328 | tf_op jit(solution)/shard_map/ppermute | solution.py:28
  243.6 38.6 %collective-permute-start.8 = (bf16[2,256,2560]{2,1,0:T(8,128)(2,1)}, bf16[2,256,2560]{2,1,0:T(8,128)(2,1)}, u32[]{:S(2)}, u32[]{:S(2)}) collective-permute-start(bf16[2,256,2560]{2,1,0:T(8,128)(2,1)} %collective-permute-done.7.refs_5_), channel_id=1, source_target_pairs={{0,1},{1,0},{2,3},{3,2},{4,5},{5,4},{6,7},{7,6},{8,9},{9,8},{10,11... | collective-permute-start | bytes 7864328 | tf_op jit(solution)/shard_map/ppermute | solution.py:28
  301.5 4.9 %copy-start.3 = (bf16[256,2560]{1,0:T(8,128)(2,1)S(1)}, bf16[256,2560]{1,0:T(8,128)(2,1)}, u32[]{:S(2)}) copy-start(bf16[256,2560]{1,0:T(8,128)(2,1)} %shard_map.65) | copy-start | bytes 3932164
  305.1 20.9 %collective-permute-start.11 = (bf16[256,640]{1,0:T(8,128)(2,1)S(1)}, bf16[256,640]{1,0:T(8,128)(2,1)S(1)}, u32[]{:S(2)}, u32[]{:S(2)}) collective-permute-start(bf16[256,640]{1,0:T(8,128)(2,1)S(1)} %fusion.16), channel_id=1, source_target_pairs={{0,16},{16,0},{1,17},{17,1},{2,18},{18,2},{3,19},{19,3},{4,20},{20... | collective-permute-start | bytes 983048 | tf_op jit(solution)/shard_map/ppermute | solution.py:28
  309.5 16.5 %collective-permute-start.12 = (bf16[256,640]{1,0:T(8,128)(2,1)S(1)}, bf16[256,640]{1,0:T(8,128)(2,1)S(1)}, u32[]{:S(2)}, u32[]{:S(2)}) collective-permute-start(bf16[256,640]{1,0:T(8,128)(2,1)S(1)} %fusion.19), channel_id=1, source_target_pairs={{0,16},{16,0},{1,17},{17,1},{2,18},{18,2},{3,19},{19,3},{4,20},{20... | collective-permute-start | bytes 983048 | tf_op jit(solution)/shard_map/ppermute | solution.py:28
  313.0 15.9 %collective-permute-start.13 = (bf16[256,640]{1,0:T(8,128)(2,1)S(1)}, bf16[256,640]{1,0:T(8,128)(2,1)S(1)}, u32[]{:S(2)}, u32[]{:S(2)}) collective-permute-start(bf16[256,640]{1,0:T(8,128)(2,1)S(1)} %fusion.22), channel_id=1, source_target_pairs={{0,16},{16,0},{1,17},{17,1},{2,18},{18,2},{3,19},{19,3},{4,20},{20... | collective-permute-start | bytes 983048 | tf_op jit(solution)/shard_map/ppermute | solution.py:28
  317.4 17.5 %collective-permute-start.10 = (bf16[256,640]{1,0:T(8,128)(2,1)S(1)}, bf16[256,640]{1,0:T(8,128)(2,1)S(1)}, u32[]{:S(2)}, u32[]{:S(2)}) collective-permute-start(bf16[256,640]{1,0:T(8,128)(2,1)S(1)} %fusion.13), channel_id=1, source_target_pairs={{0,16},{16,0},{1,17},{17,1},{2,18},{18,2},{3,19},{19,3},{4,20},{20... | collective-permute-start | bytes 983048 | tf_op jit(solution)/shard_map/ppermute | solution.py:28
  317.7 18.6 %copy-start.1 = (s32[32,12]{0,1:T(8,128)S(1)}, s32[32,12]{0,1:T(8,128)}, u32[]{:S(2)}) copy-start(s32[32,12]{0,1:T(8,128)} %param.10) | copy-start | bytes 4612
Sparse Core Ops, SparseCore 0:
  9.0 256.0 all-gather.1

commit v9 on v8

--- a/solution.py
+++ b/solution.py
@@ -28,14 +28,21 @@
     return lax.ppermute(x, axis, [(0, 1), (1, 0)])
 
 
-def third_neighbour(x, chips):
-    peers = chips * 2
-    pairs = []
-    for s in range(peers):
-        t = s + 3 if s % 2 == 1 else s - 3
-        if 0 <= t < peers:
-            pairs.append((s, t))
-    return lax.ppermute(x, SEQ, pairs)
+def fifth_routes(onward, across, chips):
+    far, near = [], []
+    for c in range(chips):
+        if c % 2 == 0:
+            src = 2 * c + 1
+            if c + 2 < chips:
+                far.append((src, 2 * (c + 2)))
+            if c + 1 < chips:
+                near.append((src, 2 * (c + 1)))
+        else:
+            src = 2 * c
+            if c - 2 >= 0:
+                far.append((src, 2 * (c - 2) + 1))
+            near.append((src, 2 * (c - 1) + 1))
+    return lax.ppermute(onward, SEQ, far), lax.ppermute(across, SEQ, near)
 
 
 def attention_kernel(n_blocks, tiles, group, carry_in, finish, mask_ref, q_ref, *refs):
@@ -162,7 +169,12 @@
             early.append((-sign * 2 * chip_step, block))
     from_below, from_above = fetched[0][1], fetched[1][1]
     onward = jnp.where(core == 1, from_below, from_above)
-    late = [(-REACH + 2 * REACH * core, third_neighbour(onward, chips))]
+    two_below, two_above = fetched[2][1], fetched[3][1]
+    across = jnp.where(core == 1, two_below, two_above)
+    by_chip_hop, by_level_hop = fifth_routes(onward, across, chips)
+    chip = lax.axis_index("chip")
+    fifth = jnp.where((chip + core) % 2 == 0, by_chip_hop, by_level_hop)
+    late = [(-REACH + 2 * REACH * core, fifth)]
     for offset, block in fetched:
         passed = swapped(block, "core")
         late.append((offset + 1 - 2 * core, passed))

time: 344 us -> 367 us (1.067)
  the two profiles are of different devices: /device:TPU:9 before, /device:TPU:26 now
where the time goes in v9:
time: 367 us
  waiting for transfers between devices  220 us (60%)
  starting transfers between devices  56.6 us (15%)
  Pallas kernels  37.1 us (10%)
  matrix products  21.3 us (6%)
  other arithmetic  14.8 us (4%)
  between operations  13.6 us (4%)
    ppermute x4, waiting for transfers between devices, shifted(): return lax.ppermute(x, axis, pairs)  211 us
    ppermute x9, starting transfers between devices, swapped(): return lax.ppermute(x, axis, [(0, 1), (1, 0)])  39.1 us
    pallas_call x2, Pallas kernels, block_attention(): pl.pallas_call(functools.partial(attention_kernel, n_blocks, tiles, group...  37.1 us
    ppermute x4, starting transfers between devices, shifted(): return lax.ppermute(x, axis, pairs)  14 us
    dot_general x4, matrix products, local(): jnp.dot(attended, theirs[:, cols], preferred_element_type=jnp.float32)  13 us
    ppermute x9, waiting for transfers between devices, swapped(): return lax.ppermute(x, axis, [(0, 1), (1, 0)])  8.71 us
    dot_general x1, matrix products, local(): jnp.dot(attended, mine, preferred_element_type=jnp.float32)  8.31 us
  transfers between devices with their start and end apart: 16, of which 5 were waited for; matrix products, arithmetic and copies ran while one was open for 9% of the time, Pallas kernels for 10%

profile of v9, /device:TPU:26, one launch (start us, length us, event | category | flops | bytes accessed | tf_op | source)
XLA Modules:
  0.0 366.7 jit_solution(3436839456119009924)
XLA Ops:
  6.5 0.7 all-gather.2.cloned.1.call-update
  7.3 3.5 pad_maximum_fusion.refs_0_
  10.8 1.3 collective-permute-start.3
  12.0 6.0 %collective-permute-start.4 = (bf16[2,256,2560]{2,1,0:T(8,128)(2,1)}, bf16[2,256,2560]{2,1,0:T(8,128)(2,1)}, u32[]{:S(2)}, u32[]{:S(2)}) collective-permute-start(bf16[2,256,2560]{2,1,0:T(8,128)(2,1)} %pad_maximum_fusion.refs_0_), channel_id=1, source_target_pairs={{4,0},{6,2},{8,4},{10,6},{12,8},{14,10},{5,1},{7,3},{9,5},{11,7},{... | collective-permute-start | bytes 7864328 | tf_op jit(solution)/shard_map/ppermute | solution.py:24
  18.1 3.4 collective-permute-start
  21.5 3.3 collective-permute-start.1
  24.9 101.6 %collective-permute-done.3.refs_4_ = bf16[2,256,2560]{2,1,0:T(8,128)(2,1)S(1)} collective-permute-done((bf16[2,256,2560]{2,1,0:T(8,128)(2,1)}, bf16[2,256,2560]{2,1,0:T(8,128)(2,1)S(1)}, u32[]{:S(2)}, u32[]{:S(2)}) %collective-permute-start.3) | collective-permute-done | bytes 2621472 | tf_op jit(solution)/shard_map/ppermute | solution.py:24
  126.5 3.5 collective-permute-done.4.refs_5_
  130.0 2.2 broadcast_select_fusion
  132.2 2.1 collective-permute-start.5
  134.3 105.6 %collective-permute-done.refs_2_ = bf16[2,256,2560]{2,1,0:T(8,128)(2,1)} collective-permute-done((bf16[2,256,2560]{2,1,0:T(8,128)(2,1)}, bf16[2,256,2560]{2,1,0:T(8,128)(2,1)}, u32[]{:S(2)}, u32[]{:S(2)}) %collective-permute-start) | collective-permute-done | bytes 2621472 | tf_op jit(solution)/shard_map/ppermute | solution.py:24
  240.0 3.5 broadcast_select_fusion.1
  243.5 1.3 collective-permute-start.2
  244.8 0.5 collective-permute-start.7
  245.4 34.1 %collective-permute-start.9 = (bf16[2,256,2560]{2,1,0:T(8,128)(2,1)}, bf16[2,256,2560]{2,1,0:T(8,128)(2,1)}, u32[]{:S(2)}, u32[]{:S(2)}) collective-permute-start(bf16[2,256,2560]{2,1,0:T(8,128)(2,1)} %collective-permute-done.4.refs_5_), channel_id=1, source_target_pairs={{0,1},{1,0},{2,3},{3,2},{4,5},{5,4},{6,7},{7,6},{8,9},{9,8},{10,11... | collective-permute-start | bytes 7864328 | tf_op jit(solution)/shard_map/ppermute | solution.py:28
  279.9 0.5 and_reduce_fusion
  280.4 0.1 copy.30
  280.5 0.1 copy.31
  280.6 0.1 copy.32
  280.8 0.1 copy.33
  280.9 0.1 copy.34
  281.0 0.1 copy.35
  281.1 0.1 stack.63
  281.2 0.1 copy.36
  281.3 0.6 reshape.75.mask_ref
  281.9 0.1 copy.24
  282.0 0.1 copy.25
  282.2 0.1 copy.26
  282.3 0.1 copy.27
  282.4 0.1 copy.28
  282.5 0.1 stack.53
  282.6 0.1 copy.29
  282.7 0.6 reshape.74.mask_ref
  283.3 17.7 %shard_map.64 = (f32[256,2560]{1,0:T(8,128)}, f32[256,2560]{1,0:T(8,128)}, f32[256,2560]{1,0:T(8,128)}) custom-call(s32[24]{0:T(128)} %reshape.75.mask_ref, bf16[256,2560]{1,0:T(8,128)(2,1)} %q_ref.3, bf16[2,256,2560]{2,1,0:T(8,128)(2,1)} %pad_maximum_fusion.refs_0_, bf16[2,256,2560]{2,1,0:T(8,128)(2,1)} %collective-permute-done.10.refs_1_, ...), custom_call_target="tpu_custom_call" | custom-call | flops 4026531840 | bytes 34078720 | tf_op jit(solution)/shard_map/pallas_call | solution.py:133
  301.1 3.6 broadcast_select_fusion.2.refs_0_
  304.7 19.3 %shard_map.65 = bf16[256,2560]{1,0:T(8,128)(2,1)} custom-call(s32[20]{0:T(128)} %reshape.74.mask_ref, bf16[256,2560]{1,0:T(8,128)(2,1)} %q_ref.3, bf16[2,256,2560]{2,1,0:T(8,128)(2,1)} %broadcast_select_fusion.2.refs_0_, bf16[2,256,2560]{2,1,0:T(8,128)(2,1)} %collective-permute-done.6.refs_1_, bf16[2,256,2560]{2,1,0:T(8,128)(2,1)} %collective-permute-done.7.refs_2_, ...), custom_call_target="tpu_custom_call" | custom-call | flops 3355443200 | bytes 31457280 | tf_op jit(solution)/shard_map/pallas_call | solution.py:133
  324.0 3.6 fusion.16
  327.7 0.6 collective-permute-start.12
  328.3 3.1 fusion.19
  331.4 1.6 collective-permute-start.13
  333.0 3.1 fusion.22
  336.1 0.6 collective-permute-start.14
  336.7 3.1 fusion.13
  339.8 1.6 collective-permute-start.11
  341.4 8.3 %fusion.2 = bf16[256,2560]{1,0:T(8,128)(2,1)S(1)} fusion(bf16[256,2560]{1,0:T(8,128)(2,1)S(1)} %copy-done.3, bf16[2560,5120]{0,1:T(8,128)(2,1)} %all-gather.2.cloned.1.call-done, s32[]{:T(128)S(6)} %select_n.42), kind=kOutput, calls=%fused_computation.2 | convolution fusion | flops 3356098560 | bytes 15728644 | tf_op jit(solution)/shard_map/dot_general | solution.py:201
  349.7 2.6 collective-permute-done.14
  352.3 6.1 %collective-permute-done.11 = bf16[256,640]{1,0:T(8,128)(2,1)S(1)} collective-permute-done((bf16[256,640]{1,0:T(8,128)(2,1)S(1)}, bf16[256,640]{1,0:T(8,128)(2,1)S(1)}, u32[]{:S(2)}, u32[]{:S(2)}) %collective-permute-start.11) | collective-permute-done | bytes 327712 | tf_op jit(solution)/shard_map/ppermute | solution.py:28
  358.4 1.4 add_convert_fusion
  (37 shorter events, 0.6 us)
Async XLA Ops:
  6.5 273.0 %copy-start = (s32[32,12]{0,1:T(8,128)S(1)}, s32[32,12]{0,1:T(8,128)}, u32[]{:S(2)}) copy-start(s32[32,12]{0,1:T(8,128)} %param.10) | copy-start | bytes 4612
  6.5 317.5 %all-gather.2.cloned.1.call-start = ((), (), s32[]{:S(2)}) async-start(), calls=%async_computation | async-start | bytes 27852800 | tf_op jit(solution)/shard_map/all_gather | solution.py:187
  10.8 115.7 %collective-permute-start.3 = (bf16[2,256,2560]{2,1,0:T(8,128)(2,1)}, bf16[2,256,2560]{2,1,0:T(8,128)(2,1)S(1)}, u32[]{:S(2)}, u32[]{:S(2)}) collective-permute-start(bf16[2,256,2560]{2,1,0:T(8,128)(2,1)} %pad_maximum_fusion.refs_0_), channel_id=1, source_target_pairs={{0,4},{2,6},{4,8},{6,10},{8,12},{10,14},{1,5},{3,7},{5,9},{7,11},{... | collective-permute-start | bytes 7864328 | tf_op jit(solution)/shard_map/ppermute | solution.py:24
  12.0 117.9 %collective-permute-start.4 = (bf16[2,256,2560]{2,1,0:T(8,128)(2,1)}, bf16[2,256,2560]{2,1,0:T(8,128)(2,1)}, u32[]{:S(2)}, u32[]{:S(2)}) collective-permute-start(bf16[2,256,2560]{2,1,0:T(8,128)(2,1)} %pad_maximum_fusion.refs_0_), channel_id=1, source_target_pairs={{4,0},{6,2},{8,4},{10,6},{12,8},{14,10},{5,1},{7,3},{9,5},{11,7},{... | collective-permute-start | bytes 7864328 | tf_op jit(solution)/shard_map/ppermute | solution.py:24
  18.1 221.9 %collective-permute-start = (bf16[2,256,2560]{2,1,0:T(8,128)(2,1)}, bf16[2,256,2560]{2,1,0:T(8,128)(2,1)}, u32[]{:S(2)}, u32[]{:S(2)}) collective-permute-start(bf16[2,256,2560]{2,1,0:T(8,128)(2,1)} %pad_maximum_fusion.refs_0_), channel_id=1, source_target_pairs={{0,2},{2,4},{4,6},{6,8},{8,10},{10,12},{12,14},{1,3},{3,5},{5,7},{... | collective-permute-start | bytes 7864328 | tf_op jit(solution)/shard_map/ppermute | solution.py:24
  21.5 218.5 %collective-permute-start.1 = (bf16[2,256,2560]{2,1,0:T(8,128)(2,1)}, bf16[2,256,2560]{2,1,0:T(8,128)(2,1)}, u32[]{:S(2)}, u32[]{:S(2)}) collective-permute-start(bf16[2,256,2560]{2,1,0:T(8,128)(2,1)} %pad_maximum_fusion.refs_0_), channel_id=1, source_target_pairs={{2,0},{4,2},{6,4},{8,6},{10,8},{12,10},{14,12},{3,1},{5,3},{7,5},{... | collective-permute-start | bytes 7864328 | tf_op jit(solution)/shard_map/ppermute | solution.py:24
  24.8 220.5 %collective-permute-start.10 = (bf16[2,256,2560]{2,1,0:T(8,128)(2,1)}, bf16[2,256,2560]{2,1,0:T(8,128)(2,1)}, u32[]{:S(2)}, u32[]{:S(2)}) collective-permute-start(bf16[2,256,2560]{2,1,0:T(8,128)(2,1)} %pad_maximum_fusion.refs_0_), channel_id=1, source_target_pairs={{0,1},{1,0},{2,3},{3,2},{4,5},{5,4},{6,7},{7,6},{8,9},{9,8},{10,11... | collective-permute-start | bytes 7864328 | tf_op jit(solution)/shard_map/ppermute | solution.py:28
  126.5 118.9 %copy-start.2 = (bf16[2,256,2560]{2,1,0:T(8,128)(2,1)}, bf16[2,256,2560]{2,1,0:T(8,128)(2,1)S(1)}, u32[]{:S(2)}) copy-start(bf16[2,256,2560]{2,1,0:T(8,128)(2,1)S(1)} %collective-permute-done.3.refs_4_) | copy-start | bytes 7864324
  132.2 147.5 %copy-start.4 = (s32[32]{0:T(128)S(1)}, s32[32]{0:T(128)}, u32[]{:S(2)}) copy-start(s32[32]{0:T(128)} %param.11) | copy-start | bytes 388
  132.2 113.2 %collective-permute-start.5 = (bf16[2,256,2560]{2,1,0:T(8,128)(2,1)S(1)}, bf16[2,256,2560]{2,1,0:T(8,128)(2,1)}, u32[]{:S(2)}, u32[]{:S(2)}) collective-permute-start(bf16[2,256,2560]{2,1,0:T(8,128)(2,1)S(1)} %broadcast_select_fusion), channel_id=1, source_target_pairs={{1,2},{2,1},{5,6},{6,5},{9,10},{10,9},{13,14},{14,13},{17,18},{18,... | collective-permute-start | bytes 7864328 | tf_op jit(solution)/shard_map/ppermute | solution.py:45
  243.5 57.6 %collective-permute-start.2 = (bf16[2,256,2560]{2,1,0:T(8,128)(2,1)}, bf16[2,256,2560]{2,1,0:T(8,128)(2,1)}, u32[]{:S(2)}, u32[]{:S(2)}) collective-permute-start(bf16[2,256,2560]{2,1,0:T(8,128)(2,1)} %broadcast_select_fusion.1), channel_id=1, source_target_pairs={{1,4},{5,8},{6,3},{9,12},{10,7},{14,11},{17,20},{21,24},{22,19},{2... | collective-permute-start | bytes 7864328 | tf_op jit(solution)/shard_map/ppermute | solution.py:45
  244.8 59.9 %collective-permute-start.6 = (bf16[2,256,2560]{2,1,0:T(8,128)(2,1)}, bf16[2,256,2560]{2,1,0:T(8,128)(2,1)}, u32[]{:S(2)}, u32[]{:S(2)}) collective-permute-start(bf16[2,256,2560]{2,1,0:T(8,128)(2,1)} %collective-permute-done.refs_2_), channel_id=1, source_target_pairs={{0,1},{1,0},{2,3},{3,2},{4,5},{5,4},{6,7},{7,6},{8,9},{9,8},{10,11... | collective-permute-start | bytes 7864328 | tf_op jit(solution)/shard_map/ppermute | solution.py:28
  244.8 59.8 %collective-permute-start.7 = (bf16[2,256,2560]{2,1,0:T(8,128)(2,1)}, bf16[2,256,2560]{2,1,0:T(8,128)(2,1)}, u32[]{:S(2)}, u32[]{:S(2)}) collective-permute-start(bf16[2,256,2560]{2,1,0:T(8,128)(2,1)} %collective-permute-done.1.refs_3_), channel_id=1, source_target_pairs={{0,1},{1,0},{2,3},{3,2},{4,5},{5,4},{6,7},{7,6},{8,9},{9,8},{10,11... | collective-permute-start | bytes 7864328 | tf_op jit(solution)/shard_map/ppermute | solution.py:28
  245.3 59.3 %collective-permute-start.8 = (bf16[2,256,2560]{2,1,0:T(8,128)(2,1)S(1)}, bf16[2,256,2560]{2,1,0:T(8,128)(2,1)}, u32[]{:S(2)}, u32[]{:S(2)}) collective-permute-start(bf16[2,256,2560]{2,1,0:T(8,128)(2,1)S(1)} %collective-permute-done.3.refs_4_), channel_id=1, source_target_pairs={{0,1},{1,0},{2,3},{3,2},{4,5},{5,4},{6,7},{7,6},{8,9},{9,8},{10,11... | collective-permute-start | bytes 7864328 | tf_op jit(solution)/shard_map/ppermute | solution.py:28
  245.4 59.2 %collective-permute-start.9 = (bf16[2,256,2560]{2,1,0:T(8,128)(2,1)}, bf16[2,256,2560]{2,1,0:T(8,128)(2,1)}, u32[]{:S(2)}, u32[]{:S(2)}) collective-permute-start(bf16[2,256,2560]{2,1,0:T(8,128)(2,1)} %collective-permute-done.4.refs_5_), channel_id=1, source_target_pairs={{0,1},{1,0},{2,3},{3,2},{4,5},{5,4},{6,7},{7,6},{8,9},{9,8},{10,11... | collective-permute-start | bytes 7864328 | tf_op jit(solution)/shard_map/ppermute | solution.py:28
  324.0 4.3 %copy-start.3 = (bf16[256,2560]{1,0:T(8,128)(2,1)S(1)}, bf16[256,2560]{1,0:T(8,128)(2,1)}, u32[]{:S(2)}) copy-start(bf16[256,2560]{1,0:T(8,128)(2,1)} %shard_map.65) | copy-start | bytes 3932164
  327.7 22.1 %collective-permute-start.12 = (bf16[256,640]{1,0:T(8,128)(2,1)S(1)}, bf16[256,640]{1,0:T(8,128)(2,1)S(1)}, u32[]{:S(2)}, u32[]{:S(2)}) collective-permute-start(bf16[256,640]{1,0:T(8,128)(2,1)S(1)} %fusion.16), channel_id=1, source_target_pairs={{0,16},{16,0},{1,17},{17,1},{2,18},{18,2},{3,19},{19,3},{4,20},{20... | collective-permute-start | bytes 983048 | tf_op jit(solution)/shard_map/ppermute | solution.py:28
  331.4 18.3 %collective-permute-start.13 = (bf16[256,640]{1,0:T(8,128)(2,1)S(1)}, bf16[256,640]{1,0:T(8,128)(2,1)S(1)}, u32[]{:S(2)}, u32[]{:S(2)}) collective-permute-start(bf16[256,640]{1,0:T(8,128)(2,1)S(1)} %fusion.19), channel_id=1, source_target_pairs={{0,16},{16,0},{1,17},{17,1},{2,18},{18,2},{3,19},{19,3},{4,20},{20... | collective-permute-start | bytes 983048 | tf_op jit(solution)/shard_map/ppermute | solution.py:28
  336.1 16.2 %collective-permute-start.14 = (bf16[256,640]{1,0:T(8,128)(2,1)S(1)}, bf16[256,640]{1,0:T(8,128)(2,1)S(1)}, u32[]{:S(2)}, u32[]{:S(2)}) collective-permute-start(bf16[256,640]{1,0:T(8,128)(2,1)S(1)} %fusion.22), channel_id=1, source_target_pairs={{0,16},{16,0},{1,17},{17,1},{2,18},{18,2},{3,19},{19,3},{4,20},{20... | collective-permute-start | bytes 983048 | tf_op jit(solution)/shard_map/ppermute | solution.py:28
  339.8 18.6 %collective-permute-start.11 = (bf16[256,640]{1,0:T(8,128)(2,1)S(1)}, bf16[256,640]{1,0:T(8,128)(2,1)S(1)}, u32[]{:S(2)}, u32[]{:S(2)}) collective-permute-start(bf16[256,640]{1,0:T(8,128)(2,1)S(1)} %fusion.13), channel_id=1, source_target_pairs={{0,16},{16,0},{1,17},{17,1},{2,18},{18,2},{3,19},{19,3},{4,20},{20... | collective-permute-start | bytes 983048 | tf_op jit(solution)/shard_map/ppermute | solution.py:28
  341.4 18.4 %copy-start.1 = (s32[32,12]{0,1:T(8,128)S(1)}, s32[32,12]{0,1:T(8,128)}, u32[]{:S(2)}) copy-start(s32[32,12]{0,1:T(8,128)} %param.10) | copy-start | bytes 4612
Sparse Core Ops, SparseCore 0:
  9.0 275.9 all-gather.1

commit v10 on v8

--- a/solution.py
+++ b/solution.py
@@ -165,7 +165,7 @@
     late = [(-REACH + 2 * REACH * core, third_neighbour(onward, chips))]
     for offset, block in fetched:
         passed = swapped(block, "core")
-        late.append((offset + 1 - 2 * core, passed))
+        early.append((offset + 1 - 2 * core, passed))
 
     def masks_of(blocks):
         return jnp.stack([tile_need(offset) for offset, _ in blocks]).astype(jnp.int32).reshape(-1)

time: 344 us -> 340 us (0.988)
  starting transfers between devices: 72.2 us -> 31.4 us
  waiting for transfers between devices: 188 us -> 220 us
  Pallas kernels: 37 us -> 41.5 us
    ppermute x4, waiting for transfers between devices: 162 us -> 206 us  [shifted(): return lax.ppermute(x, axis, pairs)]
    ppermute x9, starting transfers between devices: 52.3 us -> 16.5 us  [swapped(): return lax.ppermute(x, axis, [(0, 1), (1, 0)])]
    ppermute x1, waiting for transfers between devices: 17 us -> 4.67 us  [third_neighbour(): return lax.ppermute(x, SEQ, pairs)]
    ppermute x1, starting transfers between devices: 6.92 us -> 1.91 us  [third_neighbour(): return lax.ppermute(x, SEQ, pairs)]
    pallas_call x2, Pallas kernels: 37 us -> 41.5 us  [block_attention(): pl.pallas_call(functools.partial(attention_kernel, n_blocks, tiles, group...]
  transfers between devices with their start and end apart: 15 -> 15, of which waited for: 6 -> 7; matrix products, arithmetic and copies ran while one was open for 8% -> 8% of each run, Pallas kernels for 11% -> 12%
where the time goes in v10:
time: 340 us; the launch traced here: 339 us
  waiting for transfers between devices  220 us (65%)
  Pallas kernels  41.5 us (12%)
  starting transfers between devices  31.4 us (9%)
  matrix products  21.3 us (6%)
  between operations  13.6 us (4%)
  other arithmetic  7.46 us (2%)
  local copies, waits for them, and re-layouts  4.32 us (1%)
    ppermute x4, waiting for transfers between devices, shifted(): return lax.ppermute(x, axis, pairs)  206 us
    pallas_call x2, Pallas kernels, block_attention(): pl.pallas_call(functools.partial(attention_kernel, n_blocks, tiles, group...  41.5 us
    ppermute x9, starting transfers between devices, swapped(): return lax.ppermute(x, axis, [(0, 1), (1, 0)])  16.5 us
    dot_general x4, matrix products, local(): jnp.dot(attended, theirs[:, cols], preferred_element_type=jnp.float32)  13 us
    ppermute x4, starting transfers between devices, shifted(): return lax.ppermute(x, axis, pairs)  12.9 us
    ppermute x9, waiting for transfers between devices, swapped(): return lax.ppermute(x, axis, [(0, 1), (1, 0)])  8.85 us
    dot_general x1, matrix products, local(): jnp.dot(attended, mine, preferred_element_type=jnp.float32)  8.31 us
  transfers between devices with their start and end apart: 15, of which 7 were waited for; matrix products, arithmetic and copies ran while one was open for 8% of the time, Pallas kernels for 12%

profile of v10, /device:TPU:9, one launch (start us, length us, event | category | flops | bytes accessed | tf_op | source)
XLA Modules:
  0.0 339.4 jit_solution(4512137427435358721)
XLA Ops:
  6.5 0.7 all-gather.2.cloned.1.call-update
  7.3 2.0 pad_maximum_fusion.refs_0_
  9.2 3.1 collective-permute-start
  12.4 3.0 collective-permute-start.1
  15.4 3.2 collective-permute-start.4
  18.6 3.5 %collective-permute-start.5 = (bf16[2,256,2560]{2,1,0:T(8,128)(2,1)S(1)}, bf16[2,256,2560]{2,1,0:T(8,128)(2,1)}, u32[]{:S(2)}, u32[]{:S(2)}) collective-permute-start(bf16[2,256,2560]{2,1,0:T(8,128)(2,1)S(1)} %pad_maximum_fusion.refs_0_), channel_id=1, source_target_pairs={{4,0},{6,2},{8,4},{10,6},{12,8},{14,10},{5,1},{7,3},{9,5},{11,7},{... | collective-permute-start | bytes 7864328 | tf_op jit(solution)/shard_map/ppermute | solution.py:24
  22.2 1.9 collective-permute-start.3
  24.0 95.3 %collective-permute-done.refs_2_ = bf16[2,256,2560]{2,1,0:T(8,128)(2,1)} collective-permute-done((bf16[2,256,2560]{2,1,0:T(8,128)(2,1)S(1)}, bf16[2,256,2560]{2,1,0:T(8,128)(2,1)}, u32[]{:S(2)}, u32[]{:S(2)}) %collective-permute-start) | collective-permute-done | bytes 2621472 | tf_op jit(solution)/shard_map/ppermute | solution.py:24
  119.3 3.0 collective-permute-start.6
  122.4 4.7 %collective-permute-done.1.refs_3_ = bf16[2,256,2560]{2,1,0:T(8,128)(2,1)} collective-permute-done((bf16[2,256,2560]{2,1,0:T(8,128)(2,1)S(1)}, bf16[2,256,2560]{2,1,0:T(8,128)(2,1)}, u32[]{:S(2)}, u32[]{:S(2)}) %collective-permute-start.1) | collective-permute-done | bytes 2621472 | tf_op jit(solution)/shard_map/ppermute | solution.py:24
  127.1 2.7 collective-permute-start.7
  129.8 1.1 collective-permute-done.4.refs_4_
  130.9 2.1 collective-permute-start.8
  133.0 104.4 %collective-permute-done.5.refs_5_ = bf16[2,256,2560]{2,1,0:T(8,128)(2,1)} collective-permute-done((bf16[2,256,2560]{2,1,0:T(8,128)(2,1)S(1)}, bf16[2,256,2560]{2,1,0:T(8,128)(2,1)}, u32[]{:S(2)}, u32[]{:S(2)}) %collective-permute-start.5) | collective-permute-done | bytes 2621472 | tf_op jit(solution)/shard_map/ppermute | solution.py:24
  237.4 3.7 %collective-permute-start.9 = (bf16[2,256,2560]{2,1,0:T(8,128)(2,1)}, bf16[2,256,2560]{2,1,0:T(8,128)(2,1)}, u32[]{:S(2)}, u32[]{:S(2)}) collective-permute-start(bf16[2,256,2560]{2,1,0:T(8,128)(2,1)} %collective-permute-done.5.refs_5_), channel_id=1, source_target_pairs={{0,1},{1,0},{2,3},{3,2},{4,5},{5,4},{6,7},{7,6},{8,9},{9,8},{10,11... | collective-permute-start | bytes 7864328 | tf_op jit(solution)/shard_map/ppermute | solution.py:28
  241.1 3.5 %broadcast_select_fusion = bf16[2,256,2560]{2,1,0:T(8,128)(2,1)} fusion(bf16[2,256,2560]{2,1,0:T(8,128)(2,1)} %collective-permute-done.refs_2_, bf16[2,256,2560]{2,1,0:T(8,128)(2,1)} %collective-permute-done.1.refs_3_, pred[]{:T(512)S(6)} %eq.51), kind=kLoop, calls=%fused_computation.13 | loop fusion | flops 1310720 | bytes 7864321 | tf_op jit(solution)/shard_map/jit(_where)/select_n | solution.py:164
  244.5 1.9 collective-permute-start.2
  246.9 0.5 and_reduce_fusion
  247.4 0.1 copy.22
  247.5 0.1 copy.23
  247.6 0.1 copy.24
  247.7 0.1 copy.25
  247.8 0.1 copy.26
  248.0 0.1 copy.27
  248.1 0.1 copy.28
  248.2 0.1 copy.29
  248.3 0.1 copy.30
  248.4 0.1 copy.31
  248.5 0.1 stack.56
  248.7 0.1 copy.32
  248.8 0.6 reshape.77.mask_ref
  249.4 0.6 reshape.76.mask_ref
  250.0 26.3 %shard_map.64 = (f32[256,2560]{1,0:T(8,128)}, f32[256,2560]{1,0:T(8,128)}, f32[256,2560]{1,0:T(8,128)}) custom-call(s32[40]{0:T(128)} %reshape.77.mask_ref, bf16[256,2560]{1,0:T(8,128)(2,1)} %q_ref.3, bf16[2,256,2560]{2,1,0:T(8,128)(2,1)} %copy-done.2, bf16[2,256,2560]{2,1,0:T(8,128)(2,1)} %collective-permute-done.3.refs_1_, ...), custom_call_target="tpu_custom_call" | custom-call | flops 6710886400 | bytes 44564480 | tf_op jit(solution)/shard_map/pallas_call | solution.py:126
  276.3 4.7 %collective-permute-done.2.refs_0_ = bf16[2,256,2560]{2,1,0:T(8,128)(2,1)S(1)} collective-permute-done((bf16[2,256,2560]{2,1,0:T(8,128)(2,1)}, bf16[2,256,2560]{2,1,0:T(8,128)(2,1)S(1)}, u32[]{:S(2)}, u32[]{:S(2)}) %collective-permute-start.2) | collective-permute-done | bytes 2621472 | tf_op jit(solution)/shard_map/ppermute | solution.py:38
  281.0 1.5 copy-done.3
  282.5 15.2 %shard_map.65 = bf16[256,2560]{1,0:T(8,128)(2,1)} custom-call(s32[4]{0:T(128)} %reshape.76.mask_ref, bf16[256,2560]{1,0:T(8,128)(2,1)} %q_ref.3, bf16[2,256,2560]{2,1,0:T(8,128)(2,1)} %copy-done.3, f32[256,2560]{1,0:T(8,128)} %get-tuple-element.8.refs_1_, f32[256,2560]{1,0:T(8,128)} %get-tuple-element.9.refs_2_, f32[256,2560]{1,0:T(8,128)} %get-tuple-element.10.refs_3_), custom_call_target="tpu_custom_call" | custom-call | flops 671088640 | bytes 20971520 | tf_op jit(solution)/shard_map/pallas_call | solution.py:126
  297.7 3.6 %fusion.16 = bf16[256,640]{1,0:T(8,128)(2,1)S(1)} fusion(bf16[256,2560]{1,0:T(8,128)(2,1)} %shard_map.65, bf16[2560,5120]{0,1:T(8,128)(2,1)} %all-gather.2.cloned.1.call-done, s32[]{:T(128)S(6)} %add.193), kind=kOutput, calls=%fused_computation.15 | convolution fusion | flops 839024640 | bytes 4915204 | tf_op jit(solution)/shard_map/dot_general | solution.py:187
  301.4 1.3 collective-permute-start.11
  302.6 3.1 fusion.19
  305.8 0.3 collective-permute-start.12
  306.1 3.1 fusion.22
  309.3 1.3 collective-permute-start.13
  310.5 3.1 fusion.13
  313.7 0.3 collective-permute-start.10
  314.0 8.3 %fusion.2 = bf16[256,2560]{1,0:T(8,128)(2,1)S(1)} fusion(bf16[256,2560]{1,0:T(8,128)(2,1)S(1)} %copy-done.4, bf16[2560,5120]{0,1:T(8,128)(2,1)} %all-gather.2.cloned.1.call-done, s32[]{:T(128)S(6)} %select_n.21), kind=kOutput, calls=%fused_computation.2 | convolution fusion | flops 3356098560 | bytes 15728644 | tf_op jit(solution)/shard_map/dot_general | solution.py:189
  322.3 2.9 collective-permute-done.13
  325.2 6.0 %collective-permute-done.10 = bf16[256,640]{1,0:T(8,128)(2,1)S(1)} collective-permute-done((bf16[256,640]{1,0:T(8,128)(2,1)S(1)}, bf16[256,640]{1,0:T(8,128)(2,1)S(1)}, u32[]{:S(2)}, u32[]{:S(2)}) %collective-permute-start.10) | collective-permute-done | bytes 327712 | tf_op jit(solution)/shard_map/ppermute | solution.py:28
  331.2 1.4 add_convert_fusion
  (32 shorter events, 0.4 us)
Async XLA Ops:
  6.5 239.9 %copy-start = (s32[32,12]{0,1:T(8,128)S(1)}, s32[32,12]{0,1:T(8,128)}, u32[]{:S(2)}) copy-start(s32[32,12]{0,1:T(8,128)} %param.10) | copy-start | bytes 4612
  6.5 291.2 %all-gather.2.cloned.1.call-start = ((), (), s32[]{:S(2)}) async-start(), calls=%async_computation | async-start | bytes 27852800 | tf_op jit(solution)/shard_map/all_gather | solution.py:175
  9.2 235.3 %copy-start.2 = (bf16[2,256,2560]{2,1,0:T(8,128)(2,1)}, bf16[2,256,2560]{2,1,0:T(8,128)(2,1)S(1)}, u32[]{:S(2)}) copy-start(bf16[2,256,2560]{2,1,0:T(8,128)(2,1)S(1)} %pad_maximum_fusion.refs_0_) | copy-start | bytes 7864324
  9.2 110.1 %collective-permute-start = (bf16[2,256,2560]{2,1,0:T(8,128)(2,1)S(1)}, bf16[2,256,2560]{2,1,0:T(8,128)(2,1)}, u32[]{:S(2)}, u32[]{:S(2)}) collective-permute-start(bf16[2,256,2560]{2,1,0:T(8,128)(2,1)S(1)} %pad_maximum_fusion.refs_0_), channel_id=1, source_target_pairs={{0,2},{2,4},{4,6},{6,8},{8,10},{10,12},{12,14},{1,3},{3,5},{5,7},{... | collective-permute-start | bytes 7864328 | tf_op jit(solution)/shard_map/ppermute | solution.py:24
  12.4 114.7 %collective-permute-start.1 = (bf16[2,256,2560]{2,1,0:T(8,128)(2,1)S(1)}, bf16[2,256,2560]{2,1,0:T(8,128)(2,1)}, u32[]{:S(2)}, u32[]{:S(2)}) collective-permute-start(bf16[2,256,2560]{2,1,0:T(8,128)(2,1)S(1)} %pad_maximum_fusion.refs_0_), channel_id=1, source_target_pairs={{2,0},{4,2},{6,4},{8,6},{10,8},{12,10},{14,12},{3,1},{5,3},{7,5},{... | collective-permute-start | bytes 7864328 | tf_op jit(solution)/shard_map/ppermute | solution.py:24
  15.4 115.5 %collective-permute-start.4 = (bf16[2,256,2560]{2,1,0:T(8,128)(2,1)S(1)}, bf16[2,256,2560]{2,1,0:T(8,128)(2,1)}, u32[]{:S(2)}, u32[]{:S(2)}) collective-permute-start(bf16[2,256,2560]{2,1,0:T(8,128)(2,1)S(1)} %pad_maximum_fusion.refs_0_), channel_id=1, source_target_pairs={{0,4},{2,6},{4,8},{6,10},{8,12},{10,14},{1,5},{3,7},{5,9},{7,11},{... | collective-permute-start | bytes 7864328 | tf_op jit(solution)/shard_map/ppermute | solution.py:24
  18.6 218.8 %collective-permute-start.5 = (bf16[2,256,2560]{2,1,0:T(8,128)(2,1)S(1)}, bf16[2,256,2560]{2,1,0:T(8,128)(2,1)}, u32[]{:S(2)}, u32[]{:S(2)}) collective-permute-start(bf16[2,256,2560]{2,1,0:T(8,128)(2,1)S(1)} %pad_maximum_fusion.refs_0_), channel_id=1, source_target_pairs={{4,0},{6,2},{8,4},{10,6},{12,8},{14,10},{5,1},{7,3},{9,5},{11,7},{... | collective-permute-start | bytes 7864328 | tf_op jit(solution)/shard_map/ppermute | solution.py:24
  22.2 222.4 %collective-permute-start.3 = (bf16[2,256,2560]{2,1,0:T(8,128)(2,1)S(1)}, bf16[2,256,2560]{2,1,0:T(8,128)(2,1)}, u32[]{:S(2)}, u32[]{:S(2)}) collective-permute-start(bf16[2,256,2560]{2,1,0:T(8,128)(2,1)S(1)} %pad_maximum_fusion.refs_0_), channel_id=1, source_target_pairs={{0,1},{1,0},{2,3},{3,2},{4,5},{5,4},{6,7},{7,6},{8,9},{9,8},{10,11... | collective-permute-start | bytes 7864328 | tf_op jit(solution)/shard_map/ppermute | solution.py:28
  24.0 222.6 %copy-start.5 = (s32[32]{0:T(128)S(1)}, s32[32]{0:T(128)}, u32[]{:S(2)}) copy-start(s32[32]{0:T(128)} %param.11) | copy-start | bytes 388
  119.3 130.7 %collective-permute-start.6 = (bf16[2,256,2560]{2,1,0:T(8,128)(2,1)}, bf16[2,256,2560]{2,1,0:T(8,128)(2,1)}, u32[]{:S(2)}, u32[]{:S(2)}) collective-permute-start(bf16[2,256,2560]{2,1,0:T(8,128)(2,1)} %collective-permute-done.refs_2_), channel_id=1, source_target_pairs={{0,1},{1,0},{2,3},{3,2},{4,5},{5,4},{6,7},{7,6},{8,9},{9,8},{10,11... | collective-permute-start | bytes 7864328 | tf_op jit(solution)/shard_map/ppermute | solution.py:28
  127.1 122.9 %collective-permute-start.7 = (bf16[2,256,2560]{2,1,0:T(8,128)(2,1)}, bf16[2,256,2560]{2,1,0:T(8,128)(2,1)}, u32[]{:S(2)}, u32[]{:S(2)}) collective-permute-start(bf16[2,256,2560]{2,1,0:T(8,128)(2,1)} %collective-permute-done.1.refs_3_), channel_id=1, source_target_pairs={{0,1},{1,0},{2,3},{3,2},{4,5},{5,4},{6,7},{7,6},{8,9},{9,8},{10,11... | collective-permute-start | bytes 7864328 | tf_op jit(solution)/shard_map/ppermute | solution.py:28
  130.9 119.1 %collective-permute-start.8 = (bf16[2,256,2560]{2,1,0:T(8,128)(2,1)}, bf16[2,256,2560]{2,1,0:T(8,128)(2,1)}, u32[]{:S(2)}, u32[]{:S(2)}) collective-permute-start(bf16[2,256,2560]{2,1,0:T(8,128)(2,1)} %collective-permute-done.4.refs_4_), channel_id=1, source_target_pairs={{0,1},{1,0},{2,3},{3,2},{4,5},{5,4},{6,7},{7,6},{8,9},{9,8},{10,11... | collective-permute-start | bytes 7864328 | tf_op jit(solution)/shard_map/ppermute | solution.py:28
  237.4 12.6 %collective-permute-start.9 = (bf16[2,256,2560]{2,1,0:T(8,128)(2,1)}, bf16[2,256,2560]{2,1,0:T(8,128)(2,1)}, u32[]{:S(2)}, u32[]{:S(2)}) collective-permute-start(bf16[2,256,2560]{2,1,0:T(8,128)(2,1)} %collective-permute-done.5.refs_5_), channel_id=1, source_target_pairs={{0,1},{1,0},{2,3},{3,2},{4,5},{5,4},{6,7},{7,6},{8,9},{9,8},{10,11... | collective-permute-start | bytes 7864328 | tf_op jit(solution)/shard_map/ppermute | solution.py:28
  244.5 36.5 %collective-permute-start.2 = (bf16[2,256,2560]{2,1,0:T(8,128)(2,1)}, bf16[2,256,2560]{2,1,0:T(8,128)(2,1)S(1)}, u32[]{:S(2)}, u32[]{:S(2)}) collective-permute-start(bf16[2,256,2560]{2,1,0:T(8,128)(2,1)} %broadcast_select_fusion), channel_id=1, source_target_pairs={{1,4},{3,6},{4,1},{5,8},{6,3},{7,10},{8,5},{9,12},{10,7},{11,14},{... | collective-permute-start | bytes 7864328 | tf_op jit(solution)/shard_map/ppermute | solution.py:38
  281.0 1.5 copy-start.3
  297.7 4.9 %copy-start.4 = (bf16[256,2560]{1,0:T(8,128)(2,1)S(1)}, bf16[256,2560]{1,0:T(8,128)(2,1)}, u32[]{:S(2)}) copy-start(bf16[256,2560]{1,0:T(8,128)(2,1)} %shard_map.65) | copy-start | bytes 3932164
  301.4 20.9 %collective-permute-start.11 = (bf16[256,640]{1,0:T(8,128)(2,1)S(1)}, bf16[256,640]{1,0:T(8,128)(2,1)S(1)}, u32[]{:S(2)}, u32[]{:S(2)}) collective-permute-start(bf16[256,640]{1,0:T(8,128)(2,1)S(1)} %fusion.16), channel_id=1, source_target_pairs={{0,16},{16,0},{1,17},{17,1},{2,18},{18,2},{3,19},{19,3},{4,20},{20... | collective-permute-start | bytes 983048 | tf_op jit(solution)/shard_map/ppermute | solution.py:28
  305.8 16.5 %collective-permute-start.12 = (bf16[256,640]{1,0:T(8,128)(2,1)S(1)}, bf16[256,640]{1,0:T(8,128)(2,1)S(1)}, u32[]{:S(2)}, u32[]{:S(2)}) collective-permute-start(bf16[256,640]{1,0:T(8,128)(2,1)S(1)} %fusion.19), channel_id=1, source_target_pairs={{0,16},{16,0},{1,17},{17,1},{2,18},{18,2},{3,19},{19,3},{4,20},{20... | collective-permute-start | bytes 983048 | tf_op jit(solution)/shard_map/ppermute | solution.py:28
  309.3 15.9 %collective-permute-start.13 = (bf16[256,640]{1,0:T(8,128)(2,1)S(1)}, bf16[256,640]{1,0:T(8,128)(2,1)S(1)}, u32[]{:S(2)}, u32[]{:S(2)}) collective-permute-start(bf16[256,640]{1,0:T(8,128)(2,1)S(1)} %fusion.22), channel_id=1, source_target_pairs={{0,16},{16,0},{1,17},{17,1},{2,18},{18,2},{3,19},{19,3},{4,20},{20... | collective-permute-start | bytes 983048 | tf_op jit(solution)/shard_map/ppermute | solution.py:28
  313.7 17.5 %collective-permute-start.10 = (bf16[256,640]{1,0:T(8,128)(2,1)S(1)}, bf16[256,640]{1,0:T(8,128)(2,1)S(1)}, u32[]{:S(2)}, u32[]{:S(2)}) collective-permute-start(bf16[256,640]{1,0:T(8,128)(2,1)S(1)} %fusion.13), channel_id=1, source_target_pairs={{0,16},{16,0},{1,17},{17,1},{2,18},{18,2},{3,19},{19,3},{4,20},{20... | collective-permute-start | bytes 983048 | tf_op jit(solution)/shard_map/ppermute | solution.py:28
  314.0 18.6 %copy-start.1 = (s32[32,12]{0,1:T(8,128)S(1)}, s32[32,12]{0,1:T(8,128)}, u32[]{:S(2)}) copy-start(s32[32,12]{0,1:T(8,128)} %param.10) | copy-start | bytes 4612
Sparse Core Ops, SparseCore 0:
  9.0 248.2 all-gather.1

commit v11 on v10

--- a/solution.py
+++ b/solution.py
@@ -28,14 +28,11 @@
     return lax.ppermute(x, axis, [(0, 1), (1, 0)])
 
 
-def third_neighbour(x, chips):
+def third_neighbours(from_below, from_above, chips):
     peers = chips * 2
-    pairs = []
-    for s in range(peers):
-        t = s + 3 if s % 2 == 1 else s - 3
-        if 0 <= t < peers:
-            pairs.append((s, t))
-    return lax.ppermute(x, SEQ, pairs)
+    up = [(s, s + 3) for s in range(1, peers, 2) if s + 3 < peers]
+    down = [(s, s - 3) for s in range(0, peers, 2) if s - 3 >= 0]
+    return lax.ppermute(from_below, SEQ, up), lax.ppermute(from_above, SEQ, down)
 
 
 def attention_kernel(n_blocks, tiles, group, carry_in, finish, mask_ref, q_ref, *refs):
@@ -161,8 +158,8 @@
             fetched.append((-sign * 2 * chip_step, block))
             early.append((-sign * 2 * chip_step, block))
     from_below, from_above = fetched[0][1], fetched[1][1]
-    onward = jnp.where(core == 1, from_below, from_above)
-    late = [(-REACH + 2 * REACH * core, third_neighbour(onward, chips))]
+    up_three, down_three = third_neighbours(from_below, from_above, chips)
+    late = [(-REACH, up_three, core == 0), (REACH, down_three, core == 1)]
     for offset, block in fetched:
         passed = swapped(block, "core")
         early.append((offset + 1 - 2 * core, passed))
@@ -170,8 +167,9 @@
     def masks_of(blocks):
         return jnp.stack([tile_need(offset) for offset, _ in blocks]).astype(jnp.int32).reshape(-1)
 
+    late_masks = jnp.stack([tile_need(offset) & here for offset, _, here in late]).astype(jnp.int32).reshape(-1)
     carry = block_attention(queries, [b for _, b in early], masks_of(early), finish=False)
-    attended = block_attention(queries, [b for _, b in late], masks_of(late), carry=carry)
+    attended = block_attention(queries, [b for _, b, _ in late], late_masks, carry=carry)
     weight_rows = lax.all_gather(out_weight, SEQ, axis=1, tiled=True)
     heads = lax.axis_size("head")
     if heads == 2:

time: 340 us -> 336 us (0.988)
  waiting for transfers between devices: 220 us -> 225 us
    ppermute x4, waiting for transfers between devices: 206 us -> 209 us  [shifted(): return lax.ppermute(x, axis, pairs)]
    select_n x1 -> x0, other arithmetic: 3.48 us -> none  [local(): onward = jnp.where(core == 1, from_below, from_above)]
  transfers between devices with their start and end apart: 15 -> 16, of which waited for: 7 -> 7; matrix products, arithmetic and copies ran while one was open for 8% -> 7% of each run, Pallas kernels for 12% -> 11%
where the time goes in v11:
time: 336 us; the launch traced here: 335 us
  waiting for transfers between devices  225 us (67%)
  Pallas kernels  38.2 us (11%)
  starting transfers between devices  29.9 us (9%)
  matrix products  21.3 us (6%)
  between operations  13.6 us (4%)
  other arithmetic  4.07 us (1%)
    ppermute x4, waiting for transfers between devices, shifted(): return lax.ppermute(x, axis, pairs)  209 us
    pallas_call x2, Pallas kernels, block_attention(): pl.pallas_call(functools.partial(attention_kernel, n_blocks, tiles, group...  38.2 us
    ppermute x9, starting transfers between devices, swapped(): return lax.ppermute(x, axis, [(0, 1), (1, 0)])  14.4 us
    dot_general x4, matrix products, local(): jnp.dot(attended, theirs[:, cols], preferred_element_type=jnp.float32)  13 us
    ppermute x4, starting transfers between devices, shifted(): return lax.ppermute(x, axis, pairs)  11.5 us
    ppermute x9, waiting for transfers between devices, swapped(): return lax.ppermute(x, axis, [(0, 1), (1, 0)])  10.6 us
    dot_general x1, matrix products, local(): jnp.dot(attended, mine, preferred_element_type=jnp.float32)  8.31 us
  transfers between devices with their start and end apart: 16, of which 7 were waited for; matrix products, arithmetic and copies ran while one was open for 7% of the time, Pallas kernels for 11%

profile of v11, /device:TPU:9, one launch (start us, length us, event | category | flops | bytes accessed | tf_op | source)
XLA Modules:
  0.0 335.2 jit_solution(3296427740839343347)
XLA Ops:
  6.5 0.7 all-gather.2.cloned.1.call-update
  7.3 2.0 pad_maximum_fusion.refs_0_
  9.2 3.1 collective-permute-start
  12.4 3.0 collective-permute-start.2
  15.4 1.9 collective-permute-start.6
  17.4 3.4 %collective-permute-start.5 = (bf16[2,256,2560]{2,1,0:T(8,128)(2,1)S(1)}, bf16[2,256,2560]{2,1,0:T(8,128)(2,1)}, u32[]{:S(2)}, u32[]{:S(2)}) collective-permute-start(bf16[2,256,2560]{2,1,0:T(8,128)(2,1)S(1)} %pad_maximum_fusion.refs_0_), channel_id=1, source_target_pairs={{0,4},{2,6},{4,8},{6,10},{8,12},{10,14},{1,5},{3,7},{5,9},{7,11},{... | collective-permute-start | bytes 7864328 | tf_op jit(solution)/shard_map/ppermute | solution.py:24
  20.7 1.9 collective-permute-start.4
  22.6 96.7 %collective-permute-done.refs_2_ = bf16[2,256,2560]{2,1,0:T(8,128)(2,1)} collective-permute-done((bf16[2,256,2560]{2,1,0:T(8,128)(2,1)S(1)}, bf16[2,256,2560]{2,1,0:T(8,128)(2,1)}, u32[]{:S(2)}, u32[]{:S(2)}) %collective-permute-start) | collective-permute-done | bytes 2621472 | tf_op jit(solution)/shard_map/ppermute | solution.py:24
  119.3 3.0 collective-permute-start.7
  122.3 4.8 %collective-permute-done.2.refs_3_ = bf16[2,256,2560]{2,1,0:T(8,128)(2,1)} collective-permute-done((bf16[2,256,2560]{2,1,0:T(8,128)(2,1)S(1)}, bf16[2,256,2560]{2,1,0:T(8,128)(2,1)}, u32[]{:S(2)}, u32[]{:S(2)}) %collective-permute-start.2) | collective-permute-done | bytes 2621472 | tf_op jit(solution)/shard_map/ppermute | solution.py:24
  127.1 2.7 collective-permute-start.8
  129.8 107.7 %collective-permute-done.6.refs_5_ = bf16[2,256,2560]{2,1,0:T(8,128)(2,1)} collective-permute-done((bf16[2,256,2560]{2,1,0:T(8,128)(2,1)S(1)}, bf16[2,256,2560]{2,1,0:T(8,128)(2,1)}, u32[]{:S(2)}, u32[]{:S(2)}) %collective-permute-start.6) | collective-permute-done | bytes 2621472 | tf_op jit(solution)/shard_map/ppermute | solution.py:24
  237.5 3.6 %collective-permute-start.10 = (bf16[2,256,2560]{2,1,0:T(8,128)(2,1)}, bf16[2,256,2560]{2,1,0:T(8,128)(2,1)}, u32[]{:S(2)}, u32[]{:S(2)}) collective-permute-start(bf16[2,256,2560]{2,1,0:T(8,128)(2,1)} %collective-permute-done.6.refs_5_), channel_id=1, source_target_pairs={{0,1},{1,0},{2,3},{3,2},{4,5},{5,4},{6,7},{7,6},{8,9},{9,8},{10,11... | collective-permute-start | bytes 7864328 | tf_op jit(solution)/shard_map/ppermute | solution.py:28
  241.1 0.1 constant_dynamic-slice_fusion
  241.2 0.1 copy.21
  241.3 2.8 collective-permute-start.1
  244.1 1.3 collective-permute-start.3
  245.6 0.6 and_reduce_fusion
  246.2 0.1 copy.22
  246.3 0.1 copy.23
  246.4 0.1 copy.24
  246.5 0.1 copy.25
  246.6 0.1 copy.26
  246.7 0.1 copy.27
  246.9 0.1 copy.28
  247.0 0.1 copy.29
  247.1 0.1 copy.30
  247.2 0.1 copy.31
  247.3 0.1 stack.61
  247.4 0.1 copy.32
  247.5 0.6 reshape.97.mask_ref
  248.2 0.7 reshape.96.mask_ref
  248.8 1.4 collective-permute-done.9.refs_8_
  250.3 26.3 %shard_map.64 = (f32[256,2560]{1,0:T(8,128)}, f32[256,2560]{1,0:T(8,128)}, f32[256,2560]{1,0:T(8,128)}) custom-call(s32[40]{0:T(128)} %reshape.97.mask_ref, bf16[256,2560]{1,0:T(8,128)(2,1)} %q_ref.3, bf16[2,256,2560]{2,1,0:T(8,128)(2,1)} %copy-done.2, bf16[2,256,2560]{2,1,0:T(8,128)(2,1)} %collective-permute-done.4.refs_1_, ...), custom_call_target="tpu_custom_call" | custom-call | flops 6710886400 | bytes 44564480 | tf_op jit(solution)/shard_map/pallas_call | solution.py:123
  276.6 4.6 %collective-permute-done.3.refs_1_ = bf16[2,256,2560]{2,1,0:T(8,128)(2,1)} collective-permute-done((bf16[2,256,2560]{2,1,0:T(8,128)(2,1)}, bf16[2,256,2560]{2,1,0:T(8,128)(2,1)}, u32[]{:S(2)}, u32[]{:S(2)}) %collective-permute-start.3) | collective-permute-done | bytes 2621472 | tf_op jit(solution)/shard_map/ppermute | solution.py:35
  281.1 12.0 %shard_map.65 = bf16[256,2560]{1,0:T(8,128)(2,1)} custom-call(s32[8]{0:T(128)} %reshape.96.mask_ref, bf16[256,2560]{1,0:T(8,128)(2,1)} %q_ref.3, bf16[2,256,2560]{2,1,0:T(8,128)(2,1)} %collective-permute-done.1.refs_0_, bf16[2,256,2560]{2,1,0:T(8,128)(2,1)} %collective-permute-done.3.refs_1_, f32[256,2560]{1,0:T(8,128)} %get-tuple-element.8.refs_2_, ...), custom_call_target="tpu_custom_call" | custom-call | flops 1342177280 | bytes 23592960 | tf_op jit(solution)/shard_map/pallas_call | solution.py:123
  293.1 3.6 %fusion.16 = bf16[256,640]{1,0:T(8,128)(2,1)S(1)} fusion(bf16[256,2560]{1,0:T(8,128)(2,1)} %shard_map.65, bf16[2560,5120]{0,1:T(8,128)(2,1)} %all-gather.2.cloned.1.call-done, s32[]{:T(128)S(6)} %add.210), kind=kOutput, calls=%fused_computation.14 | convolution fusion | flops 839024640 | bytes 4915204 | tf_op jit(solution)/shard_map/dot_general | solution.py:185
  296.8 1.3 collective-permute-start.12
  298.1 3.1 fusion.19
  301.2 0.3 collective-permute-start.13
  301.5 3.1 fusion.22
  304.7 1.3 collective-permute-start.14
  306.0 3.1 fusion.13
  309.1 0.3 collective-permute-start.11
  309.4 8.3 %fusion.2 = bf16[256,2560]{1,0:T(8,128)(2,1)S(1)} fusion(bf16[256,2560]{1,0:T(8,128)(2,1)S(1)} %copy-done.3, bf16[2560,5120]{0,1:T(8,128)(2,1)} %all-gather.2.cloned.1.call-done, s32[]{:T(128)S(6)} %select_n.11), kind=kOutput, calls=%fused_computation.2 | convolution fusion | flops 3356098560 | bytes 15728644 | tf_op jit(solution)/shard_map/dot_general | solution.py:187
  317.7 2.8 collective-permute-done.14
  320.5 6.4 %collective-permute-done.11 = bf16[256,640]{1,0:T(8,128)(2,1)S(1)} collective-permute-done((bf16[256,640]{1,0:T(8,128)(2,1)S(1)}, bf16[256,640]{1,0:T(8,128)(2,1)S(1)}, u32[]{:S(2)}, u32[]{:S(2)}) %collective-permute-start.11) | collective-permute-done | bytes 327712 | tf_op jit(solution)/shard_map/ppermute | solution.py:28
  326.9 1.4 add_convert_fusion
  (38 shorter events, 0.3 us)
Async XLA Ops:
  6.5 234.5 %copy-start = (s32[32,12]{0,1:T(8,128)S(1)}, s32[32,12]{0,1:T(8,128)}, u32[]{:S(2)}) copy-start(s32[32,12]{0,1:T(8,128)} %param.10) | copy-start | bytes 4612
  6.5 286.6 %all-gather.2.cloned.1.call-start = ((), (), s32[]{:S(2)}) async-start(), calls=%async_computation | async-start | bytes 27852800 | tf_op jit(solution)/shard_map/all_gather | solution.py:173
  7.3 234.0 %copy-start.4 = (s32[32]{0:T(128)S(1)}, s32[32]{0:T(128)}, u32[]{:S(2)}) copy-start(s32[32]{0:T(128)} %param.11) | copy-start | bytes 388
  9.2 241.1 %copy-start.2 = (bf16[2,256,2560]{2,1,0:T(8,128)(2,1)}, bf16[2,256,2560]{2,1,0:T(8,128)(2,1)S(1)}, u32[]{:S(2)}) copy-start(bf16[2,256,2560]{2,1,0:T(8,128)(2,1)S(1)} %pad_maximum_fusion.refs_0_) | copy-start | bytes 7864324
  9.2 110.1 %collective-permute-start = (bf16[2,256,2560]{2,1,0:T(8,128)(2,1)S(1)}, bf16[2,256,2560]{2,1,0:T(8,128)(2,1)}, u32[]{:S(2)}, u32[]{:S(2)}) collective-permute-start(bf16[2,256,2560]{2,1,0:T(8,128)(2,1)S(1)} %pad_maximum_fusion.refs_0_), channel_id=1, source_target_pairs={{0,2},{2,4},{4,6},{6,8},{8,10},{10,12},{12,14},{1,3},{3,5},{5,7},{... | collective-permute-start | bytes 7864328 | tf_op jit(solution)/shard_map/ppermute | solution.py:24
  12.4 114.7 %collective-permute-start.2 = (bf16[2,256,2560]{2,1,0:T(8,128)(2,1)S(1)}, bf16[2,256,2560]{2,1,0:T(8,128)(2,1)}, u32[]{:S(2)}, u32[]{:S(2)}) collective-permute-start(bf16[2,256,2560]{2,1,0:T(8,128)(2,1)S(1)} %pad_maximum_fusion.refs_0_), channel_id=1, source_target_pairs={{2,0},{4,2},{6,4},{8,6},{10,8},{12,10},{14,12},{3,1},{5,3},{7,5},{... | collective-permute-start | bytes 7864328 | tf_op jit(solution)/shard_map/ppermute | solution.py:24
  15.4 222.0 %collective-permute-start.6 = (bf16[2,256,2560]{2,1,0:T(8,128)(2,1)S(1)}, bf16[2,256,2560]{2,1,0:T(8,128)(2,1)}, u32[]{:S(2)}, u32[]{:S(2)}) collective-permute-start(bf16[2,256,2560]{2,1,0:T(8,128)(2,1)S(1)} %pad_maximum_fusion.refs_0_), channel_id=1, source_target_pairs={{4,0},{6,2},{8,4},{10,6},{12,8},{14,10},{5,1},{7,3},{9,5},{11,7},{... | collective-permute-start | bytes 7864328 | tf_op jit(solution)/shard_map/ppermute | solution.py:24
  17.4 223.7 %collective-permute-start.5 = (bf16[2,256,2560]{2,1,0:T(8,128)(2,1)S(1)}, bf16[2,256,2560]{2,1,0:T(8,128)(2,1)}, u32[]{:S(2)}, u32[]{:S(2)}) collective-permute-start(bf16[2,256,2560]{2,1,0:T(8,128)(2,1)S(1)} %pad_maximum_fusion.refs_0_), channel_id=1, source_target_pairs={{0,4},{2,6},{4,8},{6,10},{8,12},{10,14},{1,5},{3,7},{5,9},{7,11},{... | collective-permute-start | bytes 7864328 | tf_op jit(solution)/shard_map/ppermute | solution.py:24
  20.7 220.6 %collective-permute-start.4 = (bf16[2,256,2560]{2,1,0:T(8,128)(2,1)S(1)}, bf16[2,256,2560]{2,1,0:T(8,128)(2,1)}, u32[]{:S(2)}, u32[]{:S(2)}) collective-permute-start(bf16[2,256,2560]{2,1,0:T(8,128)(2,1)S(1)} %pad_maximum_fusion.refs_0_), channel_id=1, source_target_pairs={{0,1},{1,0},{2,3},{3,2},{4,5},{5,4},{6,7},{7,6},{8,9},{9,8},{10,11... | collective-permute-start | bytes 7864328 | tf_op jit(solution)/shard_map/ppermute | solution.py:28
  119.3 124.8 %collective-permute-start.7 = (bf16[2,256,2560]{2,1,0:T(8,128)(2,1)}, bf16[2,256,2560]{2,1,0:T(8,128)(2,1)}, u32[]{:S(2)}, u32[]{:S(2)}) collective-permute-start(bf16[2,256,2560]{2,1,0:T(8,128)(2,1)} %collective-permute-done.refs_2_), channel_id=1, source_target_pairs={{0,1},{1,0},{2,3},{3,2},{4,5},{5,4},{6,7},{7,6},{8,9},{9,8},{10,11... | collective-permute-start | bytes 7864328 | tf_op jit(solution)/shard_map/ppermute | solution.py:28
  127.1 121.7 %collective-permute-start.8 = (bf16[2,256,2560]{2,1,0:T(8,128)(2,1)}, bf16[2,256,2560]{2,1,0:T(8,128)(2,1)}, u32[]{:S(2)}, u32[]{:S(2)}) collective-permute-start(bf16[2,256,2560]{2,1,0:T(8,128)(2,1)} %collective-permute-done.2.refs_3_), channel_id=1, source_target_pairs={{0,1},{1,0},{2,3},{3,2},{4,5},{5,4},{6,7},{7,6},{8,9},{9,8},{10,11... | collective-permute-start | bytes 7864328 | tf_op jit(solution)/shard_map/ppermute | solution.py:28
  237.5 11.4 %collective-permute-start.10 = (bf16[2,256,2560]{2,1,0:T(8,128)(2,1)}, bf16[2,256,2560]{2,1,0:T(8,128)(2,1)}, u32[]{:S(2)}, u32[]{:S(2)}) collective-permute-start(bf16[2,256,2560]{2,1,0:T(8,128)(2,1)} %collective-permute-done.6.refs_5_), channel_id=1, source_target_pairs={{0,1},{1,0},{2,3},{3,2},{4,5},{5,4},{6,7},{7,6},{8,9},{9,8},{10,11... | collective-permute-start | bytes 7864328 | tf_op jit(solution)/shard_map/ppermute | solution.py:28
  241.1 9.2 %collective-permute-start.9 = (bf16[2,256,2560]{2,1,0:T(8,128)(2,1)}, bf16[2,256,2560]{2,1,0:T(8,128)(2,1)}, u32[]{:S(2)}, u32[]{:S(2)}) collective-permute-start(bf16[2,256,2560]{2,1,0:T(8,128)(2,1)} %collective-permute-done.5.refs_4_), channel_id=1, source_target_pairs={{0,1},{1,0},{2,3},{3,2},{4,5},{5,4},{6,7},{7,6},{8,9},{9,8},{10,11... | collective-permute-start | bytes 7864328 | tf_op jit(solution)/shard_map/ppermute | solution.py:28
  241.3 35.2 %collective-permute-start.1 = (bf16[2,256,2560]{2,1,0:T(8,128)(2,1)}, bf16[2,256,2560]{2,1,0:T(8,128)(2,1)}, u32[]{:S(2)}, u32[]{:S(2)}) collective-permute-start(bf16[2,256,2560]{2,1,0:T(8,128)(2,1)} %collective-permute-done.refs_2_), channel_id=1, source_target_pairs={{1,4},{3,6},{5,8},{7,10},{9,12},{11,14},{17,20},{19,22},{21,24},{2... | collective-permute-start | bytes 7864328 | tf_op jit(solution)/shard_map/ppermute | solution.py:35
  244.1 37.0 %collective-permute-start.3 = (bf16[2,256,2560]{2,1,0:T(8,128)(2,1)}, bf16[2,256,2560]{2,1,0:T(8,128)(2,1)}, u32[]{:S(2)}, u32[]{:S(2)}) collective-permute-start(bf16[2,256,2560]{2,1,0:T(8,128)(2,1)} %collective-permute-done.2.refs_3_), channel_id=1, source_target_pairs={{4,1},{6,3},{8,5},{10,7},{12,9},{14,11},{20,17},{22,19},{24,21},{2... | collective-permute-start | bytes 7864328 | tf_op jit(solution)/shard_map/ppermute | solution.py:35
  293.1 5.0 %copy-start.3 = (bf16[256,2560]{1,0:T(8,128)(2,1)S(1)}, bf16[256,2560]{1,0:T(8,128)(2,1)}, u32[]{:S(2)}) copy-start(bf16[256,2560]{1,0:T(8,128)(2,1)} %shard_map.65) | copy-start | bytes 3932164
  296.8 20.9 %collective-permute-start.12 = (bf16[256,640]{1,0:T(8,128)(2,1)S(1)}, bf16[256,640]{1,0:T(8,128)(2,1)S(1)}, u32[]{:S(2)}, u32[]{:S(2)}) collective-permute-start(bf16[256,640]{1,0:T(8,128)(2,1)S(1)} %fusion.16), channel_id=1, source_target_pairs={{0,16},{16,0},{1,17},{17,1},{2,18},{18,2},{3,19},{19,3},{4,20},{20... | collective-permute-start | bytes 983048 | tf_op jit(solution)/shard_map/ppermute | solution.py:28
  301.2 16.5 %collective-permute-start.13 = (bf16[256,640]{1,0:T(8,128)(2,1)S(1)}, bf16[256,640]{1,0:T(8,128)(2,1)S(1)}, u32[]{:S(2)}, u32[]{:S(2)}) collective-permute-start(bf16[256,640]{1,0:T(8,128)(2,1)S(1)} %fusion.19), channel_id=1, source_target_pairs={{0,16},{16,0},{1,17},{17,1},{2,18},{18,2},{3,19},{19,3},{4,20},{20... | collective-permute-start | bytes 983048 | tf_op jit(solution)/shard_map/ppermute | solution.py:28
  304.7 15.9 %collective-permute-start.14 = (bf16[256,640]{1,0:T(8,128)(2,1)S(1)}, bf16[256,640]{1,0:T(8,128)(2,1)S(1)}, u32[]{:S(2)}, u32[]{:S(2)}) collective-permute-start(bf16[256,640]{1,0:T(8,128)(2,1)S(1)} %fusion.22), channel_id=1, source_target_pairs={{0,16},{16,0},{1,17},{17,1},{2,18},{18,2},{3,19},{19,3},{4,20},{20... | collective-permute-start | bytes 983048 | tf_op jit(solution)/shard_map/ppermute | solution.py:28
  309.1 17.8 %collective-permute-start.11 = (bf16[256,640]{1,0:T(8,128)(2,1)S(1)}, bf16[256,640]{1,0:T(8,128)(2,1)S(1)}, u32[]{:S(2)}, u32[]{:S(2)}) collective-permute-start(bf16[256,640]{1,0:T(8,128)(2,1)S(1)} %fusion.13), channel_id=1, source_target_pairs={{0,16},{16,0},{1,17},{17,1},{2,18},{18,2},{3,19},{19,3},{4,20},{20... | collective-permute-start | bytes 983048 | tf_op jit(solution)/shard_map/ppermute | solution.py:28
  309.4 18.9 %copy-start.1 = (s32[32,12]{0,1:T(8,128)S(1)}, s32[32,12]{0,1:T(8,128)}, u32[]{:S(2)}) copy-start(s32[32,12]{0,1:T(8,128)} %param.10) | copy-start | bytes 4612
Sparse Core Ops, SparseCore 0:
  9.0 248.5 all-gather.1

commit v12 on v11

--- a/solution.py
+++ b/solution.py
@@ -56,7 +56,7 @@
             keys = kv_refs[b][0, :, cols]
             scores = lax.dot_general(
                 query, keys, (((1,), (1,)), ((), ())), preferred_element_type=jnp.float32
-            ) * (1.0 / math.sqrt(HD))
+            )
             for qi in range(tiles):
                 for kt in range(tiles):
                     flag = mask_ref[(b * tiles + qi) * tiles + kt]
@@ -70,8 +70,9 @@
         if carry_in:
             old_peak = peak_in[:, g * HD:g * HD + 1]
             peak = jnp.maximum(peak, old_peak)
-            carried = jnp.exp(old_peak - peak)
-        weights = jnp.exp(scores - peak)
+            carried = jnp.exp((old_peak - peak) * (1.0 / math.sqrt(HD)))
+        scale = 1.0 / math.sqrt(HD)
+        weights = jnp.exp(scores * scale - peak * scale)
         totals = jnp.sum(weights, axis=1, keepdims=True)
         rounded = weights.astype(jnp.bfloat16)
         summed = jnp.zeros((rows, HD), jnp.float32)

time: 336 us -> 337 us (level)
  transfers between devices with their start and end apart: 16 -> 16, of which waited for: 7 -> 7; matrix products, arithmetic and copies ran while one was open for 7% -> 7% of each run, Pallas kernels for 11% -> 12%
where the time goes in v12:
time: 337 us; the launch traced here: 335 us
  waiting for transfers between devices  224 us (66%)
  Pallas kernels  39.7 us (12%)
  starting transfers between devices  29.9 us (9%)
  matrix products  21.3 us (6%)
  between operations  13.6 us (4%)
  other arithmetic  4.07 us (1%)
    ppermute x4, waiting for transfers between devices, shifted(): return lax.ppermute(x, axis, pairs)  209 us
    pallas_call x2, Pallas kernels, block_attention(): pl.pallas_call(functools.partial(attention_kernel, n_blocks, tiles, group...  39.7 us
    ppermute x9, starting transfers between devices, swapped(): return lax.ppermute(x, axis, [(0, 1), (1, 0)])  14.4 us
    dot_general x4, matrix products, local(): jnp.dot(attended, theirs[:, cols], preferred_element_type=jnp.float32)  13 us
    ppermute x4, starting transfers between devices, shifted(): return lax.ppermute(x, axis, pairs)  11.5 us
    ppermute x9, waiting for transfers between devices, swapped(): return lax.ppermute(x, axis, [(0, 1), (1, 0)])  10.5 us
    dot_general x1, matrix products, local(): jnp.dot(attended, mine, preferred_element_type=jnp.float32)  8.31 us
  transfers between devices with their start and end apart: 16, of which 7 were waited for; matrix products, arithmetic and copies ran while one was open for 7% of the time, Pallas kernels for 12%

profile of v12, /device:TPU:9, one launch (start us, length us, event | category | flops | bytes accessed | tf_op | source)
XLA Modules:
  0.0 335.2 jit_solution(1221080879119675648)
XLA Ops:
  6.5 0.7 all-gather.2.cloned.1.call-update
  7.3 2.0 pad_maximum_fusion.refs_0_
  9.2 3.1 collective-permute-start
  12.4 3.0 collective-permute-start.2
  15.4 1.9 collective-permute-start.6
  17.4 3.4 %collective-permute-start.5 = (bf16[2,256,2560]{2,1,0:T(8,128)(2,1)S(1)}, bf16[2,256,2560]{2,1,0:T(8,128)(2,1)}, u32[]{:S(2)}, u32[]{:S(2)}) collective-permute-start(bf16[2,256,2560]{2,1,0:T(8,128)(2,1)S(1)} %pad_maximum_fusion.refs_0_), channel_id=1, source_target_pairs={{0,4},{2,6},{4,8},{6,10},{8,12},{10,14},{1,5},{3,7},{5,9},{7,11},{... | collective-permute-start | bytes 7864328 | tf_op jit(solution)/shard_map/ppermute | solution.py:24
  20.7 1.9 collective-permute-start.4
  22.6 96.7 %collective-permute-done.refs_2_ = bf16[2,256,2560]{2,1,0:T(8,128)(2,1)} collective-permute-done((bf16[2,256,2560]{2,1,0:T(8,128)(2,1)S(1)}, bf16[2,256,2560]{2,1,0:T(8,128)(2,1)}, u32[]{:S(2)}, u32[]{:S(2)}) %collective-permute-start) | collective-permute-done | bytes 2621472 | tf_op jit(solution)/shard_map/ppermute | solution.py:24
  119.3 3.0 collective-permute-start.7
  122.3 4.8 %collective-permute-done.2.refs_3_ = bf16[2,256,2560]{2,1,0:T(8,128)(2,1)} collective-permute-done((bf16[2,256,2560]{2,1,0:T(8,128)(2,1)S(1)}, bf16[2,256,2560]{2,1,0:T(8,128)(2,1)}, u32[]{:S(2)}, u32[]{:S(2)}) %collective-permute-start.2) | collective-permute-done | bytes 2621472 | tf_op jit(solution)/shard_map/ppermute | solution.py:24
  127.1 2.7 collective-permute-start.8
  129.8 107.7 %collective-permute-done.6.refs_5_ = bf16[2,256,2560]{2,1,0:T(8,128)(2,1)} collective-permute-done((bf16[2,256,2560]{2,1,0:T(8,128)(2,1)S(1)}, bf16[2,256,2560]{2,1,0:T(8,128)(2,1)}, u32[]{:S(2)}, u32[]{:S(2)}) %collective-permute-start.6) | collective-permute-done | bytes 2621472 | tf_op jit(solution)/shard_map/ppermute | solution.py:24
  237.5 3.6 %collective-permute-start.10 = (bf16[2,256,2560]{2,1,0:T(8,128)(2,1)}, bf16[2,256,2560]{2,1,0:T(8,128)(2,1)}, u32[]{:S(2)}, u32[]{:S(2)}) collective-permute-start(bf16[2,256,2560]{2,1,0:T(8,128)(2,1)} %collective-permute-done.6.refs_5_), channel_id=1, source_target_pairs={{0,1},{1,0},{2,3},{3,2},{4,5},{5,4},{6,7},{7,6},{8,9},{9,8},{10,11... | collective-permute-start | bytes 7864328 | tf_op jit(solution)/shard_map/ppermute | solution.py:28
  241.1 0.1 constant_dynamic-slice_fusion
  241.2 0.1 copy.21
  241.3 2.8 collective-permute-start.1
  244.1 1.3 collective-permute-start.3
  245.6 0.6 and_reduce_fusion
  246.2 0.1 copy.22
  246.3 0.1 copy.23
  246.4 0.1 copy.24
  246.5 0.1 copy.25
  246.6 0.1 copy.26
  246.7 0.1 copy.27
  246.9 0.1 copy.28
  247.0 0.1 copy.29
  247.1 0.1 copy.30
  247.2 0.1 copy.31
  247.3 0.1 stack.61
  247.4 0.1 copy.32
  247.5 0.6 reshape.97.mask_ref
  248.2 0.7 reshape.96.mask_ref
  248.8 1.4 collective-permute-done.9.refs_8_
  250.3 27.6 %shard_map.64 = (f32[256,2560]{1,0:T(8,128)}, f32[256,2560]{1,0:T(8,128)}, f32[256,2560]{1,0:T(8,128)}) custom-call(s32[40]{0:T(128)} %reshape.97.mask_ref, bf16[256,2560]{1,0:T(8,128)(2,1)} %q_ref.3, bf16[2,256,2560]{2,1,0:T(8,128)(2,1)} %copy-done.2, bf16[2,256,2560]{2,1,0:T(8,128)(2,1)} %collective-permute-done.4.refs_1_, ...), custom_call_target="tpu_custom_call" | custom-call | flops 6710886400 | bytes 44564480 | tf_op jit(solution)/shard_map/pallas_call | solution.py:124
  277.9 3.2 collective-permute-done.3.refs_1_
  281.1 12.1 %shard_map.65 = bf16[256,2560]{1,0:T(8,128)(2,1)} custom-call(s32[8]{0:T(128)} %reshape.96.mask_ref, bf16[256,2560]{1,0:T(8,128)(2,1)} %q_ref.3, bf16[2,256,2560]{2,1,0:T(8,128)(2,1)} %collective-permute-done.1.refs_0_, bf16[2,256,2560]{2,1,0:T(8,128)(2,1)} %collective-permute-done.3.refs_1_, f32[256,2560]{1,0:T(8,128)} %get-tuple-element.8.refs_2_, ...), custom_call_target="tpu_custom_call" | custom-call | flops 1342177280 | bytes 23592960 | tf_op jit(solution)/shard_map/pallas_call | solution.py:124
  293.3 3.6 %fusion.16 = bf16[256,640]{1,0:T(8,128)(2,1)S(1)} fusion(bf16[256,2560]{1,0:T(8,128)(2,1)} %shard_map.65, bf16[2560,5120]{0,1:T(8,128)(2,1)} %all-gather.2.cloned.1.call-done, s32[]{:T(128)S(6)} %add.210), kind=kOutput, calls=%fused_computation.14 | convolution fusion | flops 839024640 | bytes 4915204 | tf_op jit(solution)/shard_map/dot_general | solution.py:186
  296.9 1.3 collective-permute-start.12
  298.2 3.1 fusion.19
  301.4 0.3 collective-permute-start.13
  301.7 3.1 fusion.22
  304.8 1.3 collective-permute-start.14
  306.1 3.1 fusion.13
  309.2 0.3 collective-permute-start.11
  309.6 8.3 %fusion.2 = bf16[256,2560]{1,0:T(8,128)(2,1)S(1)} fusion(bf16[256,2560]{1,0:T(8,128)(2,1)S(1)} %copy-done.3, bf16[2560,5120]{0,1:T(8,128)(2,1)} %all-gather.2.cloned.1.call-done, s32[]{:T(128)S(6)} %select_n.11), kind=kOutput, calls=%fused_computation.2 | convolution fusion | flops 3356098560 | bytes 15728644 | tf_op jit(solution)/shard_map/dot_general | solution.py:188
  317.9 2.0 collective-permute-done.14
  319.9 7.0 %collective-permute-done.11 = bf16[256,640]{1,0:T(8,128)(2,1)S(1)} collective-permute-done((bf16[256,640]{1,0:T(8,128)(2,1)S(1)}, bf16[256,640]{1,0:T(8,128)(2,1)S(1)}, u32[]{:S(2)}, u32[]{:S(2)}) %collective-permute-start.11) | collective-permute-done | bytes 327712 | tf_op jit(solution)/shard_map/ppermute | solution.py:28
  326.9 1.4 add_convert_fusion
  (38 shorter events, 0.3 us)
Async XLA Ops:
  6.5 234.5 %copy-start = (s32[32,12]{0,1:T(8,128)S(1)}, s32[32,12]{0,1:T(8,128)}, u32[]{:S(2)}) copy-start(s32[32,12]{0,1:T(8,128)} %param.10) | copy-start | bytes 4612
  6.5 286.7 %all-gather.2.cloned.1.call-start = ((), (), s32[]{:S(2)}) async-start(), calls=%async_computation | async-start | bytes 27852800 | tf_op jit(solution)/shard_map/all_gather | solution.py:174
  7.3 234.0 %copy-start.4 = (s32[32]{0:T(128)S(1)}, s32[32]{0:T(128)}, u32[]{:S(2)}) copy-start(s32[32]{0:T(128)} %param.11) | copy-start | bytes 388
  9.2 241.1 %copy-start.2 = (bf16[2,256,2560]{2,1,0:T(8,128)(2,1)}, bf16[2,256,2560]{2,1,0:T(8,128)(2,1)S(1)}, u32[]{:S(2)}) copy-start(bf16[2,256,2560]{2,1,0:T(8,128)(2,1)S(1)} %pad_maximum_fusion.refs_0_) | copy-start | bytes 7864324
  9.2 110.1 %collective-permute-start = (bf16[2,256,2560]{2,1,0:T(8,128)(2,1)S(1)}, bf16[2,256,2560]{2,1,0:T(8,128)(2,1)}, u32[]{:S(2)}, u32[]{:S(2)}) collective-permute-start(bf16[2,256,2560]{2,1,0:T(8,128)(2,1)S(1)} %pad_maximum_fusion.refs_0_), channel_id=1, source_target_pairs={{0,2},{2,4},{4,6},{6,8},{8,10},{10,12},{12,14},{1,3},{3,5},{5,7},{... | collective-permute-start | bytes 7864328 | tf_op jit(solution)/shard_map/ppermute | solution.py:24
  12.4 114.7 %collective-permute-start.2 = (bf16[2,256,2560]{2,1,0:T(8,128)(2,1)S(1)}, bf16[2,256,2560]{2,1,0:T(8,128)(2,1)}, u32[]{:S(2)}, u32[]{:S(2)}) collective-permute-start(bf16[2,256,2560]{2,1,0:T(8,128)(2,1)S(1)} %pad_maximum_fusion.refs_0_), channel_id=1, source_target_pairs={{2,0},{4,2},{6,4},{8,6},{10,8},{12,10},{14,12},{3,1},{5,3},{7,5},{... | collective-permute-start | bytes 7864328 | tf_op jit(solution)/shard_map/ppermute | solution.py:24
  15.4 222.0 %collective-permute-start.6 = (bf16[2,256,2560]{2,1,0:T(8,128)(2,1)S(1)}, bf16[2,256,2560]{2,1,0:T(8,128)(2,1)}, u32[]{:S(2)}, u32[]{:S(2)}) collective-permute-start(bf16[2,256,2560]{2,1,0:T(8,128)(2,1)S(1)} %pad_maximum_fusion.refs_0_), channel_id=1, source_target_pairs={{4,0},{6,2},{8,4},{10,6},{12,8},{14,10},{5,1},{7,3},{9,5},{11,7},{... | collective-permute-start | bytes 7864328 | tf_op jit(solution)/shard_map/ppermute | solution.py:24
  17.4 223.7 %collective-permute-start.5 = (bf16[2,256,2560]{2,1,0:T(8,128)(2,1)S(1)}, bf16[2,256,2560]{2,1,0:T(8,128)(2,1)}, u32[]{:S(2)}, u32[]{:S(2)}) collective-permute-start(bf16[2,256,2560]{2,1,0:T(8,128)(2,1)S(1)} %pad_maximum_fusion.refs_0_), channel_id=1, source_target_pairs={{0,4},{2,6},{4,8},{6,10},{8,12},{10,14},{1,5},{3,7},{5,9},{7,11},{... | collective-permute-start | bytes 7864328 | tf_op jit(solution)/shard_map/ppermute | solution.py:24
  20.7 220.6 %collective-permute-start.4 = (bf16[2,256,2560]{2,1,0:T(8,128)(2,1)S(1)}, bf16[2,256,2560]{2,1,0:T(8,128)(2,1)}, u32[]{:S(2)}, u32[]{:S(2)}) collective-permute-start(bf16[2,256,2560]{2,1,0:T(8,128)(2,1)S(1)} %pad_maximum_fusion.refs_0_), channel_id=1, source_target_pairs={{0,1},{1,0},{2,3},{3,2},{4,5},{5,4},{6,7},{7,6},{8,9},{9,8},{10,11... | collective-permute-start | bytes 7864328 | tf_op jit(solution)/shard_map/ppermute | solution.py:28
  119.3 124.8 %collective-permute-start.7 = (bf16[2,256,2560]{2,1,0:T(8,128)(2,1)}, bf16[2,256,2560]{2,1,0:T(8,128)(2,1)}, u32[]{:S(2)}, u32[]{:S(2)}) collective-permute-start(bf16[2,256,2560]{2,1,0:T(8,128)(2,1)} %collective-permute-done.refs_2_), channel_id=1, source_target_pairs={{0,1},{1,0},{2,3},{3,2},{4,5},{5,4},{6,7},{7,6},{8,9},{9,8},{10,11... | collective-permute-start | bytes 7864328 | tf_op jit(solution)/shard_map/ppermute | solution.py:28
  127.1 121.7 %collective-permute-start.8 = (bf16[2,256,2560]{2,1,0:T(8,128)(2,1)}, bf16[2,256,2560]{2,1,0:T(8,128)(2,1)}, u32[]{:S(2)}, u32[]{:S(2)}) collective-permute-start(bf16[2,256,2560]{2,1,0:T(8,128)(2,1)} %collective-permute-done.2.refs_3_), channel_id=1, source_target_pairs={{0,1},{1,0},{2,3},{3,2},{4,5},{5,4},{6,7},{7,6},{8,9},{9,8},{10,11... | collective-permute-start | bytes 7864328 | tf_op jit(solution)/shard_map/ppermute | solution.py:28
  237.5 11.4 %collective-permute-start.10 = (bf16[2,256,2560]{2,1,0:T(8,128)(2,1)}, bf16[2,256,2560]{2,1,0:T(8,128)(2,1)}, u32[]{:S(2)}, u32[]{:S(2)}) collective-permute-start(bf16[2,256,2560]{2,1,0:T(8,128)(2,1)} %collective-permute-done.6.refs_5_), channel_id=1, source_target_pairs={{0,1},{1,0},{2,3},{3,2},{4,5},{5,4},{6,7},{7,6},{8,9},{9,8},{10,11... | collective-permute-start | bytes 7864328 | tf_op jit(solution)/shard_map/ppermute | solution.py:28
  241.1 9.2 %collective-permute-start.9 = (bf16[2,256,2560]{2,1,0:T(8,128)(2,1)}, bf16[2,256,2560]{2,1,0:T(8,128)(2,1)}, u32[]{:S(2)}, u32[]{:S(2)}) collective-permute-start(bf16[2,256,2560]{2,1,0:T(8,128)(2,1)} %collective-permute-done.5.refs_4_), channel_id=1, source_target_pairs={{0,1},{1,0},{2,3},{3,2},{4,5},{5,4},{6,7},{7,6},{8,9},{9,8},{10,11... | collective-permute-start | bytes 7864328 | tf_op jit(solution)/shard_map/ppermute | solution.py:28
  241.3 36.6 %collective-permute-start.1 = (bf16[2,256,2560]{2,1,0:T(8,128)(2,1)}, bf16[2,256,2560]{2,1,0:T(8,128)(2,1)}, u32[]{:S(2)}, u32[]{:S(2)}) collective-permute-start(bf16[2,256,2560]{2,1,0:T(8,128)(2,1)} %collective-permute-done.refs_2_), channel_id=1, source_target_pairs={{1,4},{3,6},{5,8},{7,10},{9,12},{11,14},{17,20},{19,22},{21,24},{2... | collective-permute-start | bytes 7864328 | tf_op jit(solution)/shard_map/ppermute | solution.py:35
  244.1 37.0 %collective-permute-start.3 = (bf16[2,256,2560]{2,1,0:T(8,128)(2,1)}, bf16[2,256,2560]{2,1,0:T(8,128)(2,1)}, u32[]{:S(2)}, u32[]{:S(2)}) collective-permute-start(bf16[2,256,2560]{2,1,0:T(8,128)(2,1)} %collective-permute-done.2.refs_3_), channel_id=1, source_target_pairs={{4,1},{6,3},{8,5},{10,7},{12,9},{14,11},{20,17},{22,19},{24,21},{2... | collective-permute-start | bytes 7864328 | tf_op jit(solution)/shard_map/ppermute | solution.py:35
  293.3 4.9 %copy-start.3 = (bf16[256,2560]{1,0:T(8,128)(2,1)S(1)}, bf16[256,2560]{1,0:T(8,128)(2,1)}, u32[]{:S(2)}) copy-start(bf16[256,2560]{1,0:T(8,128)(2,1)} %shard_map.65) | copy-start | bytes 3932164
  296.9 20.9 %collective-permute-start.12 = (bf16[256,640]{1,0:T(8,128)(2,1)S(1)}, bf16[256,640]{1,0:T(8,128)(2,1)S(1)}, u32[]{:S(2)}, u32[]{:S(2)}) collective-permute-start(bf16[256,640]{1,0:T(8,128)(2,1)S(1)} %fusion.16), channel_id=1, source_target_pairs={{0,16},{16,0},{1,17},{17,1},{2,18},{18,2},{3,19},{19,3},{4,20},{20... | collective-permute-start | bytes 983048 | tf_op jit(solution)/shard_map/ppermute | solution.py:28
  301.4 16.5 %collective-permute-start.13 = (bf16[256,640]{1,0:T(8,128)(2,1)S(1)}, bf16[256,640]{1,0:T(8,128)(2,1)S(1)}, u32[]{:S(2)}, u32[]{:S(2)}) collective-permute-start(bf16[256,640]{1,0:T(8,128)(2,1)S(1)} %fusion.19), channel_id=1, source_target_pairs={{0,16},{16,0},{1,17},{17,1},{2,18},{18,2},{3,19},{19,3},{4,20},{20... | collective-permute-start | bytes 983048 | tf_op jit(solution)/shard_map/ppermute | solution.py:28
  304.8 15.1 %collective-permute-start.14 = (bf16[256,640]{1,0:T(8,128)(2,1)S(1)}, bf16[256,640]{1,0:T(8,128)(2,1)S(1)}, u32[]{:S(2)}, u32[]{:S(2)}) collective-permute-start(bf16[256,640]{1,0:T(8,128)(2,1)S(1)} %fusion.22), channel_id=1, source_target_pairs={{0,16},{16,0},{1,17},{17,1},{2,18},{18,2},{3,19},{19,3},{4,20},{20... | collective-permute-start | bytes 983048 | tf_op jit(solution)/shard_map/ppermute | solution.py:28
  309.2 17.7 %collective-permute-start.11 = (bf16[256,640]{1,0:T(8,128)(2,1)S(1)}, bf16[256,640]{1,0:T(8,128)(2,1)S(1)}, u32[]{:S(2)}, u32[]{:S(2)}) collective-permute-start(bf16[256,640]{1,0:T(8,128)(2,1)S(1)} %fusion.13), channel_id=1, source_target_pairs={{0,16},{16,0},{1,17},{17,1},{2,18},{18,2},{3,19},{19,3},{4,20},{20... | collective-permute-start | bytes 983048 | tf_op jit(solution)/shard_map/ppermute | solution.py:28
  309.6 18.8 %copy-start.1 = (s32[32,12]{0,1:T(8,128)S(1)}, s32[32,12]{0,1:T(8,128)}, u32[]{:S(2)}) copy-start(s32[32,12]{0,1:T(8,128)} %param.10) | copy-start | bytes 4612
Sparse Core Ops, SparseCore 0:
  9.0 248.5 all-gather.1

commit v13 on v11

--- a/solution.py
+++ b/solution.py
@@ -39,14 +39,14 @@
     kv_refs = refs[:n_blocks]
     at = n_blocks
     if carry_in:
-        acc_in, peak_in, total_in = refs[at:at + 3]
-        at += 3
+        acc_in, stats_in = refs[at:at + 2]
+        at += 2
     if finish:
         out_ref = refs[at]
         at += 1
     else:
-        acc_out, peak_out, total_out = refs[at:at + 3]
-        at += 3
+        acc_out, stats_out = refs[at:at + 2]
+        at += 2
     score_ref = refs[at]
     rows = q_ref.shape[0]
     for g in range(group):
@@ -68,7 +68,7 @@
         scores = score_ref[...]
         peak = jnp.max(scores, axis=1, keepdims=True)
         if carry_in:
-            old_peak = peak_in[:, g * HD:g * HD + 1]
+            old_peak = stats_in[:, g * HD:g * HD + 1]
             peak = jnp.maximum(peak, old_peak)
             carried = jnp.exp(old_peak - peak)
         weights = jnp.exp(scores - peak)
@@ -80,14 +80,16 @@
                 rounded[:, b * rows:(b + 1) * rows], kv_refs[b][1, :, cols], preferred_element_type=jnp.float32
             )
         if carry_in:
-            totals = carried * total_in[:, g * HD:g * HD + 1] + totals
+            totals = carried * stats_in[:, g * HD + 1:g * HD + 2] + totals
             summed = carried * acc_in[:, cols] + summed
         if finish:
             out_ref[:, cols] = (summed / totals).astype(out_ref.dtype)
         else:
             acc_out[:, cols] = summed
-            peak_out[:, cols] = jnp.broadcast_to(peak, (rows, HD))
-            total_out[:, cols] = jnp.broadcast_to(totals, (rows, HD))
+            lane = lax.broadcasted_iota(jnp.int32, (rows, HD), 1)
+            stats_out[:, cols] = jnp.where(
+                lane == 0, jnp.broadcast_to(peak, (rows, HD)), jnp.broadcast_to(totals, (rows, HD))
+            )
 
 
 def block_attention(queries, kv_list, flat_masks, carry=None, finish=True):
@@ -103,14 +105,14 @@
     in_specs = [row_spec] + [kv_spec] * n_blocks
     operands = [flat_masks, queries, *kv_list]
     if carry is not None:
-        in_specs += [row_spec] * 3
+        in_specs += [row_spec] * 2
         operands += list(carry)
     if finish:
         out_shape = jax.ShapeDtypeStruct((rows, width), jnp.bfloat16)
         out_specs = row_spec
     else:
-        out_shape = (state_shape,) * 3
-        out_specs = (row_spec,) * 3
+        out_shape = (state_shape,) * 2
+        out_specs = (row_spec,) * 2
     grid_spec = pltpu.PrefetchScalarGridSpec(
         num_scalar_prefetch=1,
         grid=(heads // group,),
@@ -119,7 +121,7 @@
         scratch_shapes=[pltpu.VMEM((rows, n_blocks * rows), jnp.float32)],
     )
     flops = 4 * rows * n_blocks * rows * HD * heads
-    bytes_moved = 2 * (rows * width * 2 + n_blocks * 2 * rows * width) + 24 * rows * width
+    bytes_moved = 2 * (rows * width * 2 + n_blocks * 2 * rows * width) + 16 * rows * width
     return pl.pallas_call(
         functools.partial(attention_kernel, n_blocks, tiles, group, carry is not None, finish),
         grid_spec=grid_spec,

time: 336 us -> 335 us (level)
  no operation moved by 1% of the time
where the time goes in v13:
time: 335 us
  waiting for transfers between devices  225 us (67%)
  Pallas kernels  37.9 us (11%)
  starting transfers between devices  29.9 us (9%)
  matrix products  21.3 us (6%)
  between operations  13.6 us (4%)
  other arithmetic  4.07 us (1%)
    ppermute x4, waiting for transfers between devices, shifted(): return lax.ppermute(x, axis, pairs)  209 us
    pallas_call x2, Pallas kernels, block_attention(): pl.pallas_call(functools.partial(attention_kernel, n_blocks, tiles, group...  37.9 us
    ppermute x9, starting transfers between devices, swapped(): return lax.ppermute(x, axis, [(0, 1), (1, 0)])  14.4 us
    dot_general x4, matrix products, local(): jnp.dot(attended, theirs[:, cols], preferred_element_type=jnp.float32)  13 us
    ppermute x4, starting transfers between devices, shifted(): return lax.ppermute(x, axis, pairs)  11.5 us
    ppermute x9, waiting for transfers between devices, swapped(): return lax.ppermute(x, axis, [(0, 1), (1, 0)])  10.4 us
    dot_general x1, matrix products, local(): jnp.dot(attended, mine, preferred_element_type=jnp.float32)  8.31 us
  transfers between devices with their start and end apart: 16, of which 7 were waited for; matrix products, arithmetic and copies ran while one was open for 7% of the time, Pallas kernels for 11%

profile of v13, /device:TPU:9, one launch (start us, length us, event | category | flops | bytes accessed | tf_op | source)
XLA Modules:
  0.0 334.7 jit_solution(1450315021447821903)
XLA Ops:
  6.5 0.7 all-gather.2.cloned.1.call-update
  7.3 2.0 pad_maximum_fusion.refs_0_
  9.2 3.1 collective-permute-start
  12.4 3.0 collective-permute-start.2
  15.4 1.9 collective-permute-start.6
  17.4 3.4 %collective-permute-start.5 = (bf16[2,256,2560]{2,1,0:T(8,128)(2,1)S(1)}, bf16[2,256,2560]{2,1,0:T(8,128)(2,1)}, u32[]{:S(2)}, u32[]{:S(2)}) collective-permute-start(bf16[2,256,2560]{2,1,0:T(8,128)(2,1)S(1)} %pad_maximum_fusion.refs_0_), channel_id=1, source_target_pairs={{0,4},{2,6},{4,8},{6,10},{8,12},{10,14},{1,5},{3,7},{5,9},{7,11},{... | collective-permute-start | bytes 7864328 | tf_op jit(solution)/shard_map/ppermute | solution.py:24
  20.7 1.9 collective-permute-start.4
  22.6 96.7 %collective-permute-done.refs_2_ = bf16[2,256,2560]{2,1,0:T(8,128)(2,1)} collective-permute-done((bf16[2,256,2560]{2,1,0:T(8,128)(2,1)S(1)}, bf16[2,256,2560]{2,1,0:T(8,128)(2,1)}, u32[]{:S(2)}, u32[]{:S(2)}) %collective-permute-start) | collective-permute-done | bytes 2621472 | tf_op jit(solution)/shard_map/ppermute | solution.py:24
  119.3 3.0 collective-permute-start.7
  122.3 4.8 %collective-permute-done.2.refs_3_ = bf16[2,256,2560]{2,1,0:T(8,128)(2,1)} collective-permute-done((bf16[2,256,2560]{2,1,0:T(8,128)(2,1)S(1)}, bf16[2,256,2560]{2,1,0:T(8,128)(2,1)}, u32[]{:S(2)}, u32[]{:S(2)}) %collective-permute-start.2) | collective-permute-done | bytes 2621472 | tf_op jit(solution)/shard_map/ppermute | solution.py:24
  127.1 2.7 collective-permute-start.8
  129.8 107.7 %collective-permute-done.6.refs_5_ = bf16[2,256,2560]{2,1,0:T(8,128)(2,1)} collective-permute-done((bf16[2,256,2560]{2,1,0:T(8,128)(2,1)S(1)}, bf16[2,256,2560]{2,1,0:T(8,128)(2,1)}, u32[]{:S(2)}, u32[]{:S(2)}) %collective-permute-start.6) | collective-permute-done | bytes 2621472 | tf_op jit(solution)/shard_map/ppermute | solution.py:24
  237.5 3.6 %collective-permute-start.10 = (bf16[2,256,2560]{2,1,0:T(8,128)(2,1)}, bf16[2,256,2560]{2,1,0:T(8,128)(2,1)}, u32[]{:S(2)}, u32[]{:S(2)}) collective-permute-start(bf16[2,256,2560]{2,1,0:T(8,128)(2,1)} %collective-permute-done.6.refs_5_), channel_id=1, source_target_pairs={{0,1},{1,0},{2,3},{3,2},{4,5},{5,4},{6,7},{7,6},{8,9},{9,8},{10,11... | collective-permute-start | bytes 7864328 | tf_op jit(solution)/shard_map/ppermute | solution.py:28
  241.1 0.1 constant_dynamic-slice_fusion
  241.2 0.1 copy.21
  241.3 2.8 collective-permute-start.1
  244.1 1.3 collective-permute-start.3
  245.6 0.6 and_reduce_fusion
  246.2 0.1 copy.22
  246.3 0.1 copy.23
  246.4 0.1 copy.24
  246.5 0.1 copy.25
  246.6 0.1 copy.26
  246.7 0.1 copy.27
  246.9 0.1 copy.28
  247.0 0.1 copy.29
  247.1 0.1 copy.30
  247.2 0.1 copy.31
  247.3 0.1 stack.61
  247.4 0.1 copy.32
  247.5 0.6 reshape.97.mask_ref
  248.2 0.6 reshape.96.mask_ref
  248.8 1.5 collective-permute-done.9.refs_8_
  250.3 26.1 %shard_map.64 = (f32[256,2560]{1,0:T(8,128)}, f32[256,2560]{1,0:T(8,128)}) custom-call(s32[40]{0:T(128)} %reshape.97.mask_ref, bf16[256,2560]{1,0:T(8,128)(2,1)} %q_ref.3, bf16[2,256,2560]{2,1,0:T(8,128)(2,1)} %copy-done.2, bf16[2,256,2560]{2,1,0:T(8,128)(2,1)} %collective-permute-done.4.refs_1_, bf16[2,256,2560]{2,1,0:T(8,128)(2,1)} %collective-permute-done.refs_2_, ...), custom_call_target="tpu_custom_call" | custom-call | flops 6710886400 | bytes 39321600 | tf_op jit(solution)/shard_map/pallas_call | solution.py:125
  276.4 4.7 %collective-permute-done.3.refs_1_ = bf16[2,256,2560]{2,1,0:T(8,128)(2,1)} collective-permute-done((bf16[2,256,2560]{2,1,0:T(8,128)(2,1)}, bf16[2,256,2560]{2,1,0:T(8,128)(2,1)}, u32[]{:S(2)}, u32[]{:S(2)}) %collective-permute-start.3) | collective-permute-done | bytes 2621472 | tf_op jit(solution)/shard_map/ppermute | solution.py:35
  281.1 11.8 %shard_map.65 = bf16[256,2560]{1,0:T(8,128)(2,1)} custom-call(s32[8]{0:T(128)} %reshape.96.mask_ref, bf16[256,2560]{1,0:T(8,128)(2,1)} %q_ref.3, bf16[2,256,2560]{2,1,0:T(8,128)(2,1)} %collective-permute-done.1.refs_0_, bf16[2,256,2560]{2,1,0:T(8,128)(2,1)} %collective-permute-done.3.refs_1_, f32[256,2560]{1,0:T(8,128)} %get-tuple-element.7.refs_2_, ...), custom_call_target="tpu_custom_call" | custom-call | flops 1342177280 | bytes 18350080 | tf_op jit(solution)/shard_map/pallas_call | solution.py:125
  293.0 3.6 %fusion.16 = bf16[256,640]{1,0:T(8,128)(2,1)S(1)} fusion(bf16[256,2560]{1,0:T(8,128)(2,1)} %shard_map.65, bf16[2560,5120]{0,1:T(8,128)(2,1)} %all-gather.2.cloned.1.call-done, s32[]{:T(128)S(6)} %add.210), kind=kOutput, calls=%fused_computation.14 | convolution fusion | flops 839024640 | bytes 4915204 | tf_op jit(solution)/shard_map/dot_general | solution.py:187
  296.6 1.2 collective-permute-start.12
  297.8 3.1 fusion.19
  301.0 0.4 collective-permute-start.13
  301.3 3.1 fusion.22
  304.5 1.2 collective-permute-start.14
  305.7 3.1 fusion.13
  308.9 0.4 collective-permute-start.11
  309.2 8.3 %fusion.2 = bf16[256,2560]{1,0:T(8,128)(2,1)S(1)} fusion(bf16[256,2560]{1,0:T(8,128)(2,1)S(1)} %copy-done.3, bf16[2560,5120]{0,1:T(8,128)(2,1)} %all-gather.2.cloned.1.call-done, s32[]{:T(128)S(6)} %select_n.11), kind=kOutput, calls=%fused_computation.2 | convolution fusion | flops 3356098560 | bytes 15728644 | tf_op jit(solution)/shard_map/dot_general | solution.py:189
  317.6 2.8 collective-permute-done.14
  320.4 6.1 %collective-permute-done.11 = bf16[256,640]{1,0:T(8,128)(2,1)S(1)} collective-permute-done((bf16[256,640]{1,0:T(8,128)(2,1)S(1)}, bf16[256,640]{1,0:T(8,128)(2,1)S(1)}, u32[]{:S(2)}, u32[]{:S(2)}) %collective-permute-start.11) | collective-permute-done | bytes 327712 | tf_op jit(solution)/shard_map/ppermute | solution.py:28
  326.5 1.4 add_convert_fusion
  (38 shorter events, 0.3 us)
Async XLA Ops:
  6.5 234.5 %copy-start = (s32[32,12]{0,1:T(8,128)S(1)}, s32[32,12]{0,1:T(8,128)}, u32[]{:S(2)}) copy-start(s32[32,12]{0,1:T(8,128)} %param.10) | copy-start | bytes 4612
  6.5 286.4 %all-gather.2.cloned.1.call-start = ((), (), s32[]{:S(2)}) async-start(), calls=%async_computation | async-start | bytes 27852800 | tf_op jit(solution)/shard_map/all_gather | solution.py:175
  7.3 234.0 %copy-start.4 = (s32[32]{0:T(128)S(1)}, s32[32]{0:T(128)}, u32[]{:S(2)}) copy-start(s32[32]{0:T(128)} %param.11) | copy-start | bytes 388
  9.2 241.1 %copy-start.2 = (bf16[2,256,2560]{2,1,0:T(8,128)(2,1)}, bf16[2,256,2560]{2,1,0:T(8,128)(2,1)S(1)}, u32[]{:S(2)}) copy-start(bf16[2,256,2560]{2,1,0:T(8,128)(2,1)S(1)} %pad_maximum_fusion.refs_0_) | copy-start | bytes 7864324
  9.2 110.1 %collective-permute-start = (bf16[2,256,2560]{2,1,0:T(8,128)(2,1)S(1)}, bf16[2,256,2560]{2,1,0:T(8,128)(2,1)}, u32[]{:S(2)}, u32[]{:S(2)}) collective-permute-start(bf16[2,256,2560]{2,1,0:T(8,128)(2,1)S(1)} %pad_maximum_fusion.refs_0_), channel_id=1, source_target_pairs={{0,2},{2,4},{4,6},{6,8},{8,10},{10,12},{12,14},{1,3},{3,5},{5,7},{... | collective-permute-start | bytes 7864328 | tf_op jit(solution)/shard_map/ppermute | solution.py:24
  12.4 114.7 %collective-permute-start.2 = (bf16[2,256,2560]{2,1,0:T(8,128)(2,1)S(1)}, bf16[2,256,2560]{2,1,0:T(8,128)(2,1)}, u32[]{:S(2)}, u32[]{:S(2)}) collective-permute-start(bf16[2,256,2560]{2,1,0:T(8,128)(2,1)S(1)} %pad_maximum_fusion.refs_0_), channel_id=1, source_target_pairs={{2,0},{4,2},{6,4},{8,6},{10,8},{12,10},{14,12},{3,1},{5,3},{7,5},{... | collective-permute-start | bytes 7864328 | tf_op jit(solution)/shard_map/ppermute | solution.py:24
  15.4 222.0 %collective-permute-start.6 = (bf16[2,256,2560]{2,1,0:T(8,128)(2,1)S(1)}, bf16[2,256,2560]{2,1,0:T(8,128)(2,1)}, u32[]{:S(2)}, u32[]{:S(2)}) collective-permute-start(bf16[2,256,2560]{2,1,0:T(8,128)(2,1)S(1)} %pad_maximum_fusion.refs_0_), channel_id=1, source_target_pairs={{4,0},{6,2},{8,4},{10,6},{12,8},{14,10},{5,1},{7,3},{9,5},{11,7},{... | collective-permute-start | bytes 7864328 | tf_op jit(solution)/shard_map/ppermute | solution.py:24
  17.4 223.7 %collective-permute-start.5 = (bf16[2,256,2560]{2,1,0:T(8,128)(2,1)S(1)}, bf16[2,256,2560]{2,1,0:T(8,128)(2,1)}, u32[]{:S(2)}, u32[]{:S(2)}) collective-permute-start(bf16[2,256,2560]{2,1,0:T(8,128)(2,1)S(1)} %pad_maximum_fusion.refs_0_), channel_id=1, source_target_pairs={{0,4},{2,6},{4,8},{6,10},{8,12},{10,14},{1,5},{3,7},{5,9},{7,11},{... | collective-permute-start | bytes 7864328 | tf_op jit(solution)/shard_map/ppermute | solution.py:24
  20.7 220.6 %collective-permute-start.4 = (bf16[2,256,2560]{2,1,0:T(8,128)(2,1)S(1)}, bf16[2,256,2560]{2,1,0:T(8,128)(2,1)}, u32[]{:S(2)}, u32[]{:S(2)}) collective-permute-start(bf16[2,256,2560]{2,1,0:T(8,128)(2,1)S(1)} %pad_maximum_fusion.refs_0_), channel_id=1, source_target_pairs={{0,1},{1,0},{2,3},{3,2},{4,5},{5,4},{6,7},{7,6},{8,9},{9,8},{10,11... | collective-permute-start | bytes 7864328 | tf_op jit(solution)/shard_map/ppermute | solution.py:28
  119.3 124.8 %collective-permute-start.7 = (bf16[2,256,2560]{2,1,0:T(8,128)(2,1)}, bf16[2,256,2560]{2,1,0:T(8,128)(2,1)}, u32[]{:S(2)}, u32[]{:S(2)}) collective-permute-start(bf16[2,256,2560]{2,1,0:T(8,128)(2,1)} %collective-permute-done.refs_2_), channel_id=1, source_target_pairs={{0,1},{1,0},{2,3},{3,2},{4,5},{5,4},{6,7},{7,6},{8,9},{9,8},{10,11... | collective-permute-start | bytes 7864328 | tf_op jit(solution)/shard_map/ppermute | solution.py:28
  127.1 121.7 %collective-permute-start.8 = (bf16[2,256,2560]{2,1,0:T(8,128)(2,1)}, bf16[2,256,2560]{2,1,0:T(8,128)(2,1)}, u32[]{:S(2)}, u32[]{:S(2)}) collective-permute-start(bf16[2,256,2560]{2,1,0:T(8,128)(2,1)} %collective-permute-done.2.refs_3_), channel_id=1, source_target_pairs={{0,1},{1,0},{2,3},{3,2},{4,5},{5,4},{6,7},{7,6},{8,9},{9,8},{10,11... | collective-permute-start | bytes 7864328 | tf_op jit(solution)/shard_map/ppermute | solution.py:28
  237.5 11.3 %collective-permute-start.10 = (bf16[2,256,2560]{2,1,0:T(8,128)(2,1)}, bf16[2,256,2560]{2,1,0:T(8,128)(2,1)}, u32[]{:S(2)}, u32[]{:S(2)}) collective-permute-start(bf16[2,256,2560]{2,1,0:T(8,128)(2,1)} %collective-permute-done.6.refs_5_), channel_id=1, source_target_pairs={{0,1},{1,0},{2,3},{3,2},{4,5},{5,4},{6,7},{7,6},{8,9},{9,8},{10,11... | collective-permute-start | bytes 7864328 | tf_op jit(solution)/shard_map/ppermute | solution.py:28
  241.1 9.2 %collective-permute-start.9 = (bf16[2,256,2560]{2,1,0:T(8,128)(2,1)}, bf16[2,256,2560]{2,1,0:T(8,128)(2,1)}, u32[]{:S(2)}, u32[]{:S(2)}) collective-permute-start(bf16[2,256,2560]{2,1,0:T(8,128)(2,1)} %collective-permute-done.5.refs_4_), channel_id=1, source_target_pairs={{0,1},{1,0},{2,3},{3,2},{4,5},{5,4},{6,7},{7,6},{8,9},{9,8},{10,11... | collective-permute-start | bytes 7864328 | tf_op jit(solution)/shard_map/ppermute | solution.py:28
  241.3 35.1 %collective-permute-start.1 = (bf16[2,256,2560]{2,1,0:T(8,128)(2,1)}, bf16[2,256,2560]{2,1,0:T(8,128)(2,1)}, u32[]{:S(2)}, u32[]{:S(2)}) collective-permute-start(bf16[2,256,2560]{2,1,0:T(8,128)(2,1)} %collective-permute-done.refs_2_), channel_id=1, source_target_pairs={{1,4},{3,6},{5,8},{7,10},{9,12},{11,14},{17,20},{19,22},{21,24},{2... | collective-permute-start | bytes 7864328 | tf_op jit(solution)/shard_map/ppermute | solution.py:35
  244.1 37.0 %collective-permute-start.3 = (bf16[2,256,2560]{2,1,0:T(8,128)(2,1)}, bf16[2,256,2560]{2,1,0:T(8,128)(2,1)}, u32[]{:S(2)}, u32[]{:S(2)}) collective-permute-start(bf16[2,256,2560]{2,1,0:T(8,128)(2,1)} %collective-permute-done.2.refs_3_), channel_id=1, source_target_pairs={{4,1},{6,3},{8,5},{10,7},{12,9},{14,11},{20,17},{22,19},{24,21},{2... | collective-permute-start | bytes 7864328 | tf_op jit(solution)/shard_map/ppermute | solution.py:35
  292.9 4.9 %copy-start.3 = (bf16[256,2560]{1,0:T(8,128)(2,1)S(1)}, bf16[256,2560]{1,0:T(8,128)(2,1)}, u32[]{:S(2)}) copy-start(bf16[256,2560]{1,0:T(8,128)(2,1)} %shard_map.65) | copy-start | bytes 3932164
  296.6 20.9 %collective-permute-start.12 = (bf16[256,640]{1,0:T(8,128)(2,1)S(1)}, bf16[256,640]{1,0:T(8,128)(2,1)S(1)}, u32[]{:S(2)}, u32[]{:S(2)}) collective-permute-start(bf16[256,640]{1,0:T(8,128)(2,1)S(1)} %fusion.16), channel_id=1, source_target_pairs={{0,16},{16,0},{1,17},{17,1},{2,18},{18,2},{3,19},{19,3},{4,20},{20... | collective-permute-start | bytes 983048 | tf_op jit(solution)/shard_map/ppermute | solution.py:28
  301.0 16.6 %collective-permute-start.13 = (bf16[256,640]{1,0:T(8,128)(2,1)S(1)}, bf16[256,640]{1,0:T(8,128)(2,1)S(1)}, u32[]{:S(2)}, u32[]{:S(2)}) collective-permute-start(bf16[256,640]{1,0:T(8,128)(2,1)S(1)} %fusion.19), channel_id=1, source_target_pairs={{0,16},{16,0},{1,17},{17,1},{2,18},{18,2},{3,19},{19,3},{4,20},{20... | collective-permute-start | bytes 983048 | tf_op jit(solution)/shard_map/ppermute | solution.py:28
  304.5 15.9 %collective-permute-start.14 = (bf16[256,640]{1,0:T(8,128)(2,1)S(1)}, bf16[256,640]{1,0:T(8,128)(2,1)S(1)}, u32[]{:S(2)}, u32[]{:S(2)}) collective-permute-start(bf16[256,640]{1,0:T(8,128)(2,1)S(1)} %fusion.22), channel_id=1, source_target_pairs={{0,16},{16,0},{1,17},{17,1},{2,18},{18,2},{3,19},{19,3},{4,20},{20... | collective-permute-start | bytes 983048 | tf_op jit(solution)/shard_map/ppermute | solution.py:28
  308.9 17.6 %collective-permute-start.11 = (bf16[256,640]{1,0:T(8,128)(2,1)S(1)}, bf16[256,640]{1,0:T(8,128)(2,1)S(1)}, u32[]{:S(2)}, u32[]{:S(2)}) collective-permute-start(bf16[256,640]{1,0:T(8,128)(2,1)S(1)} %fusion.13), channel_id=1, source_target_pairs={{0,16},{16,0},{1,17},{17,1},{2,18},{18,2},{3,19},{19,3},{4,20},{20... | collective-permute-start | bytes 983048 | tf_op jit(solution)/shard_map/ppermute | solution.py:28
  309.2 18.7 %copy-start.1 = (s32[32,12]{0,1:T(8,128)S(1)}, s32[32,12]{0,1:T(8,128)}, u32[]{:S(2)}) copy-start(s32[32,12]{0,1:T(8,128)} %param.10) | copy-start | bytes 4612
Sparse Core Ops, SparseCore 0:
  9.0 248.5 all-gather.1

commit v14 on v13

--- a/solution.py
+++ b/solution.py
@@ -161,7 +161,7 @@
             early.append((-sign * 2 * chip_step, block))
     from_below, from_above = fetched[0][1], fetched[1][1]
     up_three, down_three = third_neighbours(from_below, from_above, chips)
-    late = [(-REACH, up_three, core == 0), (REACH, down_three, core == 1)]
+    late = [(-REACH + 2 * REACH * core, up_three + down_three, True)]
     for offset, block in fetched:
         passed = swapped(block, "core")
         early.append((offset + 1 - 2 * core, passed))

time: 335 us -> 375 us (1.12)
  starting transfers between devices: 29.9 us -> 89.9 us
  waiting for transfers between devices: 225 us -> 195 us
  other arithmetic: 4.07 us -> 8.61 us
    ppermute x4, waiting for transfers between devices: 209 us -> 154 us  [shifted(): return lax.ppermute(x, axis, pairs)]
    ppermute x9, starting transfers between devices: 14.4 us -> 66.2 us  [swapped(): return lax.ppermute(x, axis, [(0, 1), (1, 0)])]
    ppermute x1, waiting for transfers between devices: 4.73 us -> 30.8 us  [third_neighbours(): lax.ppermute(from_above, SEQ, down)]
    ppermute x1, starting transfers between devices: 2.76 us -> 11 us  [third_neighbours(): lax.ppermute(from_below, SEQ, up)]
    add x0 -> x1, other arithmetic: none -> 4.63 us  [local(): late = [(-REACH + 2 * REACH * core, up_three + down_three, True)]]
  transfers between devices with their start and end apart: 16 -> 16, of which waited for: 7 -> 5; matrix products, arithmetic and copies ran while one was open for 7% -> 7% of each run, Pallas kernels for 11% -> 11%
where the time goes in v14:
time: 375 us; the launch traced here: 372 us
  waiting for transfers between devices  195 us (52%)
  starting transfers between devices  89.9 us (24%)
  Pallas kernels  41.2 us (11%)
  matrix products  21.3 us (6%)
  between operations  13.6 us (4%)
  other arithmetic  8.61 us (2%)
    ppermute x4, waiting for transfers between devices, shifted(): return lax.ppermute(x, axis, pairs)  154 us
    ppermute x9, starting transfers between devices, swapped(): return lax.ppermute(x, axis, [(0, 1), (1, 0)])  66.2 us
    pallas_call x2, Pallas kernels, block_attention(): pl.pallas_call(functools.partial(attention_kernel, n_blocks, tiles, group...  41.2 us
    ppermute x1, waiting for transfers between devices, third_neighbours(): lax.ppermute(from_above, SEQ, down)  30.8 us
    dot_general x4, matrix products, local(): jnp.dot(attended, theirs[:, cols], preferred_element_type=jnp.float32)  13 us
    ppermute x4, starting transfers between devices, shifted(): return lax.ppermute(x, axis, pairs)  11.5 us
    ppermute x1, starting transfers between devices, third_neighbours(): lax.ppermute(from_below, SEQ, up)  11 us
    ppermute x9, waiting for transfers between devices, swapped(): return lax.ppermute(x, axis, [(0, 1), (1, 0)])  8.95 us
  transfers between devices with their start and end apart: 16, of which 5 were waited for; matrix products, arithmetic and copies ran while one was open for 7% of the time, Pallas kernels for 11%

profile of v14, /device:TPU:9, one launch (start us, length us, event | category | flops | bytes accessed | tf_op | source)
XLA Modules:
  0.0 372.3 jit_solution(10520201303508999004)
XLA Ops:
  6.5 0.7 all-gather.2.cloned.1.call-update
  7.3 2.0 pad_maximum_fusion.refs_0_
  9.2 3.1 collective-permute-start
  12.4 3.0 collective-permute-start.2
  15.4 1.9 collective-permute-start.6
  17.4 3.4 collective-permute-start.5
  20.7 98.6 %collective-permute-done.refs_2_ = bf16[2,256,2560]{2,1,0:T(8,128)(2,1)} collective-permute-done((bf16[2,256,2560]{2,1,0:T(8,128)(2,1)S(1)}, bf16[2,256,2560]{2,1,0:T(8,128)(2,1)}, u32[]{:S(2)}, u32[]{:S(2)}) %collective-permute-start) | collective-permute-done | bytes 2621472 | tf_op jit(solution)/shard_map/ppermute | solution.py:24
  119.3 11.0 %collective-permute-start.1 = (bf16[2,256,2560]{2,1,0:T(8,128)(2,1)}, bf16[2,256,2560]{2,1,0:T(8,128)(2,1)}, u32[]{:S(2)}, u32[]{:S(2)}) collective-permute-start(bf16[2,256,2560]{2,1,0:T(8,128)(2,1)} %collective-permute-done.refs_2_), channel_id=1, source_target_pairs={{1,4},{3,6},{5,8},{7,10},{9,12},{11,14},{17,20},{19,22},{21,24},{2... | collective-permute-start | bytes 7864328 | tf_op jit(solution)/shard_map/ppermute | solution.py:35
  130.3 1.3 collective-permute-start.3
  131.6 50.1 %collective-permute-start.4 = (bf16[2,256,2560]{2,1,0:T(8,128)(2,1)S(1)}, bf16[2,256,2560]{2,1,0:T(8,128)(2,1)}, u32[]{:S(2)}, u32[]{:S(2)}) collective-permute-start(bf16[2,256,2560]{2,1,0:T(8,128)(2,1)S(1)} %pad_maximum_fusion.refs_0_), channel_id=1, source_target_pairs={{0,1},{1,0},{2,3},{3,2},{4,5},{5,4},{6,7},{7,6},{8,9},{9,8},{10,11... | collective-permute-start | bytes 7864328 | tf_op jit(solution)/shard_map/ppermute | solution.py:28
  181.7 55.8 %collective-permute-done.6.refs_5_ = bf16[2,256,2560]{2,1,0:T(8,128)(2,1)} collective-permute-done((bf16[2,256,2560]{2,1,0:T(8,128)(2,1)S(1)}, bf16[2,256,2560]{2,1,0:T(8,128)(2,1)}, u32[]{:S(2)}, u32[]{:S(2)}) %collective-permute-start.6) | collective-permute-done | bytes 2621472 | tf_op jit(solution)/shard_map/ppermute | solution.py:24
  237.5 3.6 collective-permute-start.7
  241.1 9.3 %collective-permute-start.10 = (bf16[2,256,2560]{2,1,0:T(8,128)(2,1)}, bf16[2,256,2560]{2,1,0:T(8,128)(2,1)}, u32[]{:S(2)}, u32[]{:S(2)}) collective-permute-start(bf16[2,256,2560]{2,1,0:T(8,128)(2,1)} %collective-permute-done.6.refs_5_), channel_id=1, source_target_pairs={{0,1},{1,0},{2,3},{3,2},{4,5},{5,4},{6,7},{7,6},{8,9},{9,8},{10,11... | collective-permute-start | bytes 7864328 | tf_op jit(solution)/shard_map/ppermute | solution.py:28
  250.4 30.8 %collective-permute-done.3 = bf16[2,256,2560]{2,1,0:T(8,128)(2,1)} collective-permute-done((bf16[2,256,2560]{2,1,0:T(8,128)(2,1)}, bf16[2,256,2560]{2,1,0:T(8,128)(2,1)}, u32[]{:S(2)}, u32[]{:S(2)}) %collective-permute-start.3) | collective-permute-done | bytes 2621472 | tf_op jit(solution)/shard_map/ppermute | solution.py:35
  281.1 0.1 constant_dynamic-slice_fusion
  281.2 0.1 copy.21
  281.3 0.1 dynamic_slice.13
  281.4 0.1 iota_compare_fusion
  281.5 0.5 and_reduce_fusion
  282.1 0.1 copy.22
  282.2 0.1 copy.23
  282.3 0.1 copy.24
  282.4 0.1 copy.25
  282.5 0.1 copy.26
  282.6 0.1 copy.27
  282.7 0.1 copy.28
  282.9 0.1 copy.29
  283.0 0.1 copy.30
  283.1 0.1 copy.31
  283.2 0.1 stack.56
  283.3 0.1 copy.32
  283.4 0.6 reshape.77.mask_ref
  284.0 0.6 reshape.76.mask_ref
  284.6 4.6 %add.164.refs_0_ = bf16[2,256,2560]{2,1,0:T(8,128)(2,1)} add(bf16[2,256,2560]{2,1,0:T(8,128)(2,1)} %collective-permute-done.1, bf16[2,256,2560]{2,1,0:T(8,128)(2,1)} %collective-permute-done.3) | non-fusion elementwise | flops 1310720 | bytes 7864320 | tf_op jit(solution)/shard_map/add | solution.py:164
  289.3 26.1 %shard_map.64 = (f32[256,2560]{1,0:T(8,128)}, f32[256,2560]{1,0:T(8,128)}) custom-call(s32[40]{0:T(128)} %reshape.77.mask_ref, bf16[256,2560]{1,0:T(8,128)(2,1)} %q_ref.3, bf16[2,256,2560]{2,1,0:T(8,128)(2,1)} %copy-done.2, bf16[2,256,2560]{2,1,0:T(8,128)(2,1)} %collective-permute-done.4.refs_1_, bf16[2,256,2560]{2,1,0:T(8,128)(2,1)} %collective-permute-done.refs_2_, ...), custom_call_target="tpu_custom_call" | custom-call | flops 6710886400 | bytes 39321600 | tf_op jit(solution)/shard_map/pallas_call | solution.py:125
  315.4 15.1 %shard_map.65 = bf16[256,2560]{1,0:T(8,128)(2,1)} custom-call(s32[4]{0:T(128)} %reshape.76.mask_ref, bf16[256,2560]{1,0:T(8,128)(2,1)} %q_ref.3, bf16[2,256,2560]{2,1,0:T(8,128)(2,1)} %add.164.refs_0_, f32[256,2560]{1,0:T(8,128)} %get-tuple-element.7.refs_1_, f32[256,2560]{1,0:T(8,128)} %get-tuple-element.8.refs_2_), custom_call_target="tpu_custom_call" | custom-call | flops 671088640 | bytes 15728640 | tf_op jit(solution)/shard_map/pallas_call | solution.py:125
  330.6 3.6 fusion.16
  334.2 1.3 collective-permute-start.12
  335.5 3.1 fusion.19
  338.6 0.3 collective-permute-start.13
  338.9 3.1 fusion.22
  342.1 1.3 collective-permute-start.14
  343.4 3.1 fusion.13
  346.5 0.3 collective-permute-start.11
  346.8 8.3 %fusion.2 = bf16[256,2560]{1,0:T(8,128)(2,1)S(1)} fusion(bf16[256,2560]{1,0:T(8,128)(2,1)S(1)} %copy-done.3, bf16[2560,5120]{0,1:T(8,128)(2,1)} %all-gather.2.cloned.1.call-done, s32[]{:T(128)S(6)} %select_n.11), kind=kOutput, calls=%fused_computation.2 | convolution fusion | flops 3356098560 | bytes 15728644 | tf_op jit(solution)/shard_map/dot_general | solution.py:189
  355.2 1.9 collective-permute-done.14
  357.1 7.0 %collective-permute-done.11 = bf16[256,640]{1,0:T(8,128)(2,1)S(1)} collective-permute-done((bf16[256,640]{1,0:T(8,128)(2,1)S(1)}, bf16[256,640]{1,0:T(8,128)(2,1)S(1)}, u32[]{:S(2)}, u32[]{:S(2)}) %collective-permute-start.11) | collective-permute-done | bytes 327712 | tf_op jit(solution)/shard_map/ppermute | solution.py:28
  364.1 1.4 add_convert_fusion
  (32 shorter events, 0.1 us)
Async XLA Ops:
  6.5 274.6 %copy-start = (s32[32,12]{0,1:T(8,128)S(1)}, s32[32,12]{0,1:T(8,128)}, u32[]{:S(2)}) copy-start(s32[32,12]{0,1:T(8,128)} %param.10) | copy-start | bytes 4612
  6.5 324.0 %all-gather.2.cloned.1.call-start = ((), (), s32[]{:S(2)}) async-start(), calls=%async_computation | async-start | bytes 27852800 | tf_op jit(solution)/shard_map/all_gather | solution.py:175
  7.3 274.1 %copy-start.4 = (s32[32]{0:T(128)S(1)}, s32[32]{0:T(128)}, u32[]{:S(2)}) copy-start(s32[32]{0:T(128)} %param.11) | copy-start | bytes 388
  9.2 280.0 %copy-start.2 = (bf16[2,256,2560]{2,1,0:T(8,128)(2,1)}, bf16[2,256,2560]{2,1,0:T(8,128)(2,1)S(1)}, u32[]{:S(2)}) copy-start(bf16[2,256,2560]{2,1,0:T(8,128)(2,1)S(1)} %pad_maximum_fusion.refs_0_) | copy-start | bytes 7864324
  9.2 110.1 %collective-permute-start = (bf16[2,256,2560]{2,1,0:T(8,128)(2,1)S(1)}, bf16[2,256,2560]{2,1,0:T(8,128)(2,1)}, u32[]{:S(2)}, u32[]{:S(2)}) collective-permute-start(bf16[2,256,2560]{2,1,0:T(8,128)(2,1)S(1)} %pad_maximum_fusion.refs_0_), channel_id=1, source_target_pairs={{0,2},{2,4},{4,6},{6,8},{8,10},{10,12},{12,14},{1,3},{3,5},{5,7},{... | collective-permute-start | bytes 7864328 | tf_op jit(solution)/shard_map/ppermute | solution.py:24
  12.4 117.9 %collective-permute-start.2 = (bf16[2,256,2560]{2,1,0:T(8,128)(2,1)S(1)}, bf16[2,256,2560]{2,1,0:T(8,128)(2,1)}, u32[]{:S(2)}, u32[]{:S(2)}) collective-permute-start(bf16[2,256,2560]{2,1,0:T(8,128)(2,1)S(1)} %pad_maximum_fusion.refs_0_), channel_id=1, source_target_pairs={{2,0},{4,2},{6,4},{8,6},{10,8},{12,10},{14,12},{3,1},{5,3},{7,5},{... | collective-permute-start | bytes 7864328 | tf_op jit(solution)/shard_map/ppermute | solution.py:24
  15.4 222.0 %collective-permute-start.6 = (bf16[2,256,2560]{2,1,0:T(8,128)(2,1)S(1)}, bf16[2,256,2560]{2,1,0:T(8,128)(2,1)}, u32[]{:S(2)}, u32[]{:S(2)}) collective-permute-start(bf16[2,256,2560]{2,1,0:T(8,128)(2,1)S(1)} %pad_maximum_fusion.refs_0_), channel_id=1, source_target_pairs={{4,0},{6,2},{8,4},{10,6},{12,8},{14,10},{5,1},{7,3},{9,5},{11,7},{... | collective-permute-start | bytes 7864328 | tf_op jit(solution)/shard_map/ppermute | solution.py:24
  17.4 223.7 %collective-permute-start.5 = (bf16[2,256,2560]{2,1,0:T(8,128)(2,1)S(1)}, bf16[2,256,2560]{2,1,0:T(8,128)(2,1)}, u32[]{:S(2)}, u32[]{:S(2)}) collective-permute-start(bf16[2,256,2560]{2,1,0:T(8,128)(2,1)S(1)} %pad_maximum_fusion.refs_0_), channel_id=1, source_target_pairs={{0,4},{2,6},{4,8},{6,10},{8,12},{10,14},{1,5},{3,7},{5,9},{7,11},{... | collective-permute-start | bytes 7864328 | tf_op jit(solution)/shard_map/ppermute | solution.py:24
  119.3 121.8 %collective-permute-start.1 = (bf16[2,256,2560]{2,1,0:T(8,128)(2,1)}, bf16[2,256,2560]{2,1,0:T(8,128)(2,1)}, u32[]{:S(2)}, u32[]{:S(2)}) collective-permute-start(bf16[2,256,2560]{2,1,0:T(8,128)(2,1)} %collective-permute-done.refs_2_), channel_id=1, source_target_pairs={{1,4},{3,6},{5,8},{7,10},{9,12},{11,14},{17,20},{19,22},{21,24},{2... | collective-permute-start | bytes 7864328 | tf_op jit(solution)/shard_map/ppermute | solution.py:35
  130.3 150.8 %collective-permute-start.3 = (bf16[2,256,2560]{2,1,0:T(8,128)(2,1)}, bf16[2,256,2560]{2,1,0:T(8,128)(2,1)}, u32[]{:S(2)}, u32[]{:S(2)}) collective-permute-start(bf16[2,256,2560]{2,1,0:T(8,128)(2,1)} %collective-permute-done.2.refs_3_), channel_id=1, source_target_pairs={{4,1},{6,3},{8,5},{10,7},{12,9},{14,11},{20,17},{22,19},{24,21},{2... | collective-permute-start | bytes 7864328 | tf_op jit(solution)/shard_map/ppermute | solution.py:35
  131.6 157.7 %collective-permute-start.4 = (bf16[2,256,2560]{2,1,0:T(8,128)(2,1)S(1)}, bf16[2,256,2560]{2,1,0:T(8,128)(2,1)}, u32[]{:S(2)}, u32[]{:S(2)}) collective-permute-start(bf16[2,256,2560]{2,1,0:T(8,128)(2,1)S(1)} %pad_maximum_fusion.refs_0_), channel_id=1, source_target_pairs={{0,1},{1,0},{2,3},{3,2},{4,5},{5,4},{6,7},{7,6},{8,9},{9,8},{10,11... | collective-permute-start | bytes 7864328 | tf_op jit(solution)/shard_map/ppermute | solution.py:28
  237.5 51.8 %collective-permute-start.7 = (bf16[2,256,2560]{2,1,0:T(8,128)(2,1)}, bf16[2,256,2560]{2,1,0:T(8,128)(2,1)}, u32[]{:S(2)}, u32[]{:S(2)}) collective-permute-start(bf16[2,256,2560]{2,1,0:T(8,128)(2,1)} %collective-permute-done.refs_2_), channel_id=1, source_target_pairs={{0,1},{1,0},{2,3},{3,2},{4,5},{5,4},{6,7},{7,6},{8,9},{9,8},{10,11... | collective-permute-start | bytes 7864328 | tf_op jit(solution)/shard_map/ppermute | solution.py:28
  241.1 48.2 %collective-permute-start.8 = (bf16[2,256,2560]{2,1,0:T(8,128)(2,1)}, bf16[2,256,2560]{2,1,0:T(8,128)(2,1)}, u32[]{:S(2)}, u32[]{:S(2)}) collective-permute-start(bf16[2,256,2560]{2,1,0:T(8,128)(2,1)} %collective-permute-done.2.refs_3_), channel_id=1, source_target_pairs={{0,1},{1,0},{2,3},{3,2},{4,5},{5,4},{6,7},{7,6},{8,9},{9,8},{10,11... | collective-permute-start | bytes 7864328 | tf_op jit(solution)/shard_map/ppermute | solution.py:28
  241.1 48.2 %collective-permute-start.10 = (bf16[2,256,2560]{2,1,0:T(8,128)(2,1)}, bf16[2,256,2560]{2,1,0:T(8,128)(2,1)}, u32[]{:S(2)}, u32[]{:S(2)}) collective-permute-start(bf16[2,256,2560]{2,1,0:T(8,128)(2,1)} %collective-permute-done.6.refs_5_), channel_id=1, source_target_pairs={{0,1},{1,0},{2,3},{3,2},{4,5},{5,4},{6,7},{7,6},{8,9},{9,8},{10,11... | collective-permute-start | bytes 7864328 | tf_op jit(solution)/shard_map/ppermute | solution.py:28
  281.1 8.2 %collective-permute-start.9 = (bf16[2,256,2560]{2,1,0:T(8,128)(2,1)}, bf16[2,256,2560]{2,1,0:T(8,128)(2,1)}, u32[]{:S(2)}, u32[]{:S(2)}) collective-permute-start(bf16[2,256,2560]{2,1,0:T(8,128)(2,1)} %collective-permute-done.5.refs_4_), channel_id=1, source_target_pairs={{0,1},{1,0},{2,3},{3,2},{4,5},{5,4},{6,7},{7,6},{8,9},{9,8},{10,11... | collective-permute-start | bytes 7864328 | tf_op jit(solution)/shard_map/ppermute | solution.py:28
  330.6 4.9 %copy-start.3 = (bf16[256,2560]{1,0:T(8,128)(2,1)S(1)}, bf16[256,2560]{1,0:T(8,128)(2,1)}, u32[]{:S(2)}) copy-start(bf16[256,2560]{1,0:T(8,128)(2,1)} %shard_map.65) | copy-start | bytes 3932164
  334.2 20.9 %collective-permute-start.12 = (bf16[256,640]{1,0:T(8,128)(2,1)S(1)}, bf16[256,640]{1,0:T(8,128)(2,1)S(1)}, u32[]{:S(2)}, u32[]{:S(2)}) collective-permute-start(bf16[256,640]{1,0:T(8,128)(2,1)S(1)} %fusion.16), channel_id=1, source_target_pairs={{0,16},{16,0},{1,17},{17,1},{2,18},{18,2},{3,19},{19,3},{4,20},{20... | collective-permute-start | bytes 983048 | tf_op jit(solution)/shard_map/ppermute | solution.py:28
  338.6 16.5 %collective-permute-start.13 = (bf16[256,640]{1,0:T(8,128)(2,1)S(1)}, bf16[256,640]{1,0:T(8,128)(2,1)S(1)}, u32[]{:S(2)}, u32[]{:S(2)}) collective-permute-start(bf16[256,640]{1,0:T(8,128)(2,1)S(1)} %fusion.19), channel_id=1, source_target_pairs={{0,16},{16,0},{1,17},{17,1},{2,18},{18,2},{3,19},{19,3},{4,20},{20... | collective-permute-start | bytes 983048 | tf_op jit(solution)/shard_map/ppermute | solution.py:28
  342.1 15.0 %collective-permute-start.14 = (bf16[256,640]{1,0:T(8,128)(2,1)S(1)}, bf16[256,640]{1,0:T(8,128)(2,1)S(1)}, u32[]{:S(2)}, u32[]{:S(2)}) collective-permute-start(bf16[256,640]{1,0:T(8,128)(2,1)S(1)} %fusion.22), channel_id=1, source_target_pairs={{0,16},{16,0},{1,17},{17,1},{2,18},{18,2},{3,19},{19,3},{4,20},{20... | collective-permute-start | bytes 983048 | tf_op jit(solution)/shard_map/ppermute | solution.py:28
  346.5 17.6 %collective-permute-start.11 = (bf16[256,640]{1,0:T(8,128)(2,1)S(1)}, bf16[256,640]{1,0:T(8,128)(2,1)S(1)}, u32[]{:S(2)}, u32[]{:S(2)}) collective-permute-start(bf16[256,640]{1,0:T(8,128)(2,1)S(1)} %fusion.13), channel_id=1, source_target_pairs={{0,16},{16,0},{1,17},{17,1},{2,18},{18,2},{3,19},{19,3},{4,20},{20... | collective-permute-start | bytes 983048 | tf_op jit(solution)/shard_map/ppermute | solution.py:28
  346.8 18.7 %copy-start.1 = (s32[32,12]{0,1:T(8,128)S(1)}, s32[32,12]{0,1:T(8,128)}, u32[]{:S(2)}) copy-start(s32[32,12]{0,1:T(8,128)} %param.10) | copy-start | bytes 4612
Sparse Core Ops, SparseCore 0:
  9.0 254.6 all-gather.1

commit v15 on v13

--- a/solution.py
+++ b/solution.py
@@ -179,7 +179,7 @@
         me = lax.axis_index("head")
         mine = lax.dynamic_slice_in_dim(weight_rows, me * half, half, 1)
         theirs = lax.dynamic_slice_in_dim(weight_rows, (1 - me) * half, half, 1)
-        parts = 4
+        parts = 8
         chunk = half // parts
         got = []
         for part in range(parts):

time: 335 us -> 346 us (1.033)
  matrix products: 21.3 us -> 25.2 us
    dot_general x4 -> x8, matrix products: 13 us -> 16.9 us  [local(): jnp.dot(attended, theirs[:, cols], preferred_element_type=jnp.float32)]
    ppermute x9 -> x13, starting transfers between devices: 14.4 us -> 17.6 us  [swapped(): return lax.ppermute(x, axis, [(0, 1), (1, 0)])]
    ppermute x9 -> x13, waiting for transfers between devices: 10.4 us -> 12 us  [swapped(): return lax.ppermute(x, axis, [(0, 1), (1, 0)])]
  transfers between devices with their start and end apart: 16 -> 20, of which waited for: 7 -> 8; matrix products, arithmetic and copies ran while one was open for 7% -> 8% of each run, Pallas kernels for 11% -> 11%
where the time goes in v15:
time: 346 us; the launch traced here: 344 us
  waiting for transfers between devices  227 us (66%)
  Pallas kernels  37.9 us (11%)
  starting transfers between devices  33.1 us (10%)
  matrix products  25.2 us (7%)
  between operations  13.7 us (4%)
  local copies, waits for them, and re-layouts  4.53 us (1%)
    ppermute x4, waiting for transfers between devices, shifted(): return lax.ppermute(x, axis, pairs)  209 us
    pallas_call x2, Pallas kernels, block_attention(): pl.pallas_call(functools.partial(attention_kernel, n_blocks, tiles, group...  37.9 us
    ppermute x13, starting transfers between devices, swapped(): return lax.ppermute(x, axis, [(0, 1), (1, 0)])  17.6 us
    dot_general x8, matrix products, local(): jnp.dot(attended, theirs[:, cols], preferred_element_type=jnp.float32)  16.9 us
    ppermute x13, waiting for transfers between devices, swapped(): return lax.ppermute(x, axis, [(0, 1), (1, 0)])  12 us
    ppermute x4, starting transfers between devices, shifted(): return lax.ppermute(x, axis, pairs)  11.5 us
    dot_general x1, matrix products, local(): jnp.dot(attended, mine, preferred_element_type=jnp.float32)  8.34 us
  transfers between devices with their start and end apart: 20, of which 8 were waited for; matrix products, arithmetic and copies ran while one was open for 8% of the time, Pallas kernels for 11%

profile of v15, /device:TPU:9, one launch (start us, length us, event | category | flops | bytes accessed | tf_op | source)
XLA Modules:
  0.0 344.2 jit_solution(1891722466853424422)
XLA Ops:
  6.5 0.7 all-gather.2.cloned.1.call-update
  7.3 2.0 pad_maximum_fusion.refs_0_
  9.2 3.1 collective-permute-start
  12.4 3.0 collective-permute-start.2
  15.4 1.9 collective-permute-start.6
  17.4 3.4 collective-permute-start.5
  20.7 1.9 collective-permute-start.4
  22.6 96.7 %collective-permute-done.refs_2_ = bf16[2,256,2560]{2,1,0:T(8,128)(2,1)} collective-permute-done((bf16[2,256,2560]{2,1,0:T(8,128)(2,1)S(1)}, bf16[2,256,2560]{2,1,0:T(8,128)(2,1)}, u32[]{:S(2)}, u32[]{:S(2)}) %collective-permute-start) | collective-permute-done | bytes 2621472 | tf_op jit(solution)/shard_map/ppermute | solution.py:24
  119.3 3.0 collective-permute-start.7
  122.3 4.8 %collective-permute-done.2.refs_3_ = bf16[2,256,2560]{2,1,0:T(8,128)(2,1)} collective-permute-done((bf16[2,256,2560]{2,1,0:T(8,128)(2,1)S(1)}, bf16[2,256,2560]{2,1,0:T(8,128)(2,1)}, u32[]{:S(2)}, u32[]{:S(2)}) %collective-permute-start.2) | collective-permute-done | bytes 2621472 | tf_op jit(solution)/shard_map/ppermute | solution.py:24
  127.1 2.7 collective-permute-start.8
  129.8 107.7 %collective-permute-done.6.refs_5_ = bf16[2,256,2560]{2,1,0:T(8,128)(2,1)} collective-permute-done((bf16[2,256,2560]{2,1,0:T(8,128)(2,1)S(1)}, bf16[2,256,2560]{2,1,0:T(8,128)(2,1)}, u32[]{:S(2)}, u32[]{:S(2)}) %collective-permute-start.6) | collective-permute-done | bytes 2621472 | tf_op jit(solution)/shard_map/ppermute | solution.py:24
  237.5 3.6 %collective-permute-start.10 = (bf16[2,256,2560]{2,1,0:T(8,128)(2,1)}, bf16[2,256,2560]{2,1,0:T(8,128)(2,1)}, u32[]{:S(2)}, u32[]{:S(2)}) collective-permute-start(bf16[2,256,2560]{2,1,0:T(8,128)(2,1)} %collective-permute-done.6.refs_5_), channel_id=1, source_target_pairs={{0,1},{1,0},{2,3},{3,2},{4,5},{5,4},{6,7},{7,6},{8,9},{9,8},{10,11... | collective-permute-start | bytes 7864328 | tf_op jit(solution)/shard_map/ppermute | solution.py:28
  241.3 2.8 collective-permute-start.1
  244.1 1.3 collective-permute-start.3
  245.6 0.6 and_reduce_fusion
  246.2 0.1 copy.66
  246.3 0.1 copy.67
  246.5 0.1 copy.69
  247.3 0.1 stack.61
  247.5 0.6 reshape.97.mask_ref
  248.2 0.6 reshape.96.mask_ref
  248.8 1.5 collective-permute-done.9.refs_8_
  250.3 26.1 %shard_map.64 = (f32[256,2560]{1,0:T(8,128)}, f32[256,2560]{1,0:T(8,128)}) custom-call(s32[40]{0:T(128)} %reshape.97.mask_ref, bf16[256,2560]{1,0:T(8,128)(2,1)} %q_ref.3, bf16[2,256,2560]{2,1,0:T(8,128)(2,1)} %copy-done.2, bf16[2,256,2560]{2,1,0:T(8,128)(2,1)} %collective-permute-done.4.refs_1_, bf16[2,256,2560]{2,1,0:T(8,128)(2,1)} %collective-permute-done.refs_2_, ...), custom_call_target="tpu_custom_call" | custom-call | flops 6710886400 | bytes 39321600 | tf_op jit(solution)/shard_map/pallas_call | solution.py:125
  276.4 4.7 %collective-permute-done.3.refs_1_ = bf16[2,256,2560]{2,1,0:T(8,128)(2,1)} collective-permute-done((bf16[2,256,2560]{2,1,0:T(8,128)(2,1)}, bf16[2,256,2560]{2,1,0:T(8,128)(2,1)}, u32[]{:S(2)}, u32[]{:S(2)}) %collective-permute-start.3) | collective-permute-done | bytes 2621472 | tf_op jit(solution)/shard_map/ppermute | solution.py:35
  281.1 11.8 %shard_map.65 = bf16[256,2560]{1,0:T(8,128)(2,1)} custom-call(s32[8]{0:T(128)} %reshape.96.mask_ref, bf16[256,2560]{1,0:T(8,128)(2,1)} %q_ref.3, bf16[2,256,2560]{2,1,0:T(8,128)(2,1)} %collective-permute-done.1.refs_0_, bf16[2,256,2560]{2,1,0:T(8,128)(2,1)} %collective-permute-done.3.refs_1_, f32[256,2560]{1,0:T(8,128)} %get-tuple-element.7.refs_2_, ...), custom_call_target="tpu_custom_call" | custom-call | flops 1342177280 | bytes 18350080 | tf_op jit(solution)/shard_map/pallas_call | solution.py:125
  293.0 2.6 fusion.21
  295.5 1.2 collective-permute-start.11
  296.7 2.0 fusion.24
  298.8 0.4 collective-permute-start.12
  299.2 2.0 fusion.27
  301.2 1.2 collective-permute-start.13
  302.5 2.0 fusion.30
  304.5 0.4 collective-permute-start.14
  304.9 2.0 fusion.33
  306.9 1.2 collective-permute-start.15
  308.2 2.0 fusion.36
  310.2 2.1 fusion.39
  312.3 8.3 %fusion.2 = bf16[256,2560]{0,1:T(8,128)(2,1)S(1)} fusion(bf16[256,2560]{1,0:T(8,128)(2,1)S(1)} %copy-done.3, bf16[2560,5120]{0,1:T(8,128)(2,1)} %all-gather.2.cloned.1.call-done, s32[]{:T(128)S(6)} %select_n.11), kind=kOutput, calls=%fused_computation.2 | convolution fusion | flops 3356098560 | bytes 15728644 | tf_op jit(solution)/shard_map/dot_general | solution.py:189
  320.6 2.1 fusion.42
  322.7 0.4 collective-permute-start.16
  323.1 1.2 collective-permute-start.17
  324.3 0.4 collective-permute-start.18
  324.8 3.5 %collective-permute-done.16 = bf16[256,320]{0,1:T(8,128)(2,1)S(1)} collective-permute-done((bf16[256,320]{0,1:T(8,128)(2,1)S(1)}, bf16[256,320]{0,1:T(8,128)(2,1)S(1)}, u32[]{:S(2)}, u32[]{:S(2)}) %collective-permute-start.16) | collective-permute-done | bytes 163872 | tf_op jit(solution)/shard_map/ppermute | solution.py:28
  328.3 3.5 %collective-permute-done.17 = bf16[256,320]{0,1:T(8,128)(2,1)S(1)} collective-permute-done((bf16[256,320]{0,1:T(8,128)(2,1)S(1)}, bf16[256,320]{0,1:T(8,128)(2,1)S(1)}, u32[]{:S(2)}, u32[]{:S(2)}) %collective-permute-start.17) | collective-permute-done | bytes 163872 | tf_op jit(solution)/shard_map/ppermute | solution.py:28
  331.8 3.5 %collective-permute-done.18 = bf16[256,320]{0,1:T(8,128)(2,1)S(1)} collective-permute-done((bf16[256,320]{0,1:T(8,128)(2,1)S(1)}, bf16[256,320]{0,1:T(8,128)(2,1)S(1)}, u32[]{:S(2)}, u32[]{:S(2)}) %collective-permute-start.18) | collective-permute-done | bytes 163872 | tf_op jit(solution)/shard_map/ppermute | solution.py:28
  335.3 0.4 add_convert_fusion
  335.8 1.6 copy.78
  (59 shorter events, 1.4 us)
Async XLA Ops:
  6.5 234.5 %copy-start = (s32[32,12]{0,1:T(8,128)S(1)}, s32[32,12]{0,1:T(8,128)}, u32[]{:S(2)}) copy-start(s32[32,12]{0,1:T(8,128)} %param.10) | copy-start | bytes 4612
  6.5 286.4 %all-gather.2.cloned.1.call-start = ((), (), s32[]{:S(2)}) async-start(), calls=%async_computation | async-start | bytes 27852800 | tf_op jit(solution)/shard_map/all_gather | solution.py:175
  7.3 234.0 %copy-start.4 = (s32[32]{0:T(128)S(1)}, s32[32]{0:T(128)}, u32[]{:S(2)}) copy-start(s32[32]{0:T(128)} %param.11) | copy-start | bytes 388
  9.2 241.1 %copy-start.2 = (bf16[2,256,2560]{2,1,0:T(8,128)(2,1)}, bf16[2,256,2560]{2,1,0:T(8,128)(2,1)S(1)}, u32[]{:S(2)}) copy-start(bf16[2,256,2560]{2,1,0:T(8,128)(2,1)S(1)} %pad_maximum_fusion.refs_0_) | copy-start | bytes 7864324
  9.2 110.1 %collective-permute-start = (bf16[2,256,2560]{2,1,0:T(8,128)(2,1)S(1)}, bf16[2,256,2560]{2,1,0:T(8,128)(2,1)}, u32[]{:S(2)}, u32[]{:S(2)}) collective-permute-start(bf16[2,256,2560]{2,1,0:T(8,128)(2,1)S(1)} %pad_maximum_fusion.refs_0_), channel_id=1, source_target_pairs={{0,2},{2,4},{4,6},{6,8},{8,10},{10,12},{12,14},{1,3},{3,5},{5,7},{... | collective-permute-start | bytes 7864328 | tf_op jit(solution)/shard_map/ppermute | solution.py:24
  12.4 114.7 %collective-permute-start.2 = (bf16[2,256,2560]{2,1,0:T(8,128)(2,1)S(1)}, bf16[2,256,2560]{2,1,0:T(8,128)(2,1)}, u32[]{:S(2)}, u32[]{:S(2)}) collective-permute-start(bf16[2,256,2560]{2,1,0:T(8,128)(2,1)S(1)} %pad_maximum_fusion.refs_0_), channel_id=1, source_target_pairs={{2,0},{4,2},{6,4},{8,6},{10,8},{12,10},{14,12},{3,1},{5,3},{7,5},{... | collective-permute-start | bytes 7864328 | tf_op jit(solution)/shard_map/ppermute | solution.py:24
  15.4 222.0 %collective-permute-start.6 = (bf16[2,256,2560]{2,1,0:T(8,128)(2,1)S(1)}, bf16[2,256,2560]{2,1,0:T(8,128)(2,1)}, u32[]{:S(2)}, u32[]{:S(2)}) collective-permute-start(bf16[2,256,2560]{2,1,0:T(8,128)(2,1)S(1)} %pad_maximum_fusion.refs_0_), channel_id=1, source_target_pairs={{4,0},{6,2},{8,4},{10,6},{12,8},{14,10},{5,1},{7,3},{9,5},{11,7},{... | collective-permute-start | bytes 7864328 | tf_op jit(solution)/shard_map/ppermute | solution.py:24
  17.4 223.7 %collective-permute-start.5 = (bf16[2,256,2560]{2,1,0:T(8,128)(2,1)S(1)}, bf16[2,256,2560]{2,1,0:T(8,128)(2,1)}, u32[]{:S(2)}, u32[]{:S(2)}) collective-permute-start(bf16[2,256,2560]{2,1,0:T(8,128)(2,1)S(1)} %pad_maximum_fusion.refs_0_), channel_id=1, source_target_pairs={{0,4},{2,6},{4,8},{6,10},{8,12},{10,14},{1,5},{3,7},{5,9},{7,11},{... | collective-permute-start | bytes 7864328 | tf_op jit(solution)/shard_map/ppermute | solution.py:24
  20.7 220.6 %collective-permute-start.4 = (bf16[2,256,2560]{2,1,0:T(8,128)(2,1)S(1)}, bf16[2,256,2560]{2,1,0:T(8,128)(2,1)}, u32[]{:S(2)}, u32[]{:S(2)}) collective-permute-start(bf16[2,256,2560]{2,1,0:T(8,128)(2,1)S(1)} %pad_maximum_fusion.refs_0_), channel_id=1, source_target_pairs={{0,1},{1,0},{2,3},{3,2},{4,5},{5,4},{6,7},{7,6},{8,9},{9,8},{10,11... | collective-permute-start | bytes 7864328 | tf_op jit(solution)/shard_map/ppermute | solution.py:28
  119.3 124.8 %collective-permute-start.7 = (bf16[2,256,2560]{2,1,0:T(8,128)(2,1)}, bf16[2,256,2560]{2,1,0:T(8,128)(2,1)}, u32[]{:S(2)}, u32[]{:S(2)}) collective-permute-start(bf16[2,256,2560]{2,1,0:T(8,128)(2,1)} %collective-permute-done.refs_2_), channel_id=1, source_target_pairs={{0,1},{1,0},{2,3},{3,2},{4,5},{5,4},{6,7},{7,6},{8,9},{9,8},{10,11... | collective-permute-start | bytes 7864328 | tf_op jit(solution)/shard_map/ppermute | solution.py:28
  127.1 121.7 %collective-permute-start.8 = (bf16[2,256,2560]{2,1,0:T(8,128)(2,1)}, bf16[2,256,2560]{2,1,0:T(8,128)(2,1)}, u32[]{:S(2)}, u32[]{:S(2)}) collective-permute-start(bf16[2,256,2560]{2,1,0:T(8,128)(2,1)} %collective-permute-done.2.refs_3_), channel_id=1, source_target_pairs={{0,1},{1,0},{2,3},{3,2},{4,5},{5,4},{6,7},{7,6},{8,9},{9,8},{10,11... | collective-permute-start | bytes 7864328 | tf_op jit(solution)/shard_map/ppermute | solution.py:28
  237.5 11.3 %collective-permute-start.10 = (bf16[2,256,2560]{2,1,0:T(8,128)(2,1)}, bf16[2,256,2560]{2,1,0:T(8,128)(2,1)}, u32[]{:S(2)}, u32[]{:S(2)}) collective-permute-start(bf16[2,256,2560]{2,1,0:T(8,128)(2,1)} %collective-permute-done.6.refs_5_), channel_id=1, source_target_pairs={{0,1},{1,0},{2,3},{3,2},{4,5},{5,4},{6,7},{7,6},{8,9},{9,8},{10,11... | collective-permute-start | bytes 7864328 | tf_op jit(solution)/shard_map/ppermute | solution.py:28
  241.1 9.2 %collective-permute-start.9 = (bf16[2,256,2560]{2,1,0:T(8,128)(2,1)}, bf16[2,256,2560]{2,1,0:T(8,128)(2,1)}, u32[]{:S(2)}, u32[]{:S(2)}) collective-permute-start(bf16[2,256,2560]{2,1,0:T(8,128)(2,1)} %collective-permute-done.5.refs_4_), channel_id=1, source_target_pairs={{0,1},{1,0},{2,3},{3,2},{4,5},{5,4},{6,7},{7,6},{8,9},{9,8},{10,11... | collective-permute-start | bytes 7864328 | tf_op jit(solution)/shard_map/ppermute | solution.py:28
  241.3 35.1 %collective-permute-start.1 = (bf16[2,256,2560]{2,1,0:T(8,128)(2,1)}, bf16[2,256,2560]{2,1,0:T(8,128)(2,1)}, u32[]{:S(2)}, u32[]{:S(2)}) collective-permute-start(bf16[2,256,2560]{2,1,0:T(8,128)(2,1)} %collective-permute-done.refs_2_), channel_id=1, source_target_pairs={{1,4},{3,6},{5,8},{7,10},{9,12},{11,14},{17,20},{19,22},{21,24},{2... | collective-permute-start | bytes 7864328 | tf_op jit(solution)/shard_map/ppermute | solution.py:35
  244.1 37.0 %collective-permute-start.3 = (bf16[2,256,2560]{2,1,0:T(8,128)(2,1)}, bf16[2,256,2560]{2,1,0:T(8,128)(2,1)}, u32[]{:S(2)}, u32[]{:S(2)}) collective-permute-start(bf16[2,256,2560]{2,1,0:T(8,128)(2,1)} %collective-permute-done.2.refs_3_), channel_id=1, source_target_pairs={{4,1},{6,3},{8,5},{10,7},{12,9},{14,11},{20,17},{22,19},{24,21},{2... | collective-permute-start | bytes 7864328 | tf_op jit(solution)/shard_map/ppermute | solution.py:35
  292.9 3.8 %copy-start.3 = (bf16[256,2560]{1,0:T(8,128)(2,1)S(1)}, bf16[256,2560]{1,0:T(8,128)(2,1)}, u32[]{:S(2)}) copy-start(bf16[256,2560]{1,0:T(8,128)(2,1)} %shard_map.65) | copy-start | bytes 3932164
  295.5 27.2 %collective-permute-start.11 = (bf16[256,320]{0,1:T(8,128)(2,1)S(1)}, bf16[256,320]{0,1:T(8,128)(2,1)S(1)}, u32[]{:S(2)}, u32[]{:S(2)}) collective-permute-start(bf16[256,320]{0,1:T(8,128)(2,1)S(1)} %fusion.21), channel_id=1, source_target_pairs={{0,16},{16,0},{1,17},{17,1},{2,18},{18,2},{3,19},{19,3},{4,20},{20... | collective-permute-start | bytes 491528 | tf_op jit(solution)/shard_map/ppermute | solution.py:28
  298.8 24.3 %collective-permute-start.12 = (bf16[256,320]{0,1:T(8,128)(2,1)S(1)}, bf16[256,320]{0,1:T(8,128)(2,1)S(1)}, u32[]{:S(2)}, u32[]{:S(2)}) collective-permute-start(bf16[256,320]{0,1:T(8,128)(2,1)S(1)} %fusion.24), channel_id=1, source_target_pairs={{0,16},{16,0},{1,17},{17,1},{2,18},{18,2},{3,19},{19,3},{4,20},{20... | collective-permute-start | bytes 491528 | tf_op jit(solution)/shard_map/ppermute | solution.py:28
  301.2 23.1 %collective-permute-start.13 = (bf16[256,320]{0,1:T(8,128)(2,1)S(1)}, bf16[256,320]{0,1:T(8,128)(2,1)S(1)}, u32[]{:S(2)}, u32[]{:S(2)}) collective-permute-start(bf16[256,320]{0,1:T(8,128)(2,1)S(1)} %fusion.27), channel_id=1, source_target_pairs={{0,16},{16,0},{1,17},{17,1},{2,18},{18,2},{3,19},{19,3},{4,20},{20... | collective-permute-start | bytes 491528 | tf_op jit(solution)/shard_map/ppermute | solution.py:28
  304.5 20.2 %collective-permute-start.14 = (bf16[256,320]{0,1:T(8,128)(2,1)S(1)}, bf16[256,320]{0,1:T(8,128)(2,1)S(1)}, u32[]{:S(2)}, u32[]{:S(2)}) collective-permute-start(bf16[256,320]{0,1:T(8,128)(2,1)S(1)} %fusion.30), channel_id=1, source_target_pairs={{0,16},{16,0},{1,17},{17,1},{2,18},{18,2},{3,19},{19,3},{4,20},{20... | collective-permute-start | bytes 491528 | tf_op jit(solution)/shard_map/ppermute | solution.py:28
  306.9 17.8 %collective-permute-start.15 = (bf16[256,320]{0,1:T(8,128)(2,1)S(1)}, bf16[256,320]{0,1:T(8,128)(2,1)S(1)}, u32[]{:S(2)}, u32[]{:S(2)}) collective-permute-start(bf16[256,320]{0,1:T(8,128)(2,1)S(1)} %fusion.33), channel_id=1, source_target_pairs={{0,16},{16,0},{1,17},{17,1},{2,18},{18,2},{3,19},{19,3},{4,20},{20... | collective-permute-start | bytes 491528 | tf_op jit(solution)/shard_map/ppermute | solution.py:28
  322.7 5.6 %collective-permute-start.16 = (bf16[256,320]{0,1:T(8,128)(2,1)S(1)}, bf16[256,320]{0,1:T(8,128)(2,1)S(1)}, u32[]{:S(2)}, u32[]{:S(2)}) collective-permute-start(bf16[256,320]{0,1:T(8,128)(2,1)S(1)} %fusion.36), channel_id=1, source_target_pairs={{0,16},{16,0},{1,17},{17,1},{2,18},{18,2},{3,19},{19,3},{4,20},{20... | collective-permute-start | bytes 491528 | tf_op jit(solution)/shard_map/ppermute | solution.py:28
  323.1 8.7 %collective-permute-start.17 = (bf16[256,320]{0,1:T(8,128)(2,1)S(1)}, bf16[256,320]{0,1:T(8,128)(2,1)S(1)}, u32[]{:S(2)}, u32[]{:S(2)}) collective-permute-start(bf16[256,320]{0,1:T(8,128)(2,1)S(1)} %fusion.39), channel_id=1, source_target_pairs={{0,16},{16,0},{1,17},{17,1},{2,18},{18,2},{3,19},{19,3},{4,20},{20... | collective-permute-start | bytes 491528 | tf_op jit(solution)/shard_map/ppermute | solution.py:28
  324.3 11.0 %collective-permute-start.18 = (bf16[256,320]{0,1:T(8,128)(2,1)S(1)}, bf16[256,320]{0,1:T(8,128)(2,1)S(1)}, u32[]{:S(2)}, u32[]{:S(2)}) collective-permute-start(bf16[256,320]{0,1:T(8,128)(2,1)S(1)} %fusion.42), channel_id=1, source_target_pairs={{0,16},{16,0},{1,17},{17,1},{2,18},{18,2},{3,19},{19,3},{4,20},{20... | collective-permute-start | bytes 491528 | tf_op jit(solution)/shard_map/ppermute | solution.py:28
  335.3 2.0 copy-start.1
Sparse Core Ops, SparseCore 0:
  9.0 248.5 all-gather.1

commit v16 on v13

--- a/solution.py
+++ b/solution.py
@@ -92,10 +92,10 @@
             )
 
 
-def block_attention(queries, kv_list, flat_masks, carry=None, finish=True):
+def block_attention(queries, kv_list, flat_masks, carry=None, finish=True, per_step=5):
     rows, width = queries.shape
     heads = width // HD
-    group = 5 if heads % 5 == 0 else 1
+    group = per_step if heads % per_step == 0 else (5 if heads % 5 == 0 else 1)
     n_blocks = len(kv_list)
     tiles = rows // TILE
     span = group * HD
@@ -171,7 +171,7 @@
 
     late_masks = jnp.stack([tile_need(offset) & here for offset, _, here in late]).astype(jnp.int32).reshape(-1)
     carry = block_attention(queries, [b for _, b in early], masks_of(early), finish=False)
-    attended = block_attention(queries, [b for _, b, _ in late], late_masks, carry=carry)
+    attended = block_attention(queries, [b for _, b, _ in late], late_masks, carry=carry, per_step=10)
     weight_rows = lax.all_gather(out_weight, SEQ, axis=1, tiled=True)
     heads = lax.axis_size("head")
     if heads == 2:

time: 335 us -> 336 us (level)
  no operation moved by 1% of the time
where the time goes in v16:
time: 336 us; the launch traced here: 335 us
  waiting for transfers between devices  225 us (67%)
  Pallas kernels  38.4 us (11%)
  starting transfers between devices  29.9 us (9%)
  matrix products  21.3 us (6%)
  between operations  13.6 us (4%)
  other arithmetic  4.07 us (1%)
    ppermute x4, waiting for transfers between devices, shifted(): return lax.ppermute(x, axis, pairs)  209 us
    pallas_call x2, Pallas kernels, block_attention(): pl.pallas_call(functools.partial(attention_kernel, n_blocks, tiles, group...  38.4 us
    ppermute x9, starting transfers between devices, swapped(): return lax.ppermute(x, axis, [(0, 1), (1, 0)])  14.4 us
    dot_general x4, matrix products, local(): jnp.dot(attended, theirs[:, cols], preferred_element_type=jnp.float32)  13 us
    ppermute x4, starting transfers between devices, shifted(): return lax.ppermute(x, axis, pairs)  11.5 us
    ppermute x9, waiting for transfers between devices, swapped(): return lax.ppermute(x, axis, [(0, 1), (1, 0)])  10.5 us
    dot_general x1, matrix products, local(): jnp.dot(attended, mine, preferred_element_type=jnp.float32)  8.31 us
  transfers between devices with their start and end apart: 16, of which 7 were waited for; matrix products, arithmetic and copies ran while one was open for 7% of the time, Pallas kernels for 11%

profile of v16, /device:TPU:9, one launch (start us, length us, event | category | flops | bytes accessed | tf_op | source)
XLA Modules:
  0.0 335.3 jit_solution(15605664827047198159)
XLA Ops:
  6.5 0.7 all-gather.2.cloned.1.call-update
  7.3 2.0 pad_maximum_fusion.refs_0_
  9.2 3.1 collective-permute-start
  12.4 3.0 collective-permute-start.2
  15.4 1.9 collective-permute-start.6
  17.4 3.4 %collective-permute-start.5 = (bf16[2,256,2560]{2,1,0:T(8,128)(2,1)S(1)}, bf16[2,256,2560]{2,1,0:T(8,128)(2,1)}, u32[]{:S(2)}, u32[]{:S(2)}) collective-permute-start(bf16[2,256,2560]{2,1,0:T(8,128)(2,1)S(1)} %pad_maximum_fusion.refs_0_), channel_id=1, source_target_pairs={{0,4},{2,6},{4,8},{6,10},{8,12},{10,14},{1,5},{3,7},{5,9},{7,11},{... | collective-permute-start | bytes 7864328 | tf_op jit(solution)/shard_map/ppermute | solution.py:24
  20.7 1.9 collective-permute-start.4
  22.6 96.7 %collective-permute-done.refs_2_ = bf16[2,256,2560]{2,1,0:T(8,128)(2,1)} collective-permute-done((bf16[2,256,2560]{2,1,0:T(8,128)(2,1)S(1)}, bf16[2,256,2560]{2,1,0:T(8,128)(2,1)}, u32[]{:S(2)}, u32[]{:S(2)}) %collective-permute-start) | collective-permute-done | bytes 2621472 | tf_op jit(solution)/shard_map/ppermute | solution.py:24
  119.3 3.0 collective-permute-start.7
  122.3 4.8 %collective-permute-done.2.refs_3_ = bf16[2,256,2560]{2,1,0:T(8,128)(2,1)} collective-permute-done((bf16[2,256,2560]{2,1,0:T(8,128)(2,1)S(1)}, bf16[2,256,2560]{2,1,0:T(8,128)(2,1)}, u32[]{:S(2)}, u32[]{:S(2)}) %collective-permute-start.2) | collective-permute-done | bytes 2621472 | tf_op jit(solution)/shard_map/ppermute | solution.py:24
  127.1 2.7 collective-permute-start.8
  129.8 107.7 %collective-permute-done.6.refs_5_ = bf16[2,256,2560]{2,1,0:T(8,128)(2,1)} collective-permute-done((bf16[2,256,2560]{2,1,0:T(8,128)(2,1)S(1)}, bf16[2,256,2560]{2,1,0:T(8,128)(2,1)}, u32[]{:S(2)}, u32[]{:S(2)}) %collective-permute-start.6) | collective-permute-done | bytes 2621472 | tf_op jit(solution)/shard_map/ppermute | solution.py:24
  237.5 3.6 %collective-permute-start.10 = (bf16[2,256,2560]{2,1,0:T(8,128)(2,1)}, bf16[2,256,2560]{2,1,0:T(8,128)(2,1)}, u32[]{:S(2)}, u32[]{:S(2)}) collective-permute-start(bf16[2,256,2560]{2,1,0:T(8,128)(2,1)} %collective-permute-done.6.refs_5_), channel_id=1, source_target_pairs={{0,1},{1,0},{2,3},{3,2},{4,5},{5,4},{6,7},{7,6},{8,9},{9,8},{10,11... | collective-permute-start | bytes 7864328 | tf_op jit(solution)/shard_map/ppermute | solution.py:28
  241.1 0.1 constant_dynamic-slice_fusion
  241.2 0.1 copy.21
  241.3 2.8 collective-permute-start.1
  244.1 1.3 collective-permute-start.3
  245.6 0.6 and_reduce_fusion
  246.2 0.1 copy.22
  246.3 0.1 copy.23
  246.4 0.1 copy.24
  246.5 0.1 copy.25
  246.6 0.1 copy.26
  246.7 0.1 copy.27
  246.9 0.1 copy.28
  247.0 0.1 copy.29
  247.1 0.1 copy.30
  247.2 0.1 copy.31
  247.3 0.1 stack.61
  247.4 0.1 copy.32
  247.5 0.6 reshape.97.mask_ref
  248.2 0.6 reshape.96.mask_ref
  248.8 1.5 collective-permute-done.9.refs_8_
  250.3 26.1 %shard_map.64 = (f32[256,2560]{1,0:T(8,128)}, f32[256,2560]{1,0:T(8,128)}) custom-call(s32[40]{0:T(128)} %reshape.97.mask_ref, bf16[256,2560]{1,0:T(8,128)(2,1)} %q_ref.3, bf16[2,256,2560]{2,1,0:T(8,128)(2,1)} %copy-done.2, bf16[2,256,2560]{2,1,0:T(8,128)(2,1)} %collective-permute-done.4.refs_1_, bf16[2,256,2560]{2,1,0:T(8,128)(2,1)} %collective-permute-done.refs_2_, ...), custom_call_target="tpu_custom_call" | custom-call | flops 6710886400 | bytes 39321600 | tf_op jit(solution)/shard_map/pallas_call | solution.py:125
  276.4 4.7 %collective-permute-done.3.refs_1_ = bf16[2,256,2560]{2,1,0:T(8,128)(2,1)} collective-permute-done((bf16[2,256,2560]{2,1,0:T(8,128)(2,1)}, bf16[2,256,2560]{2,1,0:T(8,128)(2,1)}, u32[]{:S(2)}, u32[]{:S(2)}) %collective-permute-start.3) | collective-permute-done | bytes 2621472 | tf_op jit(solution)/shard_map/ppermute | solution.py:35
  281.1 12.3 %shard_map.65 = bf16[256,2560]{1,0:T(8,128)(2,1)} custom-call(s32[8]{0:T(128)} %reshape.96.mask_ref, bf16[256,2560]{1,0:T(8,128)(2,1)} %q_ref.3, bf16[2,256,2560]{2,1,0:T(8,128)(2,1)} %collective-permute-done.1.refs_0_, bf16[2,256,2560]{2,1,0:T(8,128)(2,1)} %collective-permute-done.3.refs_1_, f32[256,2560]{1,0:T(8,128)} %get-tuple-element.7.refs_2_, ...), custom_call_target="tpu_custom_call" | custom-call | flops 1342177280 | bytes 18350080 | tf_op jit(solution)/shard_map/pallas_call | solution.py:125
  293.5 3.6 %fusion.16 = bf16[256,640]{1,0:T(8,128)(2,1)S(1)} fusion(bf16[256,2560]{1,0:T(8,128)(2,1)} %shard_map.65, bf16[2560,5120]{0,1:T(8,128)(2,1)} %all-gather.2.cloned.1.call-done, s32[]{:T(128)S(6)} %add.210), kind=kOutput, calls=%fused_computation.14 | convolution fusion | flops 839024640 | bytes 4915204 | tf_op jit(solution)/shard_map/dot_general | solution.py:187
  297.1 1.3 collective-permute-start.12
  298.4 3.1 fusion.19
  301.5 0.3 collective-permute-start.13
  301.8 3.1 fusion.22
  305.0 1.3 collective-permute-start.14
  306.2 3.1 fusion.13
  309.4 0.3 collective-permute-start.11
  309.7 8.3 %fusion.2 = bf16[256,2560]{1,0:T(8,128)(2,1)S(1)} fusion(bf16[256,2560]{1,0:T(8,128)(2,1)S(1)} %copy-done.3, bf16[2560,5120]{0,1:T(8,128)(2,1)} %all-gather.2.cloned.1.call-done, s32[]{:T(128)S(6)} %select_n.11), kind=kOutput, calls=%fused_computation.2 | convolution fusion | flops 3356098560 | bytes 15728644 | tf_op jit(solution)/shard_map/dot_general | solution.py:189
  318.1 2.8 collective-permute-done.14
  320.9 6.1 %collective-permute-done.11 = bf16[256,640]{1,0:T(8,128)(2,1)S(1)} collective-permute-done((bf16[256,640]{1,0:T(8,128)(2,1)S(1)}, bf16[256,640]{1,0:T(8,128)(2,1)S(1)}, u32[]{:S(2)}, u32[]{:S(2)}) %collective-permute-start.11) | collective-permute-done | bytes 327712 | tf_op jit(solution)/shard_map/ppermute | solution.py:28
  327.0 1.4 add_convert_fusion
  (38 shorter events, 0.3 us)
Async XLA Ops:
  6.5 234.5 %copy-start = (s32[32,12]{0,1:T(8,128)S(1)}, s32[32,12]{0,1:T(8,128)}, u32[]{:S(2)}) copy-start(s32[32,12]{0,1:T(8,128)} %param.10) | copy-start | bytes 4612
  6.5 286.9 %all-gather.2.cloned.1.call-start = ((), (), s32[]{:S(2)}) async-start(), calls=%async_computation | async-start | bytes 27852800 | tf_op jit(solution)/shard_map/all_gather | solution.py:175
  7.3 234.0 %copy-start.4 = (s32[32]{0:T(128)S(1)}, s32[32]{0:T(128)}, u32[]{:S(2)}) copy-start(s32[32]{0:T(128)} %param.11) | copy-start | bytes 388
  9.2 241.1 %copy-start.2 = (bf16[2,256,2560]{2,1,0:T(8,128)(2,1)}, bf16[2,256,2560]{2,1,0:T(8,128)(2,1)S(1)}, u32[]{:S(2)}) copy-start(bf16[2,256,2560]{2,1,0:T(8,128)(2,1)S(1)} %pad_maximum_fusion.refs_0_) | copy-start | bytes 7864324
  9.2 110.1 %collective-permute-start = (bf16[2,256,2560]{2,1,0:T(8,128)(2,1)S(1)}, bf16[2,256,2560]{2,1,0:T(8,128)(2,1)}, u32[]{:S(2)}, u32[]{:S(2)}) collective-permute-start(bf16[2,256,2560]{2,1,0:T(8,128)(2,1)S(1)} %pad_maximum_fusion.refs_0_), channel_id=1, source_target_pairs={{0,2},{2,4},{4,6},{6,8},{8,10},{10,12},{12,14},{1,3},{3,5},{5,7},{... | collective-permute-start | bytes 7864328 | tf_op jit(solution)/shard_map/ppermute | solution.py:24
  12.4 114.7 %collective-permute-start.2 = (bf16[2,256,2560]{2,1,0:T(8,128)(2,1)S(1)}, bf16[2,256,2560]{2,1,0:T(8,128)(2,1)}, u32[]{:S(2)}, u32[]{:S(2)}) collective-permute-start(bf16[2,256,2560]{2,1,0:T(8,128)(2,1)S(1)} %pad_maximum_fusion.refs_0_), channel_id=1, source_target_pairs={{2,0},{4,2},{6,4},{8,6},{10,8},{12,10},{14,12},{3,1},{5,3},{7,5},{... | collective-permute-start | bytes 7864328 | tf_op jit(solution)/shard_map/ppermute | solution.py:24
  15.4 222.0 %collective-permute-start.6 = (bf16[2,256,2560]{2,1,0:T(8,128)(2,1)S(1)}, bf16[2,256,2560]{2,1,0:T(8,128)(2,1)}, u32[]{:S(2)}, u32[]{:S(2)}) collective-permute-start(bf16[2,256,2560]{2,1,0:T(8,128)(2,1)S(1)} %pad_maximum_fusion.refs_0_), channel_id=1, source_target_pairs={{4,0},{6,2},{8,4},{10,6},{12,8},{14,10},{5,1},{7,3},{9,5},{11,7},{... | collective-permute-start | bytes 7864328 | tf_op jit(solution)/shard_map/ppermute | solution.py:24
  17.4 223.7 %collective-permute-start.5 = (bf16[2,256,2560]{2,1,0:T(8,128)(2,1)S(1)}, bf16[2,256,2560]{2,1,0:T(8,128)(2,1)}, u32[]{:S(2)}, u32[]{:S(2)}) collective-permute-start(bf16[2,256,2560]{2,1,0:T(8,128)(2,1)S(1)} %pad_maximum_fusion.refs_0_), channel_id=1, source_target_pairs={{0,4},{2,6},{4,8},{6,10},{8,12},{10,14},{1,5},{3,7},{5,9},{7,11},{... | collective-permute-start | bytes 7864328 | tf_op jit(solution)/shard_map/ppermute | solution.py:24
  20.7 220.6 %collective-permute-start.4 = (bf16[2,256,2560]{2,1,0:T(8,128)(2,1)S(1)}, bf16[2,256,2560]{2,1,0:T(8,128)(2,1)}, u32[]{:S(2)}, u32[]{:S(2)}) collective-permute-start(bf16[2,256,2560]{2,1,0:T(8,128)(2,1)S(1)} %pad_maximum_fusion.refs_0_), channel_id=1, source_target_pairs={{0,1},{1,0},{2,3},{3,2},{4,5},{5,4},{6,7},{7,6},{8,9},{9,8},{10,11... | collective-permute-start | bytes 7864328 | tf_op jit(solution)/shard_map/ppermute | solution.py:28
  119.3 124.8 %collective-permute-start.7 = (bf16[2,256,2560]{2,1,0:T(8,128)(2,1)}, bf16[2,256,2560]{2,1,0:T(8,128)(2,1)}, u32[]{:S(2)}, u32[]{:S(2)}) collective-permute-start(bf16[2,256,2560]{2,1,0:T(8,128)(2,1)} %collective-permute-done.refs_2_), channel_id=1, source_target_pairs={{0,1},{1,0},{2,3},{3,2},{4,5},{5,4},{6,7},{7,6},{8,9},{9,8},{10,11... | collective-permute-start | bytes 7864328 | tf_op jit(solution)/shard_map/ppermute | solution.py:28
  127.1 121.7 %collective-permute-start.8 = (bf16[2,256,2560]{2,1,0:T(8,128)(2,1)}, bf16[2,256,2560]{2,1,0:T(8,128)(2,1)}, u32[]{:S(2)}, u32[]{:S(2)}) collective-permute-start(bf16[2,256,2560]{2,1,0:T(8,128)(2,1)} %collective-permute-done.2.refs_3_), channel_id=1, source_target_pairs={{0,1},{1,0},{2,3},{3,2},{4,5},{5,4},{6,7},{7,6},{8,9},{9,8},{10,11... | collective-permute-start | bytes 7864328 | tf_op jit(solution)/shard_map/ppermute | solution.py:28
  237.5 11.3 %collective-permute-start.10 = (bf16[2,256,2560]{2,1,0:T(8,128)(2,1)}, bf16[2,256,2560]{2,1,0:T(8,128)(2,1)}, u32[]{:S(2)}, u32[]{:S(2)}) collective-permute-start(bf16[2,256,2560]{2,1,0:T(8,128)(2,1)} %collective-permute-done.6.refs_5_), channel_id=1, source_target_pairs={{0,1},{1,0},{2,3},{3,2},{4,5},{5,4},{6,7},{7,6},{8,9},{9,8},{10,11... | collective-permute-start | bytes 7864328 | tf_op jit(solution)/shard_map/ppermute | solution.py:28
  241.1 9.2 %collective-permute-start.9 = (bf16[2,256,2560]{2,1,0:T(8,128)(2,1)}, bf16[2,256,2560]{2,1,0:T(8,128)(2,1)}, u32[]{:S(2)}, u32[]{:S(2)}) collective-permute-start(bf16[2,256,2560]{2,1,0:T(8,128)(2,1)} %collective-permute-done.5.refs_4_), channel_id=1, source_target_pairs={{0,1},{1,0},{2,3},{3,2},{4,5},{5,4},{6,7},{7,6},{8,9},{9,8},{10,11... | collective-permute-start | bytes 7864328 | tf_op jit(solution)/shard_map/ppermute | solution.py:28
  241.3 35.1 %collective-permute-start.1 = (bf16[2,256,2560]{2,1,0:T(8,128)(2,1)}, bf16[2,256,2560]{2,1,0:T(8,128)(2,1)}, u32[]{:S(2)}, u32[]{:S(2)}) collective-permute-start(bf16[2,256,2560]{2,1,0:T(8,128)(2,1)} %collective-permute-done.refs_2_), channel_id=1, source_target_pairs={{1,4},{3,6},{5,8},{7,10},{9,12},{11,14},{17,20},{19,22},{21,24},{2... | collective-permute-start | bytes 7864328 | tf_op jit(solution)/shard_map/ppermute | solution.py:35
  244.1 37.0 %collective-permute-start.3 = (bf16[2,256,2560]{2,1,0:T(8,128)(2,1)}, bf16[2,256,2560]{2,1,0:T(8,128)(2,1)}, u32[]{:S(2)}, u32[]{:S(2)}) collective-permute-start(bf16[2,256,2560]{2,1,0:T(8,128)(2,1)} %collective-permute-done.2.refs_3_), channel_id=1, source_target_pairs={{4,1},{6,3},{8,5},{10,7},{12,9},{14,11},{20,17},{22,19},{24,21},{2... | collective-permute-start | bytes 7864328 | tf_op jit(solution)/shard_map/ppermute | solution.py:35
  293.4 4.9 %copy-start.3 = (bf16[256,2560]{1,0:T(8,128)(2,1)S(1)}, bf16[256,2560]{1,0:T(8,128)(2,1)}, u32[]{:S(2)}) copy-start(bf16[256,2560]{1,0:T(8,128)(2,1)} %shard_map.65) | copy-start | bytes 3932164
  297.1 20.9 %collective-permute-start.12 = (bf16[256,640]{1,0:T(8,128)(2,1)S(1)}, bf16[256,640]{1,0:T(8,128)(2,1)S(1)}, u32[]{:S(2)}, u32[]{:S(2)}) collective-permute-start(bf16[256,640]{1,0:T(8,128)(2,1)S(1)} %fusion.16), channel_id=1, source_target_pairs={{0,16},{16,0},{1,17},{17,1},{2,18},{18,2},{3,19},{19,3},{4,20},{20... | collective-permute-start | bytes 983048 | tf_op jit(solution)/shard_map/ppermute | solution.py:28
  301.5 16.5 %collective-permute-start.13 = (bf16[256,640]{1,0:T(8,128)(2,1)S(1)}, bf16[256,640]{1,0:T(8,128)(2,1)S(1)}, u32[]{:S(2)}, u32[]{:S(2)}) collective-permute-start(bf16[256,640]{1,0:T(8,128)(2,1)S(1)} %fusion.19), channel_id=1, source_target_pairs={{0,16},{16,0},{1,17},{17,1},{2,18},{18,2},{3,19},{19,3},{4,20},{20... | collective-permute-start | bytes 983048 | tf_op jit(solution)/shard_map/ppermute | solution.py:28
  305.0 15.9 %collective-permute-start.14 = (bf16[256,640]{1,0:T(8,128)(2,1)S(1)}, bf16[256,640]{1,0:T(8,128)(2,1)S(1)}, u32[]{:S(2)}, u32[]{:S(2)}) collective-permute-start(bf16[256,640]{1,0:T(8,128)(2,1)S(1)} %fusion.22), channel_id=1, source_target_pairs={{0,16},{16,0},{1,17},{17,1},{2,18},{18,2},{3,19},{19,3},{4,20},{20... | collective-permute-start | bytes 983048 | tf_op jit(solution)/shard_map/ppermute | solution.py:28
  309.4 17.6 %collective-permute-start.11 = (bf16[256,640]{1,0:T(8,128)(2,1)S(1)}, bf16[256,640]{1,0:T(8,128)(2,1)S(1)}, u32[]{:S(2)}, u32[]{:S(2)}) collective-permute-start(bf16[256,640]{1,0:T(8,128)(2,1)S(1)} %fusion.13), channel_id=1, source_target_pairs={{0,16},{16,0},{1,17},{17,1},{2,18},{18,2},{3,19},{19,3},{4,20},{20... | collective-permute-start | bytes 983048 | tf_op jit(solution)/shard_map/ppermute | solution.py:28
  309.7 18.7 %copy-start.1 = (s32[32,12]{0,1:T(8,128)S(1)}, s32[32,12]{0,1:T(8,128)}, u32[]{:S(2)}) copy-start(s32[32,12]{0,1:T(8,128)} %param.10) | copy-start | bytes 4612
Sparse Core Ops, SparseCore 0:
  9.0 248.5 all-gather.1
